TPU v7x, 128 devices: a whole 4x4x4 slice. The times are simulated.
128 devices in a mesh: wide: 32 (over z, y, core), narrow: 4 (over x).
Axes of the slice: x: 4, y: 4, z: 4, core: 2. Of those that a mesh axis runs over, the one named last changes fastest.
Arguments:
- atm_state: float32 [144, 262144], P(None, ('wide', 'narrow')), may hold values from -6 to 6
- group_owner: int32 [262144, 1], P(('wide', 'narrow')), may hold values from 0 to 127; in each aligned block of 2048 rows (0 to 2047, 2048 to 4095, ...) at most 32 rows name the same one
- regime_ops: bfloat16 [128, 4, 144, 144], P(('wide', 'narrow')), may hold values from -0.5 to 0.5
- flux_map: bfloat16 [144, 4], replicated, may hold values from -0.5 to 0.5
- remap_src: int32 [4, 1024, 1024], P(None, 'wide', 'narrow'), may hold values from 0 to 8
- remap_weight: float32 [4, 1024, 1024], P(None, 'wide', 'narrow'), may hold values from 0.05 to 0.6
- ocean_mask: int32 [1024, 1024], P('wide', 'narrow'), may hold values 0 or 1
- tracer: float32 [62, 1024, 1024], P(None, 'wide', 'narrow'), may hold values from -6 to 6
- surface_height: float32 [1024, 1024], P('wide', 'narrow'), may hold values from -3 to 3
- transports: float32 [2, 1024, 1024], P(None, 'wide', 'narrow'), may hold values from -3 to 3
Outputs:
- atm_new: float32 [144, 262144], P(None, ('wide', 'narrow'))
- tracer_new: float32 [62, 1024, 1024], P(None, 'wide', 'narrow')
- height_new: float32 [1024, 1024], P('wide', 'narrow')
- transports_new: float32 [2, 1024, 1024], P(None, 'wide', 'narrow')
Inputs may be any that keep to these rules, and one draw needn't show every extreme that they name: `group_owner`: among the 2048 columns of one device no owner is named more than 32 times, and one is named exactly 32 times.
All inputs are finite; a program needn't handle non-finite values. No bound on the sum of `ocean_mask` on one device may be relied on, other than what follows from the above.
Results may differ from a plain program's by a relative error of at most 0.0043.
Values may be sent and summed in bfloat16 or wider, within the bound.
No kernel may reach another device: no remote copies, remote signals or barrier semaphores. Data moves between devices by JAX's collectives and lax.ppermute only.
A program may use at most 128 MiB of HBM per device.

v0:
```python
import jax
import jax.numpy as jnp
from jax import lax
from jax.sharding import PartitionSpec as P

AC = 128
NSUB = 4
OCEAN_HALO = NSUB
ATM_HALO = OCEAN_HALO // 2 + 1


relax_rate = 0.5
kappa_mix = 0.2
heat_gain = 0.5
gravity = 0.7
depth_mean = 0.7
wind_gain = 0.3
fresh_gain = 0.3


def shift_pairs(count, step):
    return [(i, i + step) for i in range(count) if 0 <= i + step < count]


def with_halo(cells, width):
    wide_count = lax.axis_size("wide")
    narrow_count = lax.axis_size("narrow")
    rows = cells.shape[-2]
    cols = cells.shape[-1]
    above = lax.ppermute(cells[..., rows - width :, :], "wide", shift_pairs(wide_count, 1))
    below = lax.ppermute(cells[..., :width, :], "wide", shift_pairs(wide_count, -1))
    cells = jnp.concatenate([above, cells, below], axis=-2)
    left = lax.ppermute(cells[..., cols - width :], "narrow", shift_pairs(narrow_count, 1))
    right = lax.ppermute(cells[..., :width], "narrow", shift_pairs(narrow_count, -1))
    return jnp.concatenate([left, cells, right], axis=-1)


def plus_halo(cells):
    wide_count = lax.axis_size("wide")
    narrow_count = lax.axis_size("narrow")
    rows = cells.shape[-2]
    cols = cells.shape[-1]
    above = lax.ppermute(cells[..., rows - 1 :, :], "wide", shift_pairs(wide_count, 1))
    below = lax.ppermute(cells[..., :1, :], "wide", shift_pairs(wide_count, -1))
    left = lax.ppermute(cells[..., cols - 1 :], "narrow", shift_pairs(narrow_count, 1))
    right = lax.ppermute(cells[..., :1], "narrow", shift_pairs(narrow_count, -1))
    return above, below, left, right


def column_ranks(owners, peers):
    onehot = (owners[:, None] == jnp.arange(peers, dtype=jnp.int32)[None, :]).astype(jnp.int32)
    before = jnp.cumsum(onehot, axis=0) - onehot
    return jnp.sum(before * onehot, axis=1)


def block_width():
    return 512


def place_columns(source, slots, total):
    width = block_width()
    pieces = []
    for start in range(0, total, width):
        selector = (slots[:, None] == (start + jnp.arange(width, dtype=jnp.int32))[None, :]).astype(
            jnp.bfloat16
        )
        pieces.append(
            jnp.dot(source, selector, preferred_element_type=jnp.float32).astype(jnp.bfloat16)
        )
    return jnp.concatenate(pieces, axis=1)


def fetch_columns(source, slots):
    count = slots.shape[0]
    width = block_width()
    lanes = jnp.arange(source.shape[1], dtype=jnp.int32)
    pieces = []
    for start in range(0, count, width):
        wanted = slots[start : start + width]
        selector = (lanes[:, None] == wanted[None, :]).astype(jnp.bfloat16)
        pieces.append(jnp.dot(source, selector, preferred_element_type=jnp.float32))
    return jnp.concatenate(pieces, axis=1)


def physics(operators, columns, flux_map):
    initial = columns.astype(jnp.float32)
    current = initial
    for sweep in range(operators.shape[0]):
        mixed = lax.dot_general(
            operators[sweep],
            current.astype(jnp.bfloat16),
            (((0,), (0,)), ((), ())),
            preferred_element_type=jnp.float32,
        )
        current = current + relax_rate * jnp.tanh(mixed)
    final = current.astype(jnp.bfloat16)
    tendency = (current - initial).astype(jnp.bfloat16)
    fluxes = lax.dot_general(
        flux_map, final, (((0,), (0,)), ((), ())), preferred_element_type=jnp.float32
    ).astype(jnp.bfloat16)
    return (tendency, fluxes)


def selector(count, origin, offset, limit, base, size):
    fine = origin + jnp.arange(count, dtype=jnp.int32)
    coarse = jnp.clip(fine // 2 + offset, 0, limit - 1) - base
    return (coarse[:, None] == jnp.arange(size, dtype=jnp.int32)[None, :]).astype(jnp.bfloat16)


def remap(flux_ext, src_ext, weight_ext, ocean_rows, ocean_cols, atm_rows, atm_cols):
    nflux = flux_ext.shape[0]
    ext_r = src_ext.shape[1]
    ext_c = src_ext.shape[2]
    block_r = flux_ext.shape[1] - 2 * ATM_HALO
    block_c = flux_ext.shape[2] - 2 * ATM_HALO
    my_wide = lax.axis_index("wide")
    my_narrow = lax.axis_index("narrow")
    row0 = my_wide * ocean_rows - OCEAN_HALO
    col0 = my_narrow * ocean_cols - OCEAN_HALO
    arow0 = my_wide * block_r - ATM_HALO
    acol0 = my_narrow * block_c - ATM_HALO
    col_sel = jnp.concatenate(
        [
            selector(ext_c, col0, dc, atm_cols, acol0, flux_ext.shape[2]).T
            for dc in (-1, 0, 1)
        ],
        axis=1,
    )
    by_cols = jnp.dot(
        flux_ext.reshape(nflux * flux_ext.shape[1], flux_ext.shape[2]),
        col_sel,
        preferred_element_type=jnp.float32,
    ).astype(jnp.bfloat16)
    by_cols = by_cols.reshape(nflux, flux_ext.shape[1], 3 * ext_c)
    ocean_flux = jnp.zeros((nflux, ext_r, ext_c), jnp.float32)
    for dr in (-1, 0, 1):
        row_sel = selector(ext_r, row0, dr, atm_rows, arow0, flux_ext.shape[1])
        shifted = jnp.einsum(
            "ap,fpx->fax", row_sel, by_cols, preferred_element_type=jnp.float32
        )
        for dc in (-1, 0, 1):
            code = (dr + 1) * 3 + (dc + 1)
            weight_sum = jnp.sum(jnp.where(src_ext == code, weight_ext, 0.0), axis=0)
            window = shifted[:, :, (dc + 1) * ext_c : (dc + 2) * ext_c]
            ocean_flux = ocean_flux + weight_sum[None] * window
    return ocean_flux


def diffuse(centre, above, below, left, right, mask, m_above, m_below, m_left, m_right):
    north = jnp.concatenate([centre[:, 1:, :], below], axis=1)
    south = jnp.concatenate([above, centre[:, :-1, :]], axis=1)
    east = jnp.concatenate([centre[:, :, 1:], right], axis=2)
    west = jnp.concatenate([left, centre[:, :, :-1]], axis=2)
    mn = jnp.concatenate([mask[:, 1:, :], m_below], axis=1)
    ms = jnp.concatenate([m_above, mask[:, :-1, :]], axis=1)
    me = jnp.concatenate([mask[:, :, 1:], m_right], axis=2)
    mw = jnp.concatenate([m_left, mask[:, :, :-1]], axis=2)
    summed = jnp.zeros_like(centre)
    for nb, mb in ((north, mn), (south, ms), (east, me), (west, mw)):
        summed = summed + mask * mb * (nb - centre)
    return centre + kappa_mix * summed


def momentum(flow, height, height_next, mask, mask_next, stress):
    return mask * mask_next * (flow - gravity * (height_next - height) + wind_gain * stress)


def continuity(height, flow_u, flow_u_west, flow_v, flow_v_south, mask, fresh):
    return mask * (
        height - depth_mean * (flow_u - flow_u_west + (flow_v - flow_v_south)) + fresh_gain * fresh
    )


def next_col(x):
    return jnp.concatenate([x[:, 1:], jnp.zeros_like(x[:, :1])], axis=1)


def next_row(x):
    return jnp.concatenate([x[1:, :], jnp.zeros_like(x[:1, :])], axis=0)


def prev_col(x):
    return jnp.concatenate([jnp.zeros_like(x[:, :1]), x[:, :-1]], axis=1)


def prev_row(x):
    return jnp.concatenate([jnp.zeros_like(x[:1, :]), x[:-1, :]], axis=0)


def per_device(
    atm_state,
    group_owner,
    regime_ops,
    flux_map,
    remap_src,
    remap_weight,
    ocean_mask,
    tracer,
    surface_height,
    transports,
):
    peers = lax.axis_size(("wide", "narrow"))
    wide_count = lax.axis_size("wide")
    narrow_count = lax.axis_size("narrow")
    features = atm_state.shape[0]
    columns_here = atm_state.shape[1]
    nflux = flux_map.shape[1]
    capacity = 2 * columns_here // peers
    total_slots = peers * capacity
    block_rows = columns_here // AC
    ocean_rows = remap_src.shape[1]
    ocean_cols = remap_src.shape[2]
    kk = remap_src.shape[0]
    h = OCEAN_HALO

    mask = ocean_mask.astype(jnp.float32)
    planes = jnp.concatenate(
        [
            mask[None],
            surface_height[None],
            transports,
            remap_src.astype(jnp.float32),
            remap_weight,
        ],
        axis=0,
    )
    planes_ext = with_halo(planes, h)
    mask_ext = planes_ext[0]
    eta = planes_ext[1]
    flow_u = planes_ext[2]
    flow_v = planes_ext[3]
    src_ext = planes_ext[4 : 4 + kk].astype(jnp.int32)
    weight_ext = planes_ext[4 + kk : 4 + 2 * kk]
    t_above, t_below, t_left, t_right = plus_halo(tracer)
    m_above = mask_ext[None, h - 1 : h, h:-h]
    m_below = mask_ext[None, h + ocean_rows : h + ocean_rows + 1, h:-h]
    m_left = mask_ext[None, h:-h, h - 1 : h]
    m_right = mask_ext[None, h:-h, h + ocean_cols : h + ocean_cols + 1]
    tracer_mixed = diffuse(
        tracer, t_above, t_below, t_left, t_right, mask[None], m_above, m_below, m_left, m_right
    )

    owners = group_owner[:, 0]
    slots = owners * capacity + column_ranks(owners, peers)
    initial = atm_state.astype(jnp.bfloat16)
    outgoing = place_columns(initial, slots, total_slots)
    arrived = lax.all_to_all(outgoing, ("wide", "narrow"), split_axis=1, concat_axis=1, tiled=True)
    tendency, fluxes = physics(regime_ops[0], arrived, flux_map)
    back = lax.all_to_all(
        jnp.concatenate([tendency, fluxes], axis=0),
        ("wide", "narrow"),
        split_axis=1,
        concat_axis=1,
        tiled=True,
    )
    returned = fetch_columns(back, slots)
    tend_cols = returned[:features]
    flux_cols = returned[features:]
    atm_new = atm_state + tend_cols

    flux_block = flux_cols.astype(jnp.bfloat16).reshape(nflux, block_rows, AC)
    flux_ext = with_halo(flux_block, ATM_HALO)
    ocean_flux = remap(
        flux_ext,
        src_ext,
        weight_ext,
        ocean_rows,
        ocean_cols,
        wide_count * block_rows,
        narrow_count * AC,
    )

    inner = (slice(h, h + ocean_rows), slice(h, h + ocean_cols))
    tracer_new = tracer_mixed.at[0].add(heat_gain * mask * ocean_flux[0][inner])

    mask_east = next_col(mask_ext)
    mask_north = next_row(mask_ext)
    for substep in range(NSUB):
        flow_u = momentum(flow_u, eta, next_col(eta), mask_ext, mask_east, ocean_flux[2])
        flow_v = momentum(flow_v, eta, next_row(eta), mask_ext, mask_north, ocean_flux[3])
        eta = continuity(
            eta, flow_u, prev_col(flow_u), flow_v, prev_row(flow_v), mask_ext, ocean_flux[1]
        )
    return (atm_new, tracer_new, eta[inner], jnp.stack([flow_u[inner], flow_v[inner]]))


def solution(mesh):
    in_specs = (
        P(None, ("wide", "narrow")),
        P(("wide", "narrow"), None),
        P(("wide", "narrow"), None, None, None),
        P(),
        P(None, "wide", "narrow"),
        P(None, "wide", "narrow"),
        P("wide", "narrow"),
        P(None, "wide", "narrow"),
        P("wide", "narrow"),
        P(None, "wide", "narrow"),
    )
    out_specs = (
        P(None, ("wide", "narrow")),
        P(None, "wide", "narrow"),
        P("wide", "narrow"),
        P(None, "wide", "narrow"),
    )
    return jax.shard_map(
        per_device, mesh=mesh, in_specs=in_specs, out_specs=out_specs, check_vma=False
    )
```

profile of v0, /device:TPU:34, one launch (start us, length us, event | category | flops | bytes accessed | tf_op | source)
XLA Modules:
  0.0 171.0 jit_solution(9630819862411482595)
XLA Ops:
  0.7 2.0 %fusion.187 = (f32[62,1,256]{2,1,0:T(1,128)}, f32[62,1,256]{2,1,0:T(1,128)}) fusion(f32[62,32,256]{2,1,0:T(8,128)} %param.19), kind=kLoop, calls=%fused_computation.269 | loop fusion | bytes 253952 | tf_op jit(solution)/shard_map/slice | solution.py:43
  2.7 1.9 %collective-permute-start.5 = (f32[62,1,256]{2,1,0:T(1,128)}, f32[62,1,256]{2,1,0:T(1,128)}, u32[]{:S(2)}, u32[]{:S(2)}) collective-permute-start(f32[62,1,256]{2,1,0:T(1,128)} %get-tuple-element.32), channel_id=1, source_target_pairs={{0,4},{4,8},{8,12},{12,16},{16,20},{20,24},{24,28},{28,32},{32,36}... | collective-permute-start | bytes 190472 | tf_op jit(solution)/shard_map/ppermute | solution.py:43
  9.5 3.6 %collective-permute-start = (f32[12,4,256]{2,1,0:T(4,128)}, f32[12,4,256]{2,1,0:T(4,128)S(1)}, u32[]{:S(2)}, u32[]{:S(2)}) collective-permute-start(f32[12,4,256]{2,1,0:T(4,128)} %get-tuple-element.40), channel_id=1, source_target_pairs={{0,4},{4,8},{8,12},{12,16},{16,20},{20,24},{24,28},{28,32},{32,36}... | collective-permute-start | bytes 147464 | tf_op jit(solution)/shard_map/ppermute | solution.py:30
  13.0 4.1 %collective-permute-start.1 = (f32[12,4,256]{2,1,0:T(4,128)}, f32[12,4,256]{2,1,0:T(4,128)S(1)}, u32[]{:S(2)}, u32[]{:S(2)}) collective-permute-start(f32[12,4,256]{2,1,0:T(4,128)} %get-tuple-element.41), channel_id=1, source_target_pairs={{4,0},{8,4},{12,8},{16,12},{20,16},{24,20},{28,24},{32,28},{36,32}... | collective-permute-start | bytes 147464 | tf_op jit(solution)/shard_map/ppermute | solution.py:31
  27.5 2.4 %copy.22 = bf16[144,4096]{0,1:T(8,128)(2,1)} copy(bf16[144,4096]{1,0:T(8,128)(2,1)S(1)} %fusion.92) | data formatting | bytes 2359296 | tf_op jit(solution)/shard_map/concatenate | solution.py:70
  29.9 8.6 %all-to-all-start = ((bf16[144,128,32]{0,2,1:T(8,128)(2,1)}), bf16[144,128,32]{0,2,1:T(8,128)(2,1)}, u32[]{:S(2)}, u32[]{:S(2)}) async-start(bf16[144,128,32]{0,2,1:T(8,128)(2,1)} %bitcast.209), calls=%async_computation | async-start | bytes 4194304 | tf_op jit(solution)/shard_map/all_to_all | solution.py:247
  39.8 2.4 %copy.29 = f32[62,32,1]{0,1,2:T(8,128)} copy(f32[62,32,1]{2,1,0:T(8,128)} %get-tuple-element.29) | data formatting | bytes 15872
  42.2 2.4 %collective-permute-start.6 = (f32[62,32,1]{0,1,2:T(8,128)}, f32[62,32,1]{0,1,2:T(8,128)}, u32[]{:S(2)}, u32[]{:S(2)}) collective-permute-start(f32[62,32,1]{0,1,2:T(8,128)} %copy.29), channel_id=1, source_target_pairs={{1,0},{2,1},{3,2},{5,4},{6,5},{7,6},{9,8},{10,9},{11,10},{13,12},{... | collective-permute-start | bytes 23816 | tf_op jit(solution)/shard_map/ppermute | solution.py:46
  46.0 3.6 %collective-permute-start.7 = (f32[62,32,1]{0,1,2:T(8,128)}, f32[62,32,1]{0,1,2:T(8,128)S(1)}, u32[]{:S(2)}, u32[]{:S(2)}) collective-permute-start(f32[62,32,1]{0,1,2:T(8,128)} %copy.30), channel_id=1, source_target_pairs={{0,1},{1,2},{2,3},{4,5},{5,6},{6,7},{8,9},{9,10},{10,11},{12,13},{... | collective-permute-start | bytes 23816 | tf_op jit(solution)/shard_map/ppermute | solution.py:45
  54.9 2.8 %fusion.186 = (f32[62,32,255]{2,1,0:T(8,128)}, f32[62,32,255]{2,1,0:T(8,128)}) fusion(f32[62,32,256]{2,1,0:T(8,128)S(1)} %copy-done.1), kind=kLoop, calls=%fused_computation.268 | loop fusion | bytes 8094720 | tf_op jit(solution)/shard_map/slice | solution.py:153
  57.7 9.3 %all-to-all-done = bf16[144,128,32]{0,2,1:T(8,128)(2,1)} async-done(((bf16[144,128,32]{0,2,1:T(8,128)(2,1)}), bf16[144,128,32]{0,2,1:T(8,128)(2,1)}, u32[]{:S(2)}, u32[]{:S(2)}) %all-to-all-start) | async-done | bytes 1179680 | tf_op jit(solution)/shard_map/all_to_all | solution.py:247
  67.0 3.7 %copy.23 = bf16[144,4096]{1,0:T(8,128)(2,1)} copy(bf16[144,4096]{0,1:T(8,128)(2,1)} %bitcast.16) | data formatting | bytes 2359296 | tf_op jit(solution)/shard_map/all_to_all | solution.py:247
  70.7 2.8 %fusion.15 = f32[144,4096]{1,0:T(8,128)S(1)} fusion(bf16[144,4096]{0,1:T(8,128)(2,1)} %bitcast.16, bf16[144,4096]{1,0:T(8,128)(2,1)} %copy.23, bf16[1,4,144,144]{3,2,1,0:T(8,128)(2,1)S(1)} %copy-done.15), kind=kOutput, calls=%fused_computation.23 | convolution fusion | flops 171638784 | bytes 4792320 | tf_op jit(solution)/shard_map/dot_general | solution.py:89
  77.6 3.7 %copy.24 = bf16[148,4096]{0,1:T(8,128)(2,1)} copy(bf16[148,4096]{1,0:T(8,128)(2,1)} %pad_maximum_fusion) | data formatting | bytes 2424832 | tf_op jit(solution)/shard_map/concatenate | solution.py:250
  81.3 6.9 %all-to-all-start.1 = ((bf16[148,128,32]{0,2,1:T(8,128)(2,1)}), bf16[148,128,32]{0,2,1:T(8,128)(2,1)}, u32[]{:S(2)}, u32[]{:S(2)}) async-start(bf16[148,128,32]{0,2,1:T(8,128)(2,1)} %bitcast.210), calls=%async_computation.1 | async-start | bytes 4194304 | tf_op jit(solution)/shard_map/all_to_all | solution.py:249
  88.2 2.5 %fusion.188 = (f32[62,31,256]{2,1,0:T(8,128)}, f32[62,31,256]{2,1,0:T(8,128)}) fusion(f32[62,32,256]{2,1,0:T(8,128)S(1)} %copy-done.1), kind=kLoop, calls=%fused_computation.270 | loop fusion | bytes 7872512 | tf_op jit(solution)/shard_map/slice | solution.py:151
  92.2 3.4 %collective-permute-start.2 = (f32[12,40,4]{2,1,0:T(8,128)}, f32[12,40,4]{2,1,0:T(8,128)}, u32[]{:S(2)}, u32[]{:S(2)}) collective-permute-start(f32[12,40,4]{2,1,0:T(8,128)} %get-tuple-element.38), channel_id=1, source_target_pairs={{0,1},{1,2},{2,3},{4,5},{5,6},{6,7},{8,9},{9,10},{10,11},{12,13},{... | collective-permute-start | bytes 23048 | tf_op jit(solution)/shard_map/ppermute | solution.py:33
  95.6 3.2 %collective-permute-start.3 = (f32[12,40,4]{2,1,0:T(8,128)}, f32[12,40,4]{2,1,0:T(8,128)}, u32[]{:S(2)}, u32[]{:S(2)}) collective-permute-start(f32[12,40,4]{2,1,0:T(8,128)} %get-tuple-element.39), channel_id=1, source_target_pairs={{1,0},{2,1},{3,2},{5,4},{6,5},{7,6},{9,8},{10,9},{11,10},{13,12},{... | collective-permute-start | bytes 23048 | tf_op jit(solution)/shard_map/ppermute | solution.py:34
  99.9 3.7 %collective-permute-start.4 = (f32[62,1,256]{2,1,0:T(1,128)}, f32[62,1,256]{2,1,0:T(1,128)}, u32[]{:S(2)}, u32[]{:S(2)}) collective-permute-start(f32[62,1,256]{2,1,0:T(1,128)} %get-tuple-element.33), channel_id=1, source_target_pairs={{4,0},{8,4},{12,8},{16,12},{20,16},{24,20},{28,24},{32,28},{36,32}... | collective-permute-start | bytes 190472 | tf_op jit(solution)/shard_map/ppermute | solution.py:44
  105.3 2.5 %copy.26 = f32[62,32,1]{2,1,0:T(8,128)} copy(f32[62,32,1]{0,1,2:T(8,128)} %collective-permute-done.6) | data formatting | bytes 15872 | tf_op jit(solution)/shard_map/ppermute | solution.py:46
  107.8 8.6 %collective-permute-done.2 = f32[12,40,4]{2,1,0:T(8,128)} collective-permute-done((f32[12,40,4]{2,1,0:T(8,128)}, f32[12,40,4]{2,1,0:T(8,128)}, u32[]{:S(2)}, u32[]{:S(2)}) %collective-permute-start.2) | collective-permute-done | bytes 7712 | tf_op jit(solution)/shard_map/ppermute | solution.py:33
  120.0 3.3 %fusion.3 = f32[148,512]{1,0:T(8,128)S(1)} fusion(bf16[148,4096]{0,1:T(8,128)(2,1)} %bitcast.27, s32[512]{0:T(512)} %get-tuple-element.70), kind=kOutput, calls=%fused_computation.7 | convolution fusion | flops 622854144 | bytes 1517568 | tf_op jit(solution)/shard_map/dot_general | solution.py:81
  123.3 3.3 %fusion.2 = f32[148,512]{1,0:T(8,128)S(1)} fusion(bf16[148,4096]{0,1:T(8,128)(2,1)} %bitcast.27, s32[512]{0:T(512)S(1)} %get-tuple-element.71), kind=kOutput, calls=%fused_computation.6 | convolution fusion | flops 622854144 | bytes 1517568 | tf_op jit(solution)/shard_map/dot_general | solution.py:81
  126.7 3.3 %fusion.1 = f32[148,512]{1,0:T(8,128)S(1)} fusion(bf16[148,4096]{0,1:T(8,128)(2,1)} %bitcast.27, s32[512]{0:T(512)S(1)} %get-tuple-element.72), kind=kOutput, calls=%fused_computation.5 | convolution fusion | flops 622854144 | bytes 1517568 | tf_op jit(solution)/shard_map/dot_general | solution.py:81
  130.0 3.3 %fusion = f32[148,512]{1,0:T(8,128)S(1)} fusion(bf16[148,4096]{0,1:T(8,128)(2,1)} %bitcast.27, s32[512]{0:T(512)S(1)} %get-tuple-element.69), kind=kOutput, calls=%fused_computation.4 | convolution fusion | flops 622854144 | bytes 1517568 | tf_op jit(solution)/shard_map/dot_general | solution.py:81
  133.5 2.1 %collective-permute-start.8 = (bf16[4,3,128]{2,1,0:T(4,128)(2,1)S(1)}, bf16[4,3,128]{2,1,0:T(4,128)(2,1)S(1)}, u32[]{:S(2)}, u32[]{:S(2)}) collective-permute-start(bf16[4,3,128]{2,1,0:T(4,128)(2,1)S(1)} %get-tuple-element.67), channel_id=1, source_target_pairs={{0,4},{4,8},{8,12},{12,16},{16,20},{20,24},{24,28},{28,32},{32,36}... | collective-permute-start | bytes 9224 | tf_op jit(solution)/shard_map/ppermute | solution.py:30
  135.6 5.8 %collective-permute-start.9 = (bf16[4,3,128]{2,1,0:T(4,128)(2,1)S(1)}, bf16[4,3,128]{2,1,0:T(4,128)(2,1)S(1)}, u32[]{:S(2)}, u32[]{:S(2)}) collective-permute-start(bf16[4,3,128]{2,1,0:T(4,128)(2,1)S(1)} %get-tuple-element.68), channel_id=1, source_target_pairs={{4,0},{8,4},{12,8},{16,12},{20,16},{24,20},{28,24},{32,28},{36,32}... | collective-permute-start | bytes 9224 | tf_op jit(solution)/shard_map/ppermute | solution.py:31
  143.0 3.1 %collective-permute-start.10 = (bf16[4,22,3]{2,1,0:T(8,128)(2,1)S(1)}, bf16[4,22,3]{2,1,0:T(8,128)(2,1)S(1)}, u32[]{:S(2)}, u32[]{:S(2)}) collective-permute-start(bf16[4,22,3]{2,1,0:T(8,128)(2,1)S(1)} %get-tuple-element.65), channel_id=1, source_target_pairs={{0,1},{1,2},{2,3},{4,5},{5,6},{6,7},{8,9},{9,10},{10,11},{12,13},{... | collective-permute-start | bytes 1592 | tf_op jit(solution)/shard_map/ppermute | solution.py:33
  146.1 2.7 %collective-permute-start.11 = (bf16[4,22,3]{2,1,0:T(8,128)(2,1)S(1)}, bf16[4,22,3]{2,1,0:T(8,128)(2,1)S(1)}, u32[]{:S(2)}, u32[]{:S(2)}) collective-permute-start(bf16[4,22,3]{2,1,0:T(8,128)(2,1)S(1)} %get-tuple-element.66), channel_id=1, source_target_pairs={{1,0},{2,1},{3,2},{5,4},{6,5},{7,6},{9,8},{10,9},{11,10},{13,12},{... | collective-permute-start | bytes 1592 | tf_op jit(solution)/shard_map/ppermute | solution.py:34
  150.0 1.8 %collective-permute-done.11 = bf16[4,22,3]{2,1,0:T(8,128)(2,1)S(1)} collective-permute-done((bf16[4,22,3]{2,1,0:T(8,128)(2,1)S(1)}, bf16[4,22,3]{2,1,0:T(8,128)(2,1)S(1)}, u32[]{:S(2)}, u32[]{:S(2)}) %collective-permute-start.11) | collective-permute-done | bytes 560 | tf_op jit(solution)/shard_map/ppermute | solution.py:34
  154.0 1.9 %convolution_convert_fusion.1 = bf16[88,792]{1,0:T(8,128)(2,1)} fusion(bf16[88,134]{1,0:T(8,128)(2,1)} %reshape.212, pred[134,264]{1,0:T(8,128)(4,1)} %iota_compare_fusion.19, pred[134,264]{1,0:T(8,128)(4,1)} %iota_compare_fusion.20, pred[134,264]{1,0:T(8,128)(4,1)} %iota_compare_fusion.21), kind=kOutput, calls=%fused_computation.86 | convolution fusion | flops 18960480 | bytes 269104 | tf_op jit(solution)/shard_map/dot_general | solution.py:129
  166.9 2.7 %fusion.57 = f32[62,32,256]{2,1,0:T(8,128)S(1)} fusion(f32[62,32,256]{2,1,0:T(8,128)S(1)} %copy-done.1, f32[62,1,256]{2,1,0:T(1,128)} %collective-permute-done.4, f32[62,31,256]{2,1,0:T(8,128)S(1)} %copy-done.6, f32[62,31,256]{2,1,0:T(8,128)S(1)} %copy-done.5, f32[62,1,256]{2,1,0:T(1,128)} %collective-permute-done.5, f32[62,32,1]{2,1,0:T(8,128)S(1)} %copy-done.9, ...), kind=kLoop, calls=%fused_computation.69 | loop fusion | flops 8634368 | bytes 12320768 | tf_op jit(solution)/shard_map/add | solution.py:161
  (170 shorter events, 52.1 us)
Async XLA Ops:
  0.6 75.6 %copy-start = (bf16[144,4]{0,1:T(4,128)(2,1)S(1)}, bf16[144,4]{0,1:T(4,128)(2,1)}, u32[]{:S(2)}) copy-start(bf16[144,4]{0,1:T(4,128)(2,1)} %param.15) | copy-start | bytes 3460
  0.6 17.4 %copy-start.7 = (f32[144,2048]{1,0:T(8,128)S(1)}, f32[144,2048]{1,0:T(8,128)}, u32[]{:S(2)}) copy-start(f32[144,2048]{1,0:T(8,128)} %param.12) | copy-start | bytes 3538948
  2.7 164.0 %collective-permute-start.5 = (f32[62,1,256]{2,1,0:T(1,128)}, f32[62,1,256]{2,1,0:T(1,128)}, u32[]{:S(2)}, u32[]{:S(2)}) collective-permute-start(f32[62,1,256]{2,1,0:T(1,128)} %get-tuple-element.32), channel_id=1, source_target_pairs={{0,4},{4,8},{8,12},{12,16},{16,20},{20,24},{24,28},{28,32},{32,36}... | collective-permute-start | bytes 190472 | tf_op jit(solution)/shard_map/ppermute | solution.py:43
  9.5 81.8 %collective-permute-start = (f32[12,4,256]{2,1,0:T(4,128)}, f32[12,4,256]{2,1,0:T(4,128)S(1)}, u32[]{:S(2)}, u32[]{:S(2)}) collective-permute-start(f32[12,4,256]{2,1,0:T(4,128)} %get-tuple-element.40), channel_id=1, source_target_pairs={{0,4},{4,8},{8,12},{12,16},{16,20},{20,24},{24,28},{28,32},{32,36}... | collective-permute-start | bytes 147464 | tf_op jit(solution)/shard_map/ppermute | solution.py:30
  13.0 78.2 %collective-permute-start.1 = (f32[12,4,256]{2,1,0:T(4,128)}, f32[12,4,256]{2,1,0:T(4,128)S(1)}, u32[]{:S(2)}, u32[]{:S(2)}) collective-permute-start(f32[12,4,256]{2,1,0:T(4,128)} %get-tuple-element.41), channel_id=1, source_target_pairs={{4,0},{8,4},{12,8},{16,12},{20,16},{24,20},{28,24},{32,28},{36,32}... | collective-permute-start | bytes 147464 | tf_op jit(solution)/shard_map/ppermute | solution.py:31
  29.9 8.6 %copy-start.1 = (f32[62,32,256]{2,1,0:T(8,128)S(1)}, f32[62,32,256]{2,1,0:T(8,128)}, u32[]{:S(2)}) copy-start(f32[62,32,256]{2,1,0:T(8,128)} %param.19) | copy-start | bytes 6094852
  29.9 37.1 %all-to-all-start = ((bf16[144,128,32]{0,2,1:T(8,128)(2,1)}), bf16[144,128,32]{0,2,1:T(8,128)(2,1)}, u32[]{:S(2)}, u32[]{:S(2)}) async-start(bf16[144,128,32]{0,2,1:T(8,128)(2,1)} %bitcast.209), calls=%async_computation | async-start | bytes 4194304 | tf_op jit(solution)/shard_map/all_to_all | solution.py:247
  42.2 63.2 %collective-permute-start.6 = (f32[62,32,1]{0,1,2:T(8,128)}, f32[62,32,1]{0,1,2:T(8,128)}, u32[]{:S(2)}, u32[]{:S(2)}) collective-permute-start(f32[62,32,1]{0,1,2:T(8,128)} %copy.29), channel_id=1, source_target_pairs={{1,0},{2,1},{3,2},{5,4},{6,5},{7,6},{9,8},{10,9},{11,10},{13,12},{... | collective-permute-start | bytes 23816 | tf_op jit(solution)/shard_map/ppermute | solution.py:46
  46.0 53.4 %collective-permute-start.7 = (f32[62,32,1]{0,1,2:T(8,128)}, f32[62,32,1]{0,1,2:T(8,128)S(1)}, u32[]{:S(2)}, u32[]{:S(2)}) collective-permute-start(f32[62,32,1]{0,1,2:T(8,128)} %copy.30), channel_id=1, source_target_pairs={{0,1},{1,2},{2,3},{4,5},{5,6},{6,7},{8,9},{9,10},{10,11},{12,13},{... | collective-permute-start | bytes 23816 | tf_op jit(solution)/shard_map/ppermute | solution.py:45
  57.7 13.0 %copy-start.15 = (bf16[1,4,144,144]{3,2,1,0:T(8,128)(2,1)S(1)}, bf16[1,4,144,144]{3,2,1,0:T(8,128)(2,1)}, u32[]{:S(2)}) copy-start(bf16[1,4,144,144]{3,2,1,0:T(8,128)(2,1)} %param.14) | copy-start | bytes 497668
  81.3 38.6 %all-to-all-start.1 = ((bf16[148,128,32]{0,2,1:T(8,128)(2,1)}), bf16[148,128,32]{0,2,1:T(8,128)(2,1)}, u32[]{:S(2)}, u32[]{:S(2)}) async-start(bf16[148,128,32]{0,2,1:T(8,128)(2,1)} %bitcast.210), calls=%async_computation.1 | async-start | bytes 4194304 | tf_op jit(solution)/shard_map/all_to_all | solution.py:249
  91.3 27.6 %copy-start.11 = (f32[12,4,256]{2,1,0:T(4,128)}, f32[12,4,256]{2,1,0:T(4,128)S(1)}, u32[]{:S(2)}) copy-start(f32[12,4,256]{2,1,0:T(4,128)S(1)} %collective-permute-done.1) | copy-start | bytes 147460
  92.2 24.2 %collective-permute-start.2 = (f32[12,40,4]{2,1,0:T(8,128)}, f32[12,40,4]{2,1,0:T(8,128)}, u32[]{:S(2)}, u32[]{:S(2)}) collective-permute-start(f32[12,40,4]{2,1,0:T(8,128)} %get-tuple-element.38), channel_id=1, source_target_pairs={{0,1},{1,2},{2,3},{4,5},{5,6},{6,7},{8,9},{9,10},{10,11},{12,13},{... | collective-permute-start | bytes 23048 | tf_op jit(solution)/shard_map/ppermute | solution.py:33
  95.6 21.8 %collective-permute-start.3 = (f32[12,40,4]{2,1,0:T(8,128)}, f32[12,40,4]{2,1,0:T(8,128)}, u32[]{:S(2)}, u32[]{:S(2)}) collective-permute-start(f32[12,40,4]{2,1,0:T(8,128)} %get-tuple-element.39), channel_id=1, source_target_pairs={{1,0},{2,1},{3,2},{5,4},{6,5},{7,6},{9,8},{10,9},{11,10},{13,12},{... | collective-permute-start | bytes 23048 | tf_op jit(solution)/shard_map/ppermute | solution.py:34
  99.9 66.8 %collective-permute-start.4 = (f32[62,1,256]{2,1,0:T(1,128)}, f32[62,1,256]{2,1,0:T(1,128)}, u32[]{:S(2)}, u32[]{:S(2)}) collective-permute-start(f32[62,1,256]{2,1,0:T(1,128)} %get-tuple-element.33), channel_id=1, source_target_pairs={{4,0},{8,4},{12,8},{16,12},{20,16},{24,20},{28,24},{32,28},{36,32}... | collective-permute-start | bytes 190472 | tf_op jit(solution)/shard_map/ppermute | solution.py:44
  133.4 8.0 %copy-start.12 = (f32[12,4,256]{2,1,0:T(4,128)S(1)}, f32[12,4,256]{2,1,0:T(4,128)}, u32[]{:S(2)}) copy-start(f32[12,4,256]{2,1,0:T(4,128)} %copy-done.11) | copy-start | bytes 147460
  133.4 15.5 %copy-start.8 = (f32[144,2048]{1,0:T(8,128)S(1)}, f32[144,2048]{1,0:T(8,128)}, u32[]{:S(2)}) copy-start(f32[144,2048]{1,0:T(8,128)} %param.12) | copy-start | bytes 3538948
  133.5 9.4 %collective-permute-start.8 = (bf16[4,3,128]{2,1,0:T(4,128)(2,1)S(1)}, bf16[4,3,128]{2,1,0:T(4,128)(2,1)S(1)}, u32[]{:S(2)}, u32[]{:S(2)}) collective-permute-start(bf16[4,3,128]{2,1,0:T(4,128)(2,1)S(1)} %get-tuple-element.67), channel_id=1, source_target_pairs={{0,4},{4,8},{8,12},{12,16},{16,20},{20,24},{24,28},{28,32},{32,36}... | collective-permute-start | bytes 9224 | tf_op jit(solution)/shard_map/ppermute | solution.py:30
  135.6 7.3 %collective-permute-start.9 = (bf16[4,3,128]{2,1,0:T(4,128)(2,1)S(1)}, bf16[4,3,128]{2,1,0:T(4,128)(2,1)S(1)}, u32[]{:S(2)}, u32[]{:S(2)}) collective-permute-start(bf16[4,3,128]{2,1,0:T(4,128)(2,1)S(1)} %get-tuple-element.68), channel_id=1, source_target_pairs={{4,0},{8,4},{12,8},{16,12},{20,16},{24,20},{28,24},{32,28},{36,32}... | collective-permute-start | bytes 9224 | tf_op jit(solution)/shard_map/ppermute | solution.py:31
  143.0 7.0 %collective-permute-start.10 = (bf16[4,22,3]{2,1,0:T(8,128)(2,1)S(1)}, bf16[4,22,3]{2,1,0:T(8,128)(2,1)S(1)}, u32[]{:S(2)}, u32[]{:S(2)}) collective-permute-start(bf16[4,22,3]{2,1,0:T(8,128)(2,1)S(1)} %get-tuple-element.65), channel_id=1, source_target_pairs={{0,1},{1,2},{2,3},{4,5},{5,6},{6,7},{8,9},{9,10},{10,11},{12,13},{... | collective-permute-start | bytes 1592 | tf_op jit(solution)/shard_map/ppermute | solution.py:33
  146.1 5.7 %collective-permute-start.11 = (bf16[4,22,3]{2,1,0:T(8,128)(2,1)S(1)}, bf16[4,22,3]{2,1,0:T(8,128)(2,1)S(1)}, u32[]{:S(2)}, u32[]{:S(2)}) collective-permute-start(bf16[4,22,3]{2,1,0:T(8,128)(2,1)S(1)} %get-tuple-element.66), channel_id=1, source_target_pairs={{1,0},{2,1},{3,2},{5,4},{6,5},{7,6},{9,8},{10,9},{11,10},{13,12},{... | collective-permute-start | bytes 1592 | tf_op jit(solution)/shard_map/ppermute | solution.py:34
  157.5 3.8 %copy-start.16 = (f32[40,264]{1,0:T(8,128)S(1)}, f32[40,264]{1,0:T(8,128)}, u32[]{:S(2)}) copy-start(f32[40,264]{1,0:T(8,128)} %get-tuple-element.16) | copy-start | bytes 126724
  157.5 3.8 %copy-start.17 = (f32[40,264]{1,0:T(8,128)S(1)}, f32[40,264]{1,0:T(8,128)}, u32[]{:S(2)}) copy-start(f32[40,264]{1,0:T(8,128)} %get-tuple-element.17) | copy-start | bytes 126724
  157.5 3.8 %copy-start.18 = (f32[40,264]{1,0:T(8,128)S(1)}, f32[40,264]{1,0:T(8,128)}, u32[]{:S(2)}) copy-start(f32[40,264]{1,0:T(8,128)} %get-tuple-element.18) | copy-start | bytes 126724
  157.5 3.8 %copy-start.19 = (f32[40,264]{1,0:T(8,128)S(1)}, f32[40,264]{1,0:T(8,128)}, u32[]{:S(2)}) copy-start(f32[40,264]{1,0:T(8,128)} %get-tuple-element.19) | copy-start | bytes 126724
  157.5 3.9 %copy-start.20 = (f32[40,264]{1,0:T(8,128)S(1)}, f32[40,264]{1,0:T(8,128)}, u32[]{:S(2)}) copy-start(f32[40,264]{1,0:T(8,128)} %get-tuple-element.20) | copy-start | bytes 126724
  157.5 3.9 %copy-start.21 = (f32[40,264]{1,0:T(8,128)S(1)}, f32[40,264]{1,0:T(8,128)}, u32[]{:S(2)}) copy-start(f32[40,264]{1,0:T(8,128)} %get-tuple-element.21) | copy-start | bytes 126724
  157.5 3.9 %copy-start.22 = (f32[40,264]{1,0:T(8,128)S(1)}, f32[40,264]{1,0:T(8,128)}, u32[]{:S(2)}) copy-start(f32[40,264]{1,0:T(8,128)} %get-tuple-element.22) | copy-start | bytes 126724
  157.5 3.9 %copy-start.23 = (f32[40,264]{1,0:T(8,128)S(1)}, f32[40,264]{1,0:T(8,128)}, u32[]{:S(2)}) copy-start(f32[40,264]{1,0:T(8,128)} %get-tuple-element.23) | copy-start | bytes 126724
  157.5 3.9 %copy-start.24 = (f32[40,264]{1,0:T(8,128)S(1)}, f32[40,264]{1,0:T(8,128)}, u32[]{:S(2)}) copy-start(f32[40,264]{1,0:T(8,128)} %get-tuple-element.24) | copy-start | bytes 126724
  161.4 5.3 %copy-start.9 = (f32[62,32,1]{2,1,0:T(8,128)S(1)}, f32[62,32,1]{2,1,0:T(8,128)}, u32[]{:S(2)}) copy-start(f32[62,32,1]{2,1,0:T(8,128)} %copy.26) | copy-start | bytes 23812
  161.9 4.8 %copy-start.6 = (f32[62,31,256]{2,1,0:T(8,128)S(1)}, f32[62,31,256]{2,1,0:T(8,128)}, u32[]{:S(2)}) copy-start(f32[62,31,256]{2,1,0:T(8,128)} %get-tuple-element.35) | copy-start | bytes 5904388
  (15 other events, 23.0 us)
where the time goes:
time: 173 us; the launch traced here: 171 us
  starting transfers between devices  54.8 us (32%)
  local copies, waits for them, and re-layouts  41 us (24%)
  matrix products  30.9 us (18%)
  other arithmetic  22 us (13%)
  waiting for transfers between devices  20.6 us (12%)
    dot_general x4, matrix products, fetch_columns(): pieces.append(jnp.dot(source, selector, preferred_element_type=jnp.float32))  13.4 us
    ppermute x2, starting transfers between devices, with_halo(): lax.ppermute(cells[..., :width, :], 'wide', shift_pairs(wide_count, -1))  9.84 us
    all_to_all x1, waiting for transfers between devices, per_device(): lax.all_to_all(outgoing, ('wide', 'narrow'), split_axis=1, concat_axis=1,...  9.27 us
    unnamed x72, local copies, waits for them, and re-layouts  9.1 us
    ppermute x2, waiting for transfers between devices, with_halo(): lax.ppermute(cells[..., cols - width:], 'narrow', shift_pairs(narrow_coun...  8.61 us
    all_to_all x1, starting transfers between devices, per_device(): lax.all_to_all(outgoing, ('wide', 'narrow'), split_axis=1, concat_axis=1,...  8.56 us
    dot_general x8, matrix products, place_columns(): jnp.dot(source, selector, preferred_element_type=jnp.float32)  6.97 us
    all_to_all x1, starting transfers between devices, per_device(): lax.all_to_all(jnp.concatenate([tendency, fluxes], axis=0), ('wide', 'nar...  6.85 us
  transfers between devices with their start and end apart: 14, of which 4 were waited for; matrix products, arithmetic and copies ran while one was open for 50% of the time, Pallas kernels for 0%

commit v1 on v0

--- a/solution.py
+++ b/solution.py
@@ -61,43 +61,28 @@
     width = block_width()
     pieces = []
     for start in range(0, total, width):
-        selector = (slots[:, None] == (start + jnp.arange(width, dtype=jnp.int32))[None, :]).astype(
+        selector = ((start + jnp.arange(width, dtype=jnp.int32))[:, None] == slots[None, :]).astype(
             jnp.bfloat16
         )
         pieces.append(
-            jnp.dot(source, selector, preferred_element_type=jnp.float32).astype(jnp.bfloat16)
-        )
-    return jnp.concatenate(pieces, axis=1)
-
-
-def fetch_columns(source, slots):
-    count = slots.shape[0]
-    width = block_width()
-    lanes = jnp.arange(source.shape[1], dtype=jnp.int32)
-    pieces = []
-    for start in range(0, count, width):
-        wanted = slots[start : start + width]
-        selector = (lanes[:, None] == wanted[None, :]).astype(jnp.bfloat16)
-        pieces.append(jnp.dot(source, selector, preferred_element_type=jnp.float32))
-    return jnp.concatenate(pieces, axis=1)
+            lax.dot_general(
+                selector, source, (((1,), (1,)), ((), ())), preferred_element_type=jnp.float32
+            ).astype(jnp.bfloat16)
+        )
+    return jnp.concatenate(pieces, axis=0)
 
 
 def physics(operators, columns, flux_map):
     initial = columns.astype(jnp.float32)
     current = initial
     for sweep in range(operators.shape[0]):
-        mixed = lax.dot_general(
-            operators[sweep],
-            current.astype(jnp.bfloat16),
-            (((0,), (0,)), ((), ())),
-            preferred_element_type=jnp.float32,
+        mixed = jnp.dot(
+            current.astype(jnp.bfloat16), operators[sweep], preferred_element_type=jnp.float32
         )
         current = current + relax_rate * jnp.tanh(mixed)
     final = current.astype(jnp.bfloat16)
     tendency = (current - initial).astype(jnp.bfloat16)
-    fluxes = lax.dot_general(
-        flux_map, final, (((0,), (0,)), ((), ())), preferred_element_type=jnp.float32
-    ).astype(jnp.bfloat16)
+    fluxes = jnp.dot(final, flux_map, preferred_element_type=jnp.float32).astype(jnp.bfloat16)
     return (tendency, fluxes)
 
 
@@ -244,18 +229,18 @@
     slots = owners * capacity + column_ranks(owners, peers)
     initial = atm_state.astype(jnp.bfloat16)
     outgoing = place_columns(initial, slots, total_slots)
-    arrived = lax.all_to_all(outgoing, ("wide", "narrow"), split_axis=1, concat_axis=1, tiled=True)
+    arrived = lax.all_to_all(outgoing, ("wide", "narrow"), split_axis=0, concat_axis=0, tiled=True)
     tendency, fluxes = physics(regime_ops[0], arrived, flux_map)
     back = lax.all_to_all(
-        jnp.concatenate([tendency, fluxes], axis=0),
+        jnp.concatenate([tendency, fluxes], axis=1),
         ("wide", "narrow"),
-        split_axis=1,
-        concat_axis=1,
+        split_axis=0,
+        concat_axis=0,
         tiled=True,
     )
-    returned = fetch_columns(back, slots)
-    tend_cols = returned[:features]
-    flux_cols = returned[features:]
+    returned = jnp.take(back, slots, axis=0, mode="clip")
+    tend_cols = returned[:, :features].T.astype(jnp.float32)
+    flux_cols = returned[:, features:].T
     atm_new = atm_state + tend_cols
 
     flux_block = flux_cols.astype(jnp.bfloat16).reshape(nflux, block_rows, AC)

time: 173 us -> 155 us (0.90)
  matrix products: 30.9 us -> 14 us
  waiting for transfers between devices: 20.6 us -> 10.3 us
  local copies, waits for them, and re-layouts: 41 us -> 50 us
  starting transfers between devices: 54.8 us -> 57.3 us
  other arithmetic: 22 us -> 19.7 us
    dot_general x17 -> x13, matrix products: 25.3 us -> 12.9 us  [the longest x8 7.89 us: place_columns(): lax.dot_general(selector, source, (((1,), (1,)), ((), ())), preferred_ele...]
    all_to_all x2, waiting for transfers between devices: 9.27 us -> 0.01 us  [the longest x1 0.01 us: per_device(): lax.all_to_all(outgoing, ('wide', 'narrow'), split_axis=0, concat_axis=0,...]
    gather x0 -> x1, local copies, waits for them, and re-layouts: none -> 8.49 us  [per_device(): returned = jnp.take(back, slots, axis=0, mode='clip')]
    all_to_all x2, starting transfers between devices: 15.4 us -> 19.6 us  [the longest x1 10.7 us: per_device(): lax.all_to_all(outgoing, ('wide', 'narrow'), split_axis=0, concat_axis=0,...]
    unnamed x72 -> x110, local copies, waits for them, and re-layouts: 9.1 us -> 13.1 us
    dot_general x3, matrix products: 3.71 us -> 0.84 us  [remap(): jnp.einsum('ap,fpx->fax', row_sel, by_cols, preferred_element_type=jnp.fl...]
    add x1, other arithmetic: 1.14 us -> 3.22 us  [per_device(): atm_new = atm_state + tend_cols]
    mul x5, other arithmetic: 2.28 us -> 0.42 us  [momentum(): mask * mask_next]
  transfers between devices with their start and end apart: 14 -> 14, of which waited for: 4 -> 2; matrix products, arithmetic and copies ran while one was open for 50% -> 42% of each run, Pallas kernels for 0% -> 0%
where the time goes in v1:
time: 155 us; the launch traced here: 153 us
  starting transfers between devices  57.3 us (37%)
  local copies, waits for them, and re-layouts  50 us (32%)
  other arithmetic  19.7 us (13%)
  matrix products  14 us (9%)
  waiting for transfers between devices  10.3 us (7%)
  between operations  1.73 us (1%)
    unnamed x110, local copies, waits for them, and re-layouts  13.1 us
    ppermute x2, starting transfers between devices, with_halo(): lax.ppermute(cells[..., :width, :], 'wide', shift_pairs(wide_count, -1))  11.4 us
    all_to_all x1, starting transfers between devices, per_device(): lax.all_to_all(outgoing, ('wide', 'narrow'), split_axis=0, concat_axis=0,...  10.7 us
    ppermute x2, waiting for transfers between devices, with_halo(): lax.ppermute(cells[..., cols - width:], 'narrow', shift_pairs(narrow_coun...  9.38 us
    all_to_all x1, starting transfers between devices, per_device(): lax.all_to_all(jnp.concatenate([tendency, fluxes], axis=1), ('wide', 'nar...  8.97 us
    gather x1, local copies, waits for them, and re-layouts, per_device(): returned = jnp.take(back, slots, axis=0, mode='clip')  8.49 us
    dot_general x8, matrix products, place_columns(): lax.dot_general(selector, source, (((1,), (1,)), ((), ())), preferred_ele...  7.89 us
    ppermute x2, starting transfers between devices, with_halo(): lax.ppermute(cells[..., cols - width:], 'narrow', shift_pairs(narrow_coun...  6.47 us
  transfers between devices with their start and end apart: 14, of which 2 were waited for; matrix products, arithmetic and copies ran while one was open for 42% of the time, Pallas kernels for 0%

profile of v1, /device:TPU:34, one launch (start us, length us, event | category | flops | bytes accessed | tf_op | source)
XLA Modules:
  0.0 153.1 jit_solution(5592208041068634326)
XLA Ops:
  11.9 2.4 %copy.30 = bf16[4096,144]{1,0:T(8,128)(2,1)} copy(bf16[4096,144]{0,1:T(8,128)(2,1)S(1)} %fusion.93) | data formatting | bytes 2359296 | tf_op jit(solution)/shard_map/concatenate | solution.py:72
  14.3 10.7 %all-to-all-start = ((bf16[128,32,144]{2,1,0:T(8,128)(2,1)}), bf16[128,32,144]{2,1,0:T(8,128)(2,1)}, u32[]{:S(2)}, u32[]{:S(2)}) async-start(bf16[128,32,144]{2,1,0:T(8,128)(2,1)} %bitcast.155), calls=%async_computation | async-start | bytes 4194304 | tf_op jit(solution)/shard_map/all_to_all | solution.py:232
  25.8 2.0 %collective-permute-start = (f32[12,4,256]{2,1,0:T(4,128)}, f32[12,4,256]{2,1,0:T(4,128)S(1)}, u32[]{:S(2)}, u32[]{:S(2)}) collective-permute-start(f32[12,4,256]{2,1,0:T(4,128)} %get-tuple-element.52), channel_id=1, source_target_pairs={{0,4},{4,8},{8,12},{12,16},{16,20},{20,24},{24,28},{28,32},{32,36}... | collective-permute-start | bytes 147464 | tf_op jit(solution)/shard_map/ppermute | solution.py:30
  27.8 5.6 %collective-permute-start.1 = (f32[12,4,256]{2,1,0:T(4,128)}, f32[12,4,256]{2,1,0:T(4,128)S(1)}, u32[]{:S(2)}, u32[]{:S(2)}) collective-permute-start(f32[12,4,256]{2,1,0:T(4,128)} %get-tuple-element.53), channel_id=1, source_target_pairs={{4,0},{8,4},{12,8},{16,12},{20,16},{24,20},{28,24},{32,28},{36,32}... | collective-permute-start | bytes 147464 | tf_op jit(solution)/shard_map/ppermute | solution.py:31
  33.5 1.3 fusion.149
  34.8 2.4 %copy.42 = f32[62,32,1]{0,1,2:T(8,128)} copy(f32[62,32,1]{2,1,0:T(8,128)} %get-tuple-element.41) | data formatting | bytes 15872
  37.2 2.4 %collective-permute-start.6 = (f32[62,32,1]{0,1,2:T(8,128)}, f32[62,32,1]{0,1,2:T(8,128)}, u32[]{:S(2)}, u32[]{:S(2)}) collective-permute-start(f32[62,32,1]{0,1,2:T(8,128)} %copy.42), channel_id=1, source_target_pairs={{1,0},{2,1},{3,2},{5,4},{6,5},{7,6},{9,8},{10,9},{11,10},{13,12},{... | collective-permute-start | bytes 23816 | tf_op jit(solution)/shard_map/ppermute | solution.py:46
  39.6 1.3 copy.43
  41.0 3.4 %collective-permute-start.7 = (f32[62,32,1]{0,1,2:T(8,128)}, f32[62,32,1]{0,1,2:T(8,128)S(1)}, u32[]{:S(2)}, u32[]{:S(2)}) collective-permute-start(f32[62,32,1]{0,1,2:T(8,128)} %copy.43), channel_id=1, source_target_pairs={{0,1},{1,2},{2,3},{4,5},{5,6},{6,7},{8,9},{9,10},{10,11},{12,13},{... | collective-permute-start | bytes 23816 | tf_op jit(solution)/shard_map/ppermute | solution.py:45
  45.1 2.1 %collective-permute-start.4 = (f32[62,1,256]{2,1,0:T(1,128)}, f32[62,1,256]{2,1,0:T(1,128)}, u32[]{:S(2)}, u32[]{:S(2)}) collective-permute-start(f32[62,1,256]{2,1,0:T(1,128)} %get-tuple-element.45), channel_id=1, source_target_pairs={{4,0},{8,4},{12,8},{16,12},{20,16},{24,20},{28,24},{32,28},{36,32}... | collective-permute-start | bytes 190472 | tf_op jit(solution)/shard_map/ppermute | solution.py:44
  52.0 2.8 %fusion.150 = (f32[62,32,255]{2,1,0:T(8,128)}, f32[62,32,255]{2,1,0:T(8,128)}) fusion(f32[62,32,256]{2,1,0:T(8,128)S(1)} %copy-done.1), kind=kLoop, calls=%fused_computation.241 | loop fusion | bytes 8094720 | tf_op jit(solution)/shard_map/slice | solution.py:138
  54.8 3.8 %copy.31 = bf16[4096,144]{0,1:T(8,128)(2,1)} copy(bf16[4096,144]{1,0:T(8,128)(2,1)} %bitcast.6) | data formatting | bytes 2359296 | tf_op jit(solution)/shard_map/all_to_all | solution.py:232
  58.6 2.8 %fusion.7 = f32[4096,144]{0,1:T(8,128)S(1)} fusion(bf16[4096,144]{1,0:T(8,128)(2,1)} %bitcast.6, bf16[4096,144]{0,1:T(8,128)(2,1)} %copy.31, bf16[1,4,144,144]{3,2,1,0:T(8,128)(2,1)S(1)} %copy-done.21), kind=kOutput, calls=%fused_computation.12 | convolution fusion | flops 171638784 | bytes 4792320 | tf_op jit(solution)/shard_map/dot_general | solution.py:79
  65.5 3.7 %copy.32 = bf16[4096,148]{1,0:T(8,128)(2,1)} copy(bf16[4096,148]{0,1:T(8,128)(2,1)} %pad_maximum_fusion) | data formatting | bytes 2424832 | tf_op jit(solution)/shard_map/concatenate | solution.py:235
  69.1 9.0 %all-to-all-start.1 = ((bf16[128,32,148]{2,1,0:T(8,128)(2,1)}), bf16[128,32,148]{2,1,0:T(8,128)(2,1)}, u32[]{:S(2)}, u32[]{:S(2)}) async-start(bf16[128,32,148]{2,1,0:T(8,128)(2,1)} %bitcast.156), calls=%async_computation.1 | async-start | bytes 4194304 | tf_op jit(solution)/shard_map/all_to_all | solution.py:234
  78.1 2.5 %fusion.152 = (f32[62,31,256]{2,1,0:T(8,128)}, f32[62,31,256]{2,1,0:T(8,128)}) fusion(f32[62,32,256]{2,1,0:T(8,128)S(1)} %copy-done.1), kind=kLoop, calls=%fused_computation.243 | loop fusion | bytes 7872512 | tf_op jit(solution)/shard_map/slice | solution.py:136
  81.4 3.4 %collective-permute-start.2 = (f32[12,40,4]{2,1,0:T(8,128)S(1)}, f32[12,40,4]{2,1,0:T(8,128)S(1)}, u32[]{:S(2)}, u32[]{:S(2)}) collective-permute-start(f32[12,40,4]{2,1,0:T(8,128)S(1)} %get-tuple-element.50), channel_id=1, source_target_pairs={{0,1},{1,2},{2,3},{4,5},{5,6},{6,7},{8,9},{9,10},{10,11},{12,13},{... | collective-permute-start | bytes 23048 | tf_op jit(solution)/shard_map/ppermute | solution.py:33
  84.8 2.5 %collective-permute-start.3 = (f32[12,40,4]{2,1,0:T(8,128)S(1)}, f32[12,40,4]{2,1,0:T(8,128)S(1)}, u32[]{:S(2)}, u32[]{:S(2)}) collective-permute-start(f32[12,40,4]{2,1,0:T(8,128)S(1)} %get-tuple-element.51), channel_id=1, source_target_pairs={{1,0},{2,1},{3,2},{5,4},{6,5},{7,6},{9,8},{10,9},{11,10},{13,12},{... | collective-permute-start | bytes 23048 | tf_op jit(solution)/shard_map/ppermute | solution.py:34
  87.8 2.8 %copy.33 = f32[144,2048]{0,1:T(8,128)} copy(f32[144,2048]{1,0:T(8,128)} %param.12) | data formatting | bytes 2359296 | tf_op args[0]
  90.6 1.9 %collective-permute-start.5 = (f32[62,1,256]{2,1,0:T(1,128)}, f32[62,1,256]{2,1,0:T(1,128)}, u32[]{:S(2)}, u32[]{:S(2)}) collective-permute-start(f32[62,1,256]{2,1,0:T(1,128)} %get-tuple-element.44), channel_id=1, source_target_pairs={{0,4},{4,8},{8,12},{12,16},{16,20},{20,24},{24,28},{28,32},{32,36}... | collective-permute-start | bytes 190472 | tf_op jit(solution)/shard_map/ppermute | solution.py:43
  92.5 2.5 %copy.35 = f32[62,32,1]{2,1,0:T(8,128)} copy(f32[62,32,1]{0,1,2:T(8,128)} %collective-permute-done.6) | data formatting | bytes 15872 | tf_op jit(solution)/shard_map/ppermute | solution.py:46
  95.0 1.8 %copy.37 = f32[62,32,1]{2,1,0:T(8,128)} copy(f32[62,32,1]{0,1,2:T(8,128)S(1)} %collective-permute-done.7) | data formatting | bytes 15872 | tf_op jit(solution)/shard_map/ppermute | solution.py:45
  96.9 9.4 %collective-permute-done.2 = f32[12,40,4]{2,1,0:T(8,128)S(1)} collective-permute-done((f32[12,40,4]{2,1,0:T(8,128)S(1)}, f32[12,40,4]{2,1,0:T(8,128)S(1)}, u32[]{:S(2)}, u32[]{:S(2)}) %collective-permute-start.2) | collective-permute-done | bytes 7712 | tf_op jit(solution)/shard_map/ppermute | solution.py:33
  108.7 8.5 %gather_fusion = bf16[2048,148]{1,0:T(8,128)(2,1)S(1)} fusion(bf16[4096,148]{1,0:T(8,128)(2,1)} %bitcast.12, s32[2048]{0:T(1024)S(1)} %broadcast_clamp_fusion), kind=kCustom, calls=%fused_computation | custom fusion | bytes 1220608 | tf_op jit(solution)/shard_map/jit(_take)/gather | solution.py:241
  119.5 1.9 %collective-permute-start.8 = (bf16[4,3,128]{2,1,0:T(4,128)(2,1)S(1)}, bf16[4,3,128]{2,1,0:T(4,128)(2,1)S(1)}, u32[]{:S(2)}, u32[]{:S(2)}) collective-permute-start(bf16[4,3,128]{2,1,0:T(4,128)(2,1)S(1)} %get-tuple-element.79), channel_id=1, source_target_pairs={{0,4},{4,8},{8,12},{12,16},{16,20},{20,24},{24,28},{28,32},{32,36}... | collective-permute-start | bytes 9224 | tf_op jit(solution)/shard_map/ppermute | solution.py:30
  121.4 5.8 %collective-permute-start.9 = (bf16[4,3,128]{2,1,0:T(4,128)(2,1)S(1)}, bf16[4,3,128]{2,1,0:T(4,128)(2,1)S(1)}, u32[]{:S(2)}, u32[]{:S(2)}) collective-permute-start(bf16[4,3,128]{2,1,0:T(4,128)(2,1)S(1)} %get-tuple-element.80), channel_id=1, source_target_pairs={{4,0},{8,4},{12,8},{16,12},{20,16},{24,20},{28,24},{32,28},{36,32}... | collective-permute-start | bytes 9224 | tf_op jit(solution)/shard_map/ppermute | solution.py:31
  127.2 1.5 %maximum_bitcast_fusion.2 = (f32[39,264]{1,0:T(8,128)S(1)}, f32[39,264]{1,0:T(8,128)}) fusion(f32[12,40,4]{2,1,0:T(8,128)} %copy-done.12, f32[12,40,4]{2,1,0:T(8,128)} %copy-done.10, f32[12,4,256]{2,1,0:T(4,128)} %copy-done.17, f32[12,32,256]{2,1,0:T(8,128)S(1)} %constant_dynamic-update-slice_fusion, f32[12,4,256]{2,1,0:T(4,128)} %copy-done.15), kind=kLoop, calls=%fused_computation.151 | loop fusion | flops 82368 | bytes 589248 | tf_op jit(solution)/shard_map/slice | solution.py:164
  129.5 3.1 %collective-permute-start.10 = (bf16[4,22,3]{2,1,0:T(8,128)(2,1)}, bf16[4,22,3]{2,1,0:T(8,128)(2,1)}, u32[]{:S(2)}, u32[]{:S(2)}) collective-permute-start(bf16[4,22,3]{2,1,0:T(8,128)(2,1)} %get-tuple-element.77), channel_id=1, source_target_pairs={{0,1},{1,2},{2,3},{4,5},{5,6},{6,7},{8,9},{9,10},{10,11},{12,13},{... | collective-permute-start | bytes 1592 | tf_op jit(solution)/shard_map/ppermute | solution.py:33
  132.6 3.5 %collective-permute-start.11 = (bf16[4,22,3]{2,1,0:T(8,128)(2,1)}, bf16[4,22,3]{2,1,0:T(8,128)(2,1)}, u32[]{:S(2)}, u32[]{:S(2)}) collective-permute-start(bf16[4,22,3]{2,1,0:T(8,128)(2,1)} %get-tuple-element.78), channel_id=1, source_target_pairs={{1,0},{2,1},{3,2},{5,4},{6,5},{7,6},{9,8},{10,9},{11,10},{13,12},{... | collective-permute-start | bytes 1592 | tf_op jit(solution)/shard_map/ppermute | solution.py:34
  136.1 3.2 %bitcast_add_fusion = f32[144,2048]{0,1:T(8,128)} fusion(f32[144,2048]{0,1:T(8,128)} %copy.33, bf16[2048,148]{1,0:T(8,128)(2,1)S(1)} %gather_fusion), kind=kLoop, calls=%fused_computation.32 | loop fusion | flops 589824 | bytes 2949120 | tf_op jit(solution)/shard_map/add | solution.py:244
  139.4 2.7 %copy.41 = f32[144,2048]{1,0:T(8,128)} copy(f32[144,2048]{0,1:T(8,128)} %bitcast_add_fusion) | data formatting | bytes 2359296
  149.1 2.7 %fusion.44 = f32[62,32,256]{2,1,0:T(8,128)S(1)} fusion(f32[62,32,256]{2,1,0:T(8,128)S(1)} %copy-done.1, f32[62,1,256]{2,1,0:T(1,128)} %collective-permute-done.4, f32[62,31,256]{2,1,0:T(8,128)S(1)} %copy-done.6, f32[62,31,256]{2,1,0:T(8,128)S(1)} %copy-done.5, f32[62,1,256]{2,1,0:T(1,128)} %collective-permute-done.5, f32[62,32,1]{2,1,0:T(8,128)S(1)} %copy-done.8, ...), kind=kLoop, calls=%fused_computation.54 | loop fusion | flops 8634368 | bytes 12320768 | tf_op jit(solution)/shard_map/add | solution.py:146
  (206 shorter events, 36.0 us)
Async XLA Ops:
  0.6 63.4 %copy-start = (bf16[144,4]{0,1:T(4,128)(2,1)S(1)}, bf16[144,4]{0,1:T(4,128)(2,1)}, u32[]{:S(2)}) copy-start(bf16[144,4]{0,1:T(4,128)(2,1)} %param.15) | copy-start | bytes 3460
  14.3 10.7 %copy-start.19 = (s32[32,256]{1,0:T(8,128)S(1)}, s32[32,256]{1,0:T(8,128)}, u32[]{:S(2)}) copy-start(s32[32,256]{1,0:T(8,128)} %param.18) | copy-start | bytes 98308
  14.3 10.7 %copy-start.44 = (f32[32,256]{1,0:T(8,128)S(1)}, f32[32,256]{1,0:T(8,128)}, u32[]{:S(2)}) copy-start(f32[32,256]{1,0:T(8,128)} %param.20) | copy-start | bytes 98308
  14.3 10.8 %copy-start.40 = (f32[2,32,256]{2,1,0:T(8,128)S(1)}, f32[2,32,256]{2,1,0:T(8,128)}, u32[]{:S(2)}) copy-start(f32[2,32,256]{2,1,0:T(8,128)} %param.21) | copy-start | bytes 196612
  14.3 10.8 %copy-start.33 = (s32[4,32,256]{2,1,0:T(8,128)S(1)}, s32[4,32,256]{2,1,0:T(8,128)}, u32[]{:S(2)}) copy-start(s32[4,32,256]{2,1,0:T(8,128)} %param.16) | copy-start | bytes 393220
  14.3 10.8 %copy-start.34 = (f32[4,32,256]{2,1,0:T(8,128)S(1)}, f32[4,32,256]{2,1,0:T(8,128)}, u32[]{:S(2)}) copy-start(f32[4,32,256]{2,1,0:T(8,128)} %param.17) | copy-start | bytes 393220
  14.3 19.2 %copy-start.1 = (f32[62,32,256]{2,1,0:T(8,128)S(1)}, f32[62,32,256]{2,1,0:T(8,128)}, u32[]{:S(2)}) copy-start(f32[62,32,256]{2,1,0:T(8,128)} %param.19) | copy-start | bytes 6094852
  14.3 40.5 %all-to-all-start = ((bf16[128,32,144]{2,1,0:T(8,128)(2,1)}), bf16[128,32,144]{2,1,0:T(8,128)(2,1)}, u32[]{:S(2)}, u32[]{:S(2)}) async-start(bf16[128,32,144]{2,1,0:T(8,128)(2,1)} %bitcast.155), calls=%async_computation | async-start | bytes 4194304 | tf_op jit(solution)/shard_map/all_to_all | solution.py:232
  25.8 55.4 %collective-permute-start = (f32[12,4,256]{2,1,0:T(4,128)}, f32[12,4,256]{2,1,0:T(4,128)S(1)}, u32[]{:S(2)}, u32[]{:S(2)}) collective-permute-start(f32[12,4,256]{2,1,0:T(4,128)} %get-tuple-element.52), channel_id=1, source_target_pairs={{0,4},{4,8},{8,12},{12,16},{16,20},{20,24},{24,28},{28,32},{32,36}... | collective-permute-start | bytes 147464 | tf_op jit(solution)/shard_map/ppermute | solution.py:30
  27.8 53.4 %collective-permute-start.1 = (f32[12,4,256]{2,1,0:T(4,128)}, f32[12,4,256]{2,1,0:T(4,128)S(1)}, u32[]{:S(2)}, u32[]{:S(2)}) collective-permute-start(f32[12,4,256]{2,1,0:T(4,128)} %get-tuple-element.53), channel_id=1, source_target_pairs={{4,0},{8,4},{12,8},{16,12},{20,16},{24,20},{28,24},{32,28},{36,32}... | collective-permute-start | bytes 147464 | tf_op jit(solution)/shard_map/ppermute | solution.py:31
  37.2 53.4 %collective-permute-start.6 = (f32[62,32,1]{0,1,2:T(8,128)}, f32[62,32,1]{0,1,2:T(8,128)}, u32[]{:S(2)}, u32[]{:S(2)}) collective-permute-start(f32[62,32,1]{0,1,2:T(8,128)} %copy.42), channel_id=1, source_target_pairs={{1,0},{2,1},{3,2},{5,4},{6,5},{7,6},{9,8},{10,9},{11,10},{13,12},{... | collective-permute-start | bytes 23816 | tf_op jit(solution)/shard_map/ppermute | solution.py:46
  41.0 54.1 %collective-permute-start.7 = (f32[62,32,1]{0,1,2:T(8,128)}, f32[62,32,1]{0,1,2:T(8,128)S(1)}, u32[]{:S(2)}, u32[]{:S(2)}) collective-permute-start(f32[62,32,1]{0,1,2:T(8,128)} %copy.43), channel_id=1, source_target_pairs={{0,1},{1,2},{2,3},{4,5},{5,6},{6,7},{8,9},{9,10},{10,11},{12,13},{... | collective-permute-start | bytes 23816 | tf_op jit(solution)/shard_map/ppermute | solution.py:45
  45.1 103.2 %collective-permute-start.4 = (f32[62,1,256]{2,1,0:T(1,128)}, f32[62,1,256]{2,1,0:T(1,128)}, u32[]{:S(2)}, u32[]{:S(2)}) collective-permute-start(f32[62,1,256]{2,1,0:T(1,128)} %get-tuple-element.45), channel_id=1, source_target_pairs={{4,0},{8,4},{12,8},{16,12},{20,16},{24,20},{28,24},{32,28},{36,32}... | collective-permute-start | bytes 190472 | tf_op jit(solution)/shard_map/ppermute | solution.py:44
  54.8 3.8 %copy-start.21 = (bf16[1,4,144,144]{3,2,1,0:T(8,128)(2,1)S(1)}, bf16[1,4,144,144]{3,2,1,0:T(8,128)(2,1)}, u32[]{:S(2)}) copy-start(bf16[1,4,144,144]{3,2,1,0:T(8,128)(2,1)} %param.14) | copy-start | bytes 497668
  69.1 39.6 %all-to-all-start.1 = ((bf16[128,32,148]{2,1,0:T(8,128)(2,1)}), bf16[128,32,148]{2,1,0:T(8,128)(2,1)}, u32[]{:S(2)}, u32[]{:S(2)}) async-start(bf16[128,32,148]{2,1,0:T(8,128)(2,1)} %bitcast.156), calls=%async_computation.1 | async-start | bytes 4194304 | tf_op jit(solution)/shard_map/all_to_all | solution.py:234
  81.2 26.0 %copy-start.15 = (f32[12,4,256]{2,1,0:T(4,128)}, f32[12,4,256]{2,1,0:T(4,128)S(1)}, u32[]{:S(2)}) copy-start(f32[12,4,256]{2,1,0:T(4,128)S(1)} %collective-permute-done) | copy-start | bytes 147460
  81.2 26.0 %copy-start.17 = (f32[12,4,256]{2,1,0:T(4,128)}, f32[12,4,256]{2,1,0:T(4,128)S(1)}, u32[]{:S(2)}) copy-start(f32[12,4,256]{2,1,0:T(4,128)S(1)} %collective-permute-done.1) | copy-start | bytes 147460
  81.4 24.8 %collective-permute-start.2 = (f32[12,40,4]{2,1,0:T(8,128)S(1)}, f32[12,40,4]{2,1,0:T(8,128)S(1)}, u32[]{:S(2)}, u32[]{:S(2)}) collective-permute-start(f32[12,40,4]{2,1,0:T(8,128)S(1)} %get-tuple-element.50), channel_id=1, source_target_pairs={{0,1},{1,2},{2,3},{4,5},{5,6},{6,7},{8,9},{9,10},{10,11},{12,13},{... | collective-permute-start | bytes 23048 | tf_op jit(solution)/shard_map/ppermute | solution.py:33
  84.8 22.4 %collective-permute-start.3 = (f32[12,40,4]{2,1,0:T(8,128)S(1)}, f32[12,40,4]{2,1,0:T(8,128)S(1)}, u32[]{:S(2)}, u32[]{:S(2)}) collective-permute-start(f32[12,40,4]{2,1,0:T(8,128)S(1)} %get-tuple-element.51), channel_id=1, source_target_pairs={{1,0},{2,1},{3,2},{5,4},{6,5},{7,6},{9,8},{10,9},{11,10},{13,12},{... | collective-permute-start | bytes 23048 | tf_op jit(solution)/shard_map/ppermute | solution.py:34
  90.6 57.7 %collective-permute-start.5 = (f32[62,1,256]{2,1,0:T(1,128)}, f32[62,1,256]{2,1,0:T(1,128)}, u32[]{:S(2)}, u32[]{:S(2)}) collective-permute-start(f32[62,1,256]{2,1,0:T(1,128)} %get-tuple-element.44), channel_id=1, source_target_pairs={{0,4},{4,8},{8,12},{12,16},{16,20},{20,24},{24,28},{28,32},{32,36}... | collective-permute-start | bytes 190472 | tf_op jit(solution)/shard_map/ppermute | solution.py:43
  119.5 9.2 %collective-permute-start.8 = (bf16[4,3,128]{2,1,0:T(4,128)(2,1)S(1)}, bf16[4,3,128]{2,1,0:T(4,128)(2,1)S(1)}, u32[]{:S(2)}, u32[]{:S(2)}) collective-permute-start(bf16[4,3,128]{2,1,0:T(4,128)(2,1)S(1)} %get-tuple-element.79), channel_id=1, source_target_pairs={{0,4},{4,8},{8,12},{12,16},{16,20},{20,24},{24,28},{28,32},{32,36}... | collective-permute-start | bytes 9224 | tf_op jit(solution)/shard_map/ppermute | solution.py:30
  121.4 7.3 %collective-permute-start.9 = (bf16[4,3,128]{2,1,0:T(4,128)(2,1)S(1)}, bf16[4,3,128]{2,1,0:T(4,128)(2,1)S(1)}, u32[]{:S(2)}, u32[]{:S(2)}) collective-permute-start(bf16[4,3,128]{2,1,0:T(4,128)(2,1)S(1)} %get-tuple-element.80), channel_id=1, source_target_pairs={{4,0},{8,4},{12,8},{16,12},{20,16},{24,20},{28,24},{32,28},{36,32}... | collective-permute-start | bytes 9224 | tf_op jit(solution)/shard_map/ppermute | solution.py:31
  129.5 12.7 %collective-permute-start.10 = (bf16[4,22,3]{2,1,0:T(8,128)(2,1)}, bf16[4,22,3]{2,1,0:T(8,128)(2,1)}, u32[]{:S(2)}, u32[]{:S(2)}) collective-permute-start(bf16[4,22,3]{2,1,0:T(8,128)(2,1)} %get-tuple-element.77), channel_id=1, source_target_pairs={{0,1},{1,2},{2,3},{4,5},{5,6},{6,7},{8,9},{9,10},{10,11},{12,13},{... | collective-permute-start | bytes 1592 | tf_op jit(solution)/shard_map/ppermute | solution.py:33
  132.6 9.6 %collective-permute-start.11 = (bf16[4,22,3]{2,1,0:T(8,128)(2,1)}, bf16[4,22,3]{2,1,0:T(8,128)(2,1)}, u32[]{:S(2)}, u32[]{:S(2)}) collective-permute-start(bf16[4,22,3]{2,1,0:T(8,128)(2,1)} %get-tuple-element.78), channel_id=1, source_target_pairs={{1,0},{2,1},{3,2},{5,4},{6,5},{7,6},{9,8},{10,9},{11,10},{13,12},{... | collective-permute-start | bytes 1592 | tf_op jit(solution)/shard_map/ppermute | solution.py:34
  139.3 3.9 %copy-start.41 = (pred[134,264]{1,0:T(8,128)(4,1)S(1)}, pred[134,264]{1,0:T(8,128)(4,1)}, u32[]{:S(2)}) copy-start(pred[134,264]{1,0:T(8,128)(4,1)} %iota_compare_fusion.10) | copy-start | bytes 106132
  139.3 3.9 %copy-start.42 = (pred[134,264]{1,0:T(8,128)(4,1)S(1)}, pred[134,264]{1,0:T(8,128)(4,1)}, u32[]{:S(2)}) copy-start(pred[134,264]{1,0:T(8,128)(4,1)} %iota_compare_fusion.9) | copy-start | bytes 106132
  139.3 3.9 %copy-start.43 = (pred[134,264]{1,0:T(8,128)(4,1)S(1)}, pred[134,264]{1,0:T(8,128)(4,1)}, u32[]{:S(2)}) copy-start(pred[134,264]{1,0:T(8,128)(4,1)} %iota_compare_fusion.11) | copy-start | bytes 106132
  139.4 4.3 %copy-start.50 = (s32[40]{0:T(128)S(1)}, s32[40]{0:T(128)}, u32[]{:S(2)}) copy-start(s32[40]{0:T(128)} %get-tuple-element.86) | copy-start | bytes 484
  139.4 4.6 %copy-start.51 = (s32[40]{0:T(128)S(1)}, s32[40]{0:T(128)}, u32[]{:S(2)}) copy-start(s32[40]{0:T(128)} %clamp_subtract_fusion.5) | copy-start | bytes 484
  144.7 3.6 %copy-start.8 = (f32[62,32,1]{2,1,0:T(8,128)S(1)}, f32[62,32,1]{2,1,0:T(8,128)}, u32[]{:S(2)}) copy-start(f32[62,32,1]{2,1,0:T(8,128)} %copy.35) | copy-start | bytes 23812
  144.7 3.6 %copy-start.9 = (f32[62,32,1]{2,1,0:T(8,128)S(1)}, f32[62,32,1]{2,1,0:T(8,128)}, u32[]{:S(2)}) copy-start(f32[62,32,1]{2,1,0:T(8,128)} %copy.37) | copy-start | bytes 23812
  145.4 3.0 %copy-start.6 = (f32[62,31,256]{2,1,0:T(8,128)S(1)}, f32[62,31,256]{2,1,0:T(8,128)}, u32[]{:S(2)}) copy-start(f32[62,31,256]{2,1,0:T(8,128)} %get-tuple-element.47) | copy-start | bytes 5904388
  (34 other events, 63.0 us)

commit v2 on v1

--- a/solution.py
+++ b/solution.py
@@ -2,6 +2,8 @@
 import jax.numpy as jnp
 from jax import lax
 from jax.sharding import PartitionSpec as P
+from jax.experimental import pallas as pl
+from jax.experimental.pallas import tpu as pltpu
 
 AC = 128
 NSUB = 4
@@ -40,11 +42,11 @@
     narrow_count = lax.axis_size("narrow")
     rows = cells.shape[-2]
     cols = cells.shape[-1]
-    above = lax.ppermute(cells[..., rows - 1 :, :], "wide", shift_pairs(wide_count, 1))
-    below = lax.ppermute(cells[..., :1, :], "wide", shift_pairs(wide_count, -1))
-    left = lax.ppermute(cells[..., cols - 1 :], "narrow", shift_pairs(narrow_count, 1))
-    right = lax.ppermute(cells[..., :1], "narrow", shift_pairs(narrow_count, -1))
-    return above, below, left, right
+    above = lax.ppermute(cells[:, rows - 1 :, :], "wide", shift_pairs(wide_count, 1))
+    below = lax.ppermute(cells[:, :1, :], "wide", shift_pairs(wide_count, -1))
+    left = lax.ppermute(cells[:, :, cols - 1], "narrow", shift_pairs(narrow_count, 1))
+    right = lax.ppermute(cells[:, :, 0], "narrow", shift_pairs(narrow_count, -1))
+    return above, below, left[:, :, None], right[:, :, None]
 
 
 def column_ranks(owners, peers):
@@ -72,18 +74,43 @@
     return jnp.concatenate(pieces, axis=0)
 
 
-def physics(operators, columns, flux_map):
-    initial = columns.astype(jnp.float32)
+def physics_kernel(x_ref, op_ref, fm_ref, out_ref):
+    features = x_ref.shape[1]
+    initial = x_ref[...].astype(jnp.float32)
     current = initial
-    for sweep in range(operators.shape[0]):
+    for sweep in range(op_ref.shape[0]):
         mixed = jnp.dot(
-            current.astype(jnp.bfloat16), operators[sweep], preferred_element_type=jnp.float32
+            current.astype(jnp.bfloat16), op_ref[sweep], preferred_element_type=jnp.float32
         )
         current = current + relax_rate * jnp.tanh(mixed)
     final = current.astype(jnp.bfloat16)
-    tendency = (current - initial).astype(jnp.bfloat16)
-    fluxes = jnp.dot(final, flux_map, preferred_element_type=jnp.float32).astype(jnp.bfloat16)
-    return (tendency, fluxes)
+    out_ref[:, :features] = (current - initial).astype(jnp.bfloat16)
+    out_ref[:, features:] = jnp.dot(
+        final, fm_ref[...], preferred_element_type=jnp.float32
+    ).astype(jnp.bfloat16)
+
+
+def physics(operators, columns, flux_map):
+    slots, features = columns.shape
+    nflux = flux_map.shape[1]
+    tile = 512
+    sweeps = operators.shape[0]
+    return pl.pallas_call(
+        physics_kernel,
+        out_shape=jax.ShapeDtypeStruct((slots, features + nflux), jnp.bfloat16),
+        grid=(slots // tile,),
+        in_specs=[
+            pl.BlockSpec((tile, features), lambda i: (i, 0)),
+            pl.BlockSpec((sweeps, features, features), lambda i: (0, 0, 0)),
+            pl.BlockSpec((features, nflux), lambda i: (0, 0)),
+        ],
+        out_specs=pl.BlockSpec((tile, features + nflux), lambda i: (i, 0)),
+        cost_estimate=pl.CostEstimate(
+            flops=2 * slots * features * (sweeps * features + nflux),
+            transcendentals=sweeps * slots * features,
+            bytes_accessed=2 * slots * (2 * features + nflux) + 2 * sweeps * features * features,
+        ),
+    )(columns, operators, flux_map)
 
 
 def selector(count, origin, offset, limit, base, size):
@@ -230,9 +257,8 @@
     initial = atm_state.astype(jnp.bfloat16)
     outgoing = place_columns(initial, slots, total_slots)
     arrived = lax.all_to_all(outgoing, ("wide", "narrow"), split_axis=0, concat_axis=0, tiled=True)
-    tendency, fluxes = physics(regime_ops[0], arrived, flux_map)
     back = lax.all_to_all(
-        jnp.concatenate([tendency, fluxes], axis=1),
+        physics(regime_ops[0], arrived, flux_map),
         ("wide", "narrow"),
         split_axis=0,
         concat_axis=0,

time: 155 us -> 150 us (0.968)
  Pallas kernels: 0 us -> 9.28 us
  local copies, waits for them, and re-layouts: 50 us -> 42.6 us
  matrix products: 14 us -> 9.03 us
  other arithmetic: 19.7 us -> 17.7 us
    pallas_call x0 -> x1, Pallas kernels: none -> 9.28 us  [physics(): pl.pallas_call(physics_kernel, out_shape=jax.ShapeDtypeStruct((slots, fea...]
    dot_general x5 -> x0, matrix products: 4.96 us -> none  [the longest x4 4.69 us: physics(): jnp.dot(current.astype(jnp.bfloat16), operators[sweep], preferred_element...]
    ppermute x2 -> x0, local copies, waits for them, and re-layouts: 4.35 us -> none  [the longest x1 2.51 us: plus_halo(): lax.ppermute(cells[..., :1], 'narrow', shift_pairs(narrow_count, -1))]
    broadcast_in_dim x0 -> x2, local copies, waits for them, and re-layouts: none -> 4.34 us  [plus_halo(): return (above, below, left[:, :, None], right[:, :, None])]
    all_to_all x1 -> x0, local copies, waits for them, and re-layouts: 3.77 us -> none  [per_device(): lax.all_to_all(outgoing, ('wide', 'narrow'), split_axis=0, concat_axis=0,...]
    concatenate x1 -> x0, local copies, waits for them, and re-layouts: 3.69 us -> none  [per_device(): jnp.concatenate([tendency, fluxes], axis=1)]
    unnamed x110 -> x99, local copies, waits for them, and re-layouts: 13.1 us -> 13.1 us
  transfers between devices with their start and end apart: 14 -> 14, of which waited for: 2 -> 2; matrix products, arithmetic and copies ran while one was open for 42% -> 35% of each run, Pallas kernels for 0% -> 6%
where the time goes in v2:
time: 150 us; the launch traced here: 148 us
  starting transfers between devices  57.1 us (38%)
  local copies, waits for them, and re-layouts  42.6 us (28%)
  other arithmetic  17.7 us (12%)
  waiting for transfers between devices  10.4 us (7%)
  Pallas kernels  9.28 us (6%)
  matrix products  9.03 us (6%)
  between operations  1.65 us (1%)
    unnamed x99, local copies, waits for them, and re-layouts  13.1 us
    ppermute x2, starting transfers between devices, with_halo(): lax.ppermute(cells[..., :width, :], 'wide', shift_pairs(wide_count, -1))  11.4 us
    all_to_all x1, starting transfers between devices, per_device(): lax.all_to_all(outgoing, ('wide', 'narrow'), split_axis=0, concat_axis=0,...  10.7 us
    ppermute x2, waiting for transfers between devices, with_halo(): lax.ppermute(cells[..., cols - width:], 'narrow', shift_pairs(narrow_coun...  9.42 us
    pallas_call x1, Pallas kernels, physics(): pl.pallas_call(physics_kernel, out_shape=jax.ShapeDtypeStruct((slots, fea...  9.28 us
    all_to_all x1, starting transfers between devices, per_device(): lax.all_to_all(physics(regime_ops[0], arrived, flux_map), ('wide', 'narro...  8.96 us
    gather x1, local copies, waits for them, and re-layouts, per_device(): returned = jnp.take(back, slots, axis=0, mode='clip')  8.5 us
    dot_general x8, matrix products, place_columns(): lax.dot_general(selector, source, (((1,), (1,)), ((), ())), preferred_ele...  7.84 us
  transfers between devices with their start and end apart: 14, of which 2 were waited for; matrix products, arithmetic and copies ran while one was open for 35% of the time, Pallas kernels for 6%

profile of v2, /device:TPU:34, one launch (start us, length us, event | category | flops | bytes accessed | tf_op | source)
XLA Modules:
  0.0 147.7 jit_solution(2654596083686812071)
XLA Ops:
  11.2 2.4 %copy.23 = bf16[4096,144]{1,0:T(8,128)(2,1)} copy(bf16[4096,144]{0,1:T(8,128)(2,1)S(1)} %fusion.80) | data formatting | bytes 2359296 | tf_op jit(solution)/shard_map/concatenate | solution.py:74
  13.7 10.7 %all-to-all-start = ((bf16[128,32,144]{2,1,0:T(8,128)(2,1)}), bf16[128,32,144]{2,1,0:T(8,128)(2,1)}, u32[]{:S(2)}, u32[]{:S(2)}) async-start(bf16[128,32,144]{2,1,0:T(8,128)(2,1)} %bitcast.144), calls=%async_computation | async-start | bytes 4194304 | tf_op jit(solution)/shard_map/all_to_all | solution.py:259
  25.2 2.0 %collective-permute-start = (f32[12,4,256]{2,1,0:T(4,128)}, f32[12,4,256]{2,1,0:T(4,128)S(1)}, u32[]{:S(2)}, u32[]{:S(2)}) collective-permute-start(f32[12,4,256]{2,1,0:T(4,128)} %get-tuple-element.48), channel_id=1, source_target_pairs={{0,4},{4,8},{8,12},{12,16},{16,20},{20,24},{24,28},{28,32},{32,36}... | collective-permute-start | bytes 147464 | tf_op jit(solution)/shard_map/ppermute | solution.py:32
  27.2 5.6 %collective-permute-start.1 = (f32[12,4,256]{2,1,0:T(4,128)}, f32[12,4,256]{2,1,0:T(4,128)S(1)}, u32[]{:S(2)}, u32[]{:S(2)}) collective-permute-start(f32[12,4,256]{2,1,0:T(4,128)} %get-tuple-element.49), channel_id=1, source_target_pairs={{4,0},{8,4},{12,8},{16,12},{20,16},{24,20},{28,24},{32,28},{36,32}... | collective-permute-start | bytes 147464 | tf_op jit(solution)/shard_map/ppermute | solution.py:33
  32.9 1.3 fusion.128
  34.2 2.4 %copy.34 = f32[62,32,1]{0,1,2:T(8,128)} copy(f32[62,32,1]{2,1,0:T(8,128)} %get-tuple-element.37) | data formatting | bytes 15872
  36.6 2.4 %collective-permute-start.6 = (f32[62,32]{0,1:T(8,128)}, f32[62,32]{0,1:T(8,128)}, u32[]{:S(2)}, u32[]{:S(2)}) collective-permute-start(f32[62,32]{0,1:T(8,128)} %bitcast.162), channel_id=1, source_target_pairs={{1,0},{2,1},{3,2},{5,4},{6,5},{7,6},{9,8},{10,9},{11,10},{13,12},{... | collective-permute-start | bytes 23816 | tf_op jit(solution)/shard_map/ppermute | solution.py:48
  39.0 1.3 copy.35
  40.3 3.4 %collective-permute-start.7 = (f32[62,32]{0,1:T(8,128)}, f32[62,32]{0,1:T(8,128)S(1)}, u32[]{:S(2)}, u32[]{:S(2)}) collective-permute-start(f32[62,32]{0,1:T(8,128)} %bitcast.160), channel_id=1, source_target_pairs={{0,1},{1,2},{2,3},{4,5},{5,6},{6,7},{8,9},{9,10},{10,11},{12,13},{... | collective-permute-start | bytes 23816 | tf_op jit(solution)/shard_map/ppermute | solution.py:47
  44.4 2.1 %collective-permute-start.4 = (f32[62,1,256]{2,1,0:T(1,128)}, f32[62,1,256]{2,1,0:T(1,128)}, u32[]{:S(2)}, u32[]{:S(2)}) collective-permute-start(f32[62,1,256]{2,1,0:T(1,128)} %get-tuple-element.41), channel_id=1, source_target_pairs={{4,0},{8,4},{12,8},{16,12},{20,16},{24,20},{28,24},{32,28},{36,32}... | collective-permute-start | bytes 190472 | tf_op jit(solution)/shard_map/ppermute | solution.py:46
  46.6 1.4 copy.24.fm_ref
  52.0 2.8 %fusion.129 = (f32[62,32,255]{2,1,0:T(8,128)}, f32[62,32,255]{2,1,0:T(8,128)}) fusion(f32[62,32,256]{2,1,0:T(8,128)S(1)} %copy-done), kind=kLoop, calls=%fused_computation.213 | loop fusion | bytes 8094720 | tf_op jit(solution)/shard_map/slice | solution.py:165
  54.8 9.3 %shard_map.129 = bf16[4096,148]{1,0:T(8,128)(2,1)} custom-call(bf16[4096,144]{1,0:T(8,128)(2,1)} %bitcast.6.x_ref, bf16[4,144,144]{2,1,0:T(8,128)(2,1)} %bitcast.154, bf16[144,4]{1,0:T(8,128)(2,1)} %copy.24.fm_ref), custom_call_target="tpu_custom_call" | custom-call | flops 684195840 | bytes 2557952 | tf_op jit(solution)/shard_map/pallas_call | solution.py:98
  64.1 9.0 %all-to-all-start.1 = ((bf16[128,32,148]{2,1,0:T(8,128)(2,1)}), bf16[128,32,148]{2,1,0:T(8,128)(2,1)}, u32[]{:S(2)}, u32[]{:S(2)}) async-start(bf16[128,32,148]{2,1,0:T(8,128)(2,1)} %bitcast.143), calls=%async_computation.1 | async-start | bytes 4194304 | tf_op jit(solution)/shard_map/all_to_all | solution.py:260
  73.1 2.5 %fusion.131 = (f32[62,31,256]{2,1,0:T(8,128)}, f32[62,31,256]{2,1,0:T(8,128)}) fusion(f32[62,32,256]{2,1,0:T(8,128)S(1)} %copy-done), kind=kLoop, calls=%fused_computation.215 | loop fusion | bytes 7872512 | tf_op jit(solution)/shard_map/slice | solution.py:163
  76.3 3.4 %collective-permute-start.2 = (f32[12,40,4]{2,1,0:T(8,128)S(1)}, f32[12,40,4]{2,1,0:T(8,128)S(1)}, u32[]{:S(2)}, u32[]{:S(2)}) collective-permute-start(f32[12,40,4]{2,1,0:T(8,128)S(1)} %get-tuple-element.46), channel_id=1, source_target_pairs={{0,1},{1,2},{2,3},{4,5},{5,6},{6,7},{8,9},{9,10},{10,11},{12,13},{... | collective-permute-start | bytes 23048 | tf_op jit(solution)/shard_map/ppermute | solution.py:35
  79.7 2.5 %collective-permute-start.3 = (f32[12,40,4]{2,1,0:T(8,128)S(1)}, f32[12,40,4]{2,1,0:T(8,128)S(1)}, u32[]{:S(2)}, u32[]{:S(2)}) collective-permute-start(f32[12,40,4]{2,1,0:T(8,128)S(1)} %get-tuple-element.47), channel_id=1, source_target_pairs={{1,0},{2,1},{3,2},{5,4},{6,5},{7,6},{9,8},{10,9},{11,10},{13,12},{... | collective-permute-start | bytes 23048 | tf_op jit(solution)/shard_map/ppermute | solution.py:36
  82.8 2.8 %copy.25 = f32[144,2048]{0,1:T(8,128)} copy(f32[144,2048]{1,0:T(8,128)} %param.12) | data formatting | bytes 2359296 | tf_op args[0]
  85.5 1.9 %collective-permute-start.5 = (f32[62,1,256]{2,1,0:T(1,128)}, f32[62,1,256]{2,1,0:T(1,128)}, u32[]{:S(2)}, u32[]{:S(2)}) collective-permute-start(f32[62,1,256]{2,1,0:T(1,128)} %get-tuple-element.40), channel_id=1, source_target_pairs={{0,4},{4,8},{8,12},{12,16},{16,20},{20,24},{24,28},{28,32},{32,36}... | collective-permute-start | bytes 190472 | tf_op jit(solution)/shard_map/ppermute | solution.py:45
  87.4 2.5 %copy.27 = f32[62,32,1]{2,1,0:T(8,128)} copy(f32[62,32,1]{0,1,2:T(8,128)} %bitcast.20) | data formatting | bytes 15872 | tf_op jit(solution)/shard_map/broadcast_in_dim | solution.py:49
  90.0 1.8 %copy.29 = f32[62,32,1]{2,1,0:T(8,128)} copy(f32[62,32,1]{0,1,2:T(8,128)S(1)} %bitcast.161) | data formatting | bytes 15872 | tf_op jit(solution)/shard_map/broadcast_in_dim | solution.py:49
  91.8 9.4 %collective-permute-done.2 = f32[12,40,4]{2,1,0:T(8,128)S(1)} collective-permute-done((f32[12,40,4]{2,1,0:T(8,128)S(1)}, f32[12,40,4]{2,1,0:T(8,128)S(1)}, u32[]{:S(2)}, u32[]{:S(2)}) %collective-permute-start.2) | collective-permute-done | bytes 7712 | tf_op jit(solution)/shard_map/ppermute | solution.py:35
  103.7 8.5 %gather_fusion = bf16[2048,148]{1,0:T(8,128)(2,1)S(1)} fusion(bf16[4096,148]{1,0:T(8,128)(2,1)} %bitcast.9, s32[2048]{0:T(1024)S(1)} %broadcast_clamp_fusion), kind=kCustom, calls=%fused_computation | custom fusion | bytes 1220608 | tf_op jit(solution)/shard_map/jit(_take)/gather | solution.py:267
  114.5 1.9 %collective-permute-start.8 = (bf16[4,3,128]{2,1,0:T(4,128)(2,1)S(1)}, bf16[4,3,128]{2,1,0:T(4,128)(2,1)S(1)}, u32[]{:S(2)}, u32[]{:S(2)}) collective-permute-start(bf16[4,3,128]{2,1,0:T(4,128)(2,1)S(1)} %get-tuple-element.75), channel_id=1, source_target_pairs={{0,4},{4,8},{8,12},{12,16},{16,20},{20,24},{24,28},{28,32},{32,36}... | collective-permute-start | bytes 9224 | tf_op jit(solution)/shard_map/ppermute | solution.py:32
  116.4 5.8 %collective-permute-start.9 = (bf16[4,3,128]{2,1,0:T(4,128)(2,1)S(1)}, bf16[4,3,128]{2,1,0:T(4,128)(2,1)S(1)}, u32[]{:S(2)}, u32[]{:S(2)}) collective-permute-start(bf16[4,3,128]{2,1,0:T(4,128)(2,1)S(1)} %get-tuple-element.76), channel_id=1, source_target_pairs={{4,0},{8,4},{12,8},{16,12},{20,16},{24,20},{28,24},{32,28},{36,32}... | collective-permute-start | bytes 9224 | tf_op jit(solution)/shard_map/ppermute | solution.py:33
  122.1 1.5 %maximum_bitcast_fusion.2 = (f32[39,264]{1,0:T(8,128)S(1)}, f32[39,264]{1,0:T(8,128)}) fusion(f32[12,40,4]{2,1,0:T(8,128)} %copy-done.10, f32[12,40,4]{2,1,0:T(8,128)} %copy-done.8, f32[12,4,256]{2,1,0:T(4,128)} %copy-done.15, f32[12,32,256]{2,1,0:T(8,128)S(1)} %constant_dynamic-update-slice_fusion, f32[12,4,256]{2,1,0:T(4,128)} %copy-done.13), kind=kLoop, calls=%fused_computation.123 | loop fusion | flops 82368 | bytes 589248 | tf_op jit(solution)/shard_map/slice | solution.py:191
  124.4 3.1 %collective-permute-start.10 = (bf16[4,22,3]{2,1,0:T(8,128)(2,1)}, bf16[4,22,3]{2,1,0:T(8,128)(2,1)}, u32[]{:S(2)}, u32[]{:S(2)}) collective-permute-start(bf16[4,22,3]{2,1,0:T(8,128)(2,1)} %get-tuple-element.73), channel_id=1, source_target_pairs={{0,1},{1,2},{2,3},{4,5},{5,6},{6,7},{8,9},{9,10},{10,11},{12,13},{... | collective-permute-start | bytes 1592 | tf_op jit(solution)/shard_map/ppermute | solution.py:35
  127.5 3.3 %collective-permute-start.11 = (bf16[4,22,3]{2,1,0:T(8,128)(2,1)}, bf16[4,22,3]{2,1,0:T(8,128)(2,1)}, u32[]{:S(2)}, u32[]{:S(2)}) collective-permute-start(bf16[4,22,3]{2,1,0:T(8,128)(2,1)} %get-tuple-element.74), channel_id=1, source_target_pairs={{1,0},{2,1},{3,2},{5,4},{6,5},{7,6},{9,8},{10,9},{11,10},{13,12},{... | collective-permute-start | bytes 1592 | tf_op jit(solution)/shard_map/ppermute | solution.py:36
  130.8 3.2 %bitcast_add_fusion = f32[144,2048]{0,1:T(8,128)} fusion(f32[144,2048]{0,1:T(8,128)} %copy.25, bf16[2048,148]{1,0:T(8,128)(2,1)S(1)} %gather_fusion), kind=kLoop, calls=%fused_computation.17 | loop fusion | flops 589824 | bytes 2949120 | tf_op jit(solution)/shard_map/add | solution.py:270
  134.0 2.7 %copy.33 = f32[144,2048]{1,0:T(8,128)} copy(f32[144,2048]{0,1:T(8,128)} %bitcast_add_fusion) | data formatting | bytes 2359296
  143.7 2.7 %fusion.35 = f32[62,32,256]{2,1,0:T(8,128)S(1)} fusion(f32[62,32,256]{2,1,0:T(8,128)S(1)} %copy-done, f32[62,1,256]{2,1,0:T(1,128)} %collective-permute-done.4, f32[62,31,256]{2,1,0:T(8,128)S(1)} %copy-done.4, f32[62,31,256]{2,1,0:T(8,128)S(1)} %copy-done.3, f32[62,1,256]{2,1,0:T(1,128)} %collective-permute-done.5, f32[62,32,1]{2,1,0:T(8,128)S(1)} %copy-done.6, ...), kind=kLoop, calls=%fused_computation.39 | loop fusion | flops 8634368 | bytes 12320768 | tf_op jit(solution)/shard_map/add | solution.py:173
  146.4 1.3 copy-done.12
  (188 shorter events, 29.3 us)
Async XLA Ops:
  13.7 10.7 %copy-start.17 = (s32[32,256]{1,0:T(8,128)S(1)}, s32[32,256]{1,0:T(8,128)}, u32[]{:S(2)}) copy-start(s32[32,256]{1,0:T(8,128)} %param.18) | copy-start | bytes 98308
  13.7 10.7 %copy-start.40 = (f32[32,256]{1,0:T(8,128)S(1)}, f32[32,256]{1,0:T(8,128)}, u32[]{:S(2)}) copy-start(f32[32,256]{1,0:T(8,128)} %param.20) | copy-start | bytes 98308
  13.7 10.8 %copy-start.36 = (f32[2,32,256]{2,1,0:T(8,128)S(1)}, f32[2,32,256]{2,1,0:T(8,128)}, u32[]{:S(2)}) copy-start(f32[2,32,256]{2,1,0:T(8,128)} %param.21) | copy-start | bytes 196612
  13.7 10.8 %copy-start.30 = (s32[4,32,256]{2,1,0:T(8,128)S(1)}, s32[4,32,256]{2,1,0:T(8,128)}, u32[]{:S(2)}) copy-start(s32[4,32,256]{2,1,0:T(8,128)} %param.16) | copy-start | bytes 393220
  13.7 10.8 %copy-start.31 = (f32[4,32,256]{2,1,0:T(8,128)S(1)}, f32[4,32,256]{2,1,0:T(8,128)}, u32[]{:S(2)}) copy-start(f32[4,32,256]{2,1,0:T(8,128)} %param.17) | copy-start | bytes 393220
  13.7 19.2 %copy-start = (f32[62,32,256]{2,1,0:T(8,128)S(1)}, f32[62,32,256]{2,1,0:T(8,128)}, u32[]{:S(2)}) copy-start(f32[62,32,256]{2,1,0:T(8,128)} %param.19) | copy-start | bytes 6094852
  13.7 41.1 %all-to-all-start = ((bf16[128,32,144]{2,1,0:T(8,128)(2,1)}), bf16[128,32,144]{2,1,0:T(8,128)(2,1)}, u32[]{:S(2)}, u32[]{:S(2)}) async-start(bf16[128,32,144]{2,1,0:T(8,128)(2,1)} %bitcast.144), calls=%async_computation | async-start | bytes 4194304 | tf_op jit(solution)/shard_map/all_to_all | solution.py:259
  25.2 50.9 %collective-permute-start = (f32[12,4,256]{2,1,0:T(4,128)}, f32[12,4,256]{2,1,0:T(4,128)S(1)}, u32[]{:S(2)}, u32[]{:S(2)}) collective-permute-start(f32[12,4,256]{2,1,0:T(4,128)} %get-tuple-element.48), channel_id=1, source_target_pairs={{0,4},{4,8},{8,12},{12,16},{16,20},{20,24},{24,28},{28,32},{32,36}... | collective-permute-start | bytes 147464 | tf_op jit(solution)/shard_map/ppermute | solution.py:32
  27.2 48.9 %collective-permute-start.1 = (f32[12,4,256]{2,1,0:T(4,128)}, f32[12,4,256]{2,1,0:T(4,128)S(1)}, u32[]{:S(2)}, u32[]{:S(2)}) collective-permute-start(f32[12,4,256]{2,1,0:T(4,128)} %get-tuple-element.49), channel_id=1, source_target_pairs={{4,0},{8,4},{12,8},{16,12},{20,16},{24,20},{28,24},{32,28},{36,32}... | collective-permute-start | bytes 147464 | tf_op jit(solution)/shard_map/ppermute | solution.py:33
  36.6 48.9 %collective-permute-start.6 = (f32[62,32]{0,1:T(8,128)}, f32[62,32]{0,1:T(8,128)}, u32[]{:S(2)}, u32[]{:S(2)}) collective-permute-start(f32[62,32]{0,1:T(8,128)} %bitcast.162), channel_id=1, source_target_pairs={{1,0},{2,1},{3,2},{5,4},{6,5},{7,6},{9,8},{10,9},{11,10},{13,12},{... | collective-permute-start | bytes 23816 | tf_op jit(solution)/shard_map/ppermute | solution.py:48
  40.3 49.7 %collective-permute-start.7 = (f32[62,32]{0,1:T(8,128)}, f32[62,32]{0,1:T(8,128)S(1)}, u32[]{:S(2)}, u32[]{:S(2)}) collective-permute-start(f32[62,32]{0,1:T(8,128)} %bitcast.160), channel_id=1, source_target_pairs={{0,1},{1,2},{2,3},{4,5},{5,6},{6,7},{8,9},{9,10},{10,11},{12,13},{... | collective-permute-start | bytes 23816 | tf_op jit(solution)/shard_map/ppermute | solution.py:47
  44.4 98.6 %collective-permute-start.4 = (f32[62,1,256]{2,1,0:T(1,128)}, f32[62,1,256]{2,1,0:T(1,128)}, u32[]{:S(2)}, u32[]{:S(2)}) collective-permute-start(f32[62,1,256]{2,1,0:T(1,128)} %get-tuple-element.41), channel_id=1, source_target_pairs={{4,0},{8,4},{12,8},{16,12},{20,16},{24,20},{28,24},{32,28},{36,32}... | collective-permute-start | bytes 190472 | tf_op jit(solution)/shard_map/ppermute | solution.py:46
  64.1 39.6 %all-to-all-start.1 = ((bf16[128,32,148]{2,1,0:T(8,128)(2,1)}), bf16[128,32,148]{2,1,0:T(8,128)(2,1)}, u32[]{:S(2)}, u32[]{:S(2)}) async-start(bf16[128,32,148]{2,1,0:T(8,128)(2,1)} %bitcast.143), calls=%async_computation.1 | async-start | bytes 4194304 | tf_op jit(solution)/shard_map/all_to_all | solution.py:260
  76.1 26.0 %copy-start.13 = (f32[12,4,256]{2,1,0:T(4,128)}, f32[12,4,256]{2,1,0:T(4,128)S(1)}, u32[]{:S(2)}) copy-start(f32[12,4,256]{2,1,0:T(4,128)S(1)} %collective-permute-done) | copy-start | bytes 147460
  76.1 26.0 %copy-start.15 = (f32[12,4,256]{2,1,0:T(4,128)}, f32[12,4,256]{2,1,0:T(4,128)S(1)}, u32[]{:S(2)}) copy-start(f32[12,4,256]{2,1,0:T(4,128)S(1)} %collective-permute-done.1) | copy-start | bytes 147460
  76.3 24.9 %collective-permute-start.2 = (f32[12,40,4]{2,1,0:T(8,128)S(1)}, f32[12,40,4]{2,1,0:T(8,128)S(1)}, u32[]{:S(2)}, u32[]{:S(2)}) collective-permute-start(f32[12,40,4]{2,1,0:T(8,128)S(1)} %get-tuple-element.46), channel_id=1, source_target_pairs={{0,1},{1,2},{2,3},{4,5},{5,6},{6,7},{8,9},{9,10},{10,11},{12,13},{... | collective-permute-start | bytes 23048 | tf_op jit(solution)/shard_map/ppermute | solution.py:35
  79.7 22.4 %collective-permute-start.3 = (f32[12,40,4]{2,1,0:T(8,128)S(1)}, f32[12,40,4]{2,1,0:T(8,128)S(1)}, u32[]{:S(2)}, u32[]{:S(2)}) collective-permute-start(f32[12,40,4]{2,1,0:T(8,128)S(1)} %get-tuple-element.47), channel_id=1, source_target_pairs={{1,0},{2,1},{3,2},{5,4},{6,5},{7,6},{9,8},{10,9},{11,10},{13,12},{... | collective-permute-start | bytes 23048 | tf_op jit(solution)/shard_map/ppermute | solution.py:36
  85.5 57.5 %collective-permute-start.5 = (f32[62,1,256]{2,1,0:T(1,128)}, f32[62,1,256]{2,1,0:T(1,128)}, u32[]{:S(2)}, u32[]{:S(2)}) collective-permute-start(f32[62,1,256]{2,1,0:T(1,128)} %get-tuple-element.40), channel_id=1, source_target_pairs={{0,4},{4,8},{8,12},{12,16},{16,20},{20,24},{24,28},{28,32},{32,36}... | collective-permute-start | bytes 190472 | tf_op jit(solution)/shard_map/ppermute | solution.py:45
  114.5 9.2 %collective-permute-start.8 = (bf16[4,3,128]{2,1,0:T(4,128)(2,1)S(1)}, bf16[4,3,128]{2,1,0:T(4,128)(2,1)S(1)}, u32[]{:S(2)}, u32[]{:S(2)}) collective-permute-start(bf16[4,3,128]{2,1,0:T(4,128)(2,1)S(1)} %get-tuple-element.75), channel_id=1, source_target_pairs={{0,4},{4,8},{8,12},{12,16},{16,20},{20,24},{24,28},{28,32},{32,36}... | collective-permute-start | bytes 9224 | tf_op jit(solution)/shard_map/ppermute | solution.py:32
  116.4 7.3 %collective-permute-start.9 = (bf16[4,3,128]{2,1,0:T(4,128)(2,1)S(1)}, bf16[4,3,128]{2,1,0:T(4,128)(2,1)S(1)}, u32[]{:S(2)}, u32[]{:S(2)}) collective-permute-start(bf16[4,3,128]{2,1,0:T(4,128)(2,1)S(1)} %get-tuple-element.76), channel_id=1, source_target_pairs={{4,0},{8,4},{12,8},{16,12},{20,16},{24,20},{28,24},{32,28},{36,32}... | collective-permute-start | bytes 9224 | tf_op jit(solution)/shard_map/ppermute | solution.py:33
  124.4 12.4 %collective-permute-start.10 = (bf16[4,22,3]{2,1,0:T(8,128)(2,1)}, bf16[4,22,3]{2,1,0:T(8,128)(2,1)}, u32[]{:S(2)}, u32[]{:S(2)}) collective-permute-start(bf16[4,22,3]{2,1,0:T(8,128)(2,1)} %get-tuple-element.73), channel_id=1, source_target_pairs={{0,1},{1,2},{2,3},{4,5},{5,6},{6,7},{8,9},{9,10},{10,11},{12,13},{... | collective-permute-start | bytes 1592 | tf_op jit(solution)/shard_map/ppermute | solution.py:35
  127.5 9.3 %collective-permute-start.11 = (bf16[4,22,3]{2,1,0:T(8,128)(2,1)}, bf16[4,22,3]{2,1,0:T(8,128)(2,1)}, u32[]{:S(2)}, u32[]{:S(2)}) collective-permute-start(bf16[4,22,3]{2,1,0:T(8,128)(2,1)} %get-tuple-element.74), channel_id=1, source_target_pairs={{1,0},{2,1},{3,2},{5,4},{6,5},{7,6},{9,8},{10,9},{11,10},{13,12},{... | collective-permute-start | bytes 1592 | tf_op jit(solution)/shard_map/ppermute | solution.py:36
  134.0 2.8 %copy-start.42 = (bf16[4,3,128]{2,1,0:T(4,128)(2,1)S(1)}, bf16[4,3,128]{2,1,0:T(4,128)(2,1)}, u32[]{:S(2)}) copy-start(bf16[4,3,128]{2,1,0:T(4,128)(2,1)} %copy-done.41) | copy-start | bytes 9220
  134.0 3.9 %copy-start.37 = (pred[134,264]{1,0:T(8,128)(4,1)S(1)}, pred[134,264]{1,0:T(8,128)(4,1)}, u32[]{:S(2)}) copy-start(pred[134,264]{1,0:T(8,128)(4,1)} %iota_compare_fusion.10) | copy-start | bytes 106132
  134.0 3.9 %copy-start.38 = (pred[134,264]{1,0:T(8,128)(4,1)S(1)}, pred[134,264]{1,0:T(8,128)(4,1)}, u32[]{:S(2)}) copy-start(pred[134,264]{1,0:T(8,128)(4,1)} %iota_compare_fusion.9) | copy-start | bytes 106132
  134.0 3.9 %copy-start.39 = (pred[134,264]{1,0:T(8,128)(4,1)S(1)}, pred[134,264]{1,0:T(8,128)(4,1)}, u32[]{:S(2)}) copy-start(pred[134,264]{1,0:T(8,128)(4,1)} %iota_compare_fusion.11) | copy-start | bytes 106132
  134.0 4.3 %copy-start.44 = (s32[40]{0:T(128)S(1)}, s32[40]{0:T(128)}, u32[]{:S(2)}) copy-start(s32[40]{0:T(128)} %get-tuple-element.80) | copy-start | bytes 484
  134.0 4.6 %copy-start.45 = (s32[40]{0:T(128)S(1)}, s32[40]{0:T(128)}, u32[]{:S(2)}) copy-start(s32[40]{0:T(128)} %clamp_subtract_fusion.5) | copy-start | bytes 484
  139.4 3.6 %copy-start.6 = (f32[62,32,1]{2,1,0:T(8,128)S(1)}, f32[62,32,1]{2,1,0:T(8,128)}, u32[]{:S(2)}) copy-start(f32[62,32,1]{2,1,0:T(8,128)} %copy.27) | copy-start | bytes 23812
  139.4 3.6 %copy-start.7 = (f32[62,32,1]{2,1,0:T(8,128)S(1)}, f32[62,32,1]{2,1,0:T(8,128)}, u32[]{:S(2)}) copy-start(f32[62,32,1]{2,1,0:T(8,128)} %copy.29) | copy-start | bytes 23812
  140.0 3.0 %copy-start.4 = (f32[62,31,256]{2,1,0:T(8,128)S(1)}, f32[62,31,256]{2,1,0:T(8,128)}, u32[]{:S(2)}) copy-start(f32[62,31,256]{2,1,0:T(8,128)} %get-tuple-element.43) | copy-start | bytes 5904388
  140.8 2.9 %copy-start.2 = (f32[62,32,255]{2,1,0:T(8,128)S(1)}, f32[62,32,255]{2,1,0:T(8,128)}, u32[]{:S(2)}) copy-start(f32[62,32,255]{2,1,0:T(8,128)} %get-tuple-element.39) | copy-start | bytes 6071044
  (28 other events, 51.0 us)

commit v3 on v2

--- a/solution.py
+++ b/solution.py
@@ -37,6 +37,38 @@
     return jnp.concatenate([left, cells, right], axis=-1)
 
 
+def with_halo_once(cells, width):
+    wide_count = lax.axis_size("wide")
+    narrow_count = lax.axis_size("narrow")
+    both = ("wide", "narrow")
+    rows = cells.shape[-2]
+    cols = cells.shape[-1]
+    h = width
+
+    def diagonal(dw, dn):
+        return [
+            (w * narrow_count + n, (w + dw) * narrow_count + n + dn)
+            for w in range(wide_count)
+            for n in range(narrow_count)
+            if 0 <= w + dw < wide_count and 0 <= n + dn < narrow_count
+        ]
+
+    first_rows = cells[..., :h, :]
+    last_rows = cells[..., rows - h :, :]
+    above = lax.ppermute(last_rows, "wide", shift_pairs(wide_count, 1))
+    below = lax.ppermute(first_rows, "wide", shift_pairs(wide_count, -1))
+    left = lax.ppermute(cells[..., cols - h :], "narrow", shift_pairs(narrow_count, 1))
+    right = lax.ppermute(cells[..., :h], "narrow", shift_pairs(narrow_count, -1))
+    above_left = lax.ppermute(last_rows[..., cols - h :], both, diagonal(1, 1))
+    above_right = lax.ppermute(last_rows[..., :h], both, diagonal(1, -1))
+    below_left = lax.ppermute(first_rows[..., cols - h :], both, diagonal(-1, 1))
+    below_right = lax.ppermute(first_rows[..., :h], both, diagonal(-1, -1))
+    top = jnp.concatenate([above_left, above, above_right], axis=-1)
+    middle = jnp.concatenate([left, cells, right], axis=-1)
+    bottom = jnp.concatenate([below_left, below, below_right], axis=-1)
+    return jnp.concatenate([top, middle, bottom], axis=-2)
+
+
 def plus_halo(cells):
     wide_count = lax.axis_size("wide")
     narrow_count = lax.axis_size("narrow")
@@ -93,7 +125,7 @@
 def physics(operators, columns, flux_map):
     slots, features = columns.shape
     nflux = flux_map.shape[1]
-    tile = 512
+    tile = min(slots, 2048)
     sweeps = operators.shape[0]
     return pl.pallas_call(
         physics_kernel,
@@ -111,6 +143,44 @@
             bytes_accessed=2 * slots * (2 * features + nflux) + 2 * sweeps * features * features,
         ),
     )(columns, operators, flux_map)
+
+
+def unpack_kernel(got_ref, atm_ref, eye_ref, atm_out_ref, flux_out_ref):
+    features = atm_ref.shape[0]
+    turned = lax.dot_general(
+        eye_ref[...], got_ref[...], (((1,), (1,)), ((), ())), preferred_element_type=jnp.float32
+    )
+    atm_out_ref[...] = atm_ref[...] + turned[:features]
+    flux_out_ref[...] = turned[features:].astype(flux_out_ref.dtype)
+
+
+def unpack(got, atm_state):
+    columns, width = got.shape
+    features = atm_state.shape[0]
+    tile = min(columns, 512)
+    eye = jnp.eye(width, dtype=jnp.bfloat16)
+    return pl.pallas_call(
+        unpack_kernel,
+        out_shape=(
+            jax.ShapeDtypeStruct((features, columns), jnp.float32),
+            jax.ShapeDtypeStruct((width - features, columns), jnp.bfloat16),
+        ),
+        grid=(columns // tile,),
+        in_specs=[
+            pl.BlockSpec((tile, width), lambda i: (i, 0)),
+            pl.BlockSpec((features, tile), lambda i: (0, i)),
+            pl.BlockSpec((width, width), lambda i: (0, 0)),
+        ],
+        out_specs=(
+            pl.BlockSpec((features, tile), lambda i: (0, i)),
+            pl.BlockSpec((width - features, tile), lambda i: (0, i)),
+        ),
+        cost_estimate=pl.CostEstimate(
+            flops=2 * columns * width * width,
+            transcendentals=0,
+            bytes_accessed=2 * columns * width + 8 * columns * features + 2 * columns * width,
+        ),
+    )(got, atm_state, eye)
 
 
 def selector(count, origin, offset, limit, base, size):
@@ -265,12 +335,10 @@
         tiled=True,
     )
     returned = jnp.take(back, slots, axis=0, mode="clip")
-    tend_cols = returned[:, :features].T.astype(jnp.float32)
-    flux_cols = returned[:, features:].T
-    atm_new = atm_state + tend_cols
+    atm_new, flux_cols = unpack(returned, atm_state)
 
     flux_block = flux_cols.astype(jnp.bfloat16).reshape(nflux, block_rows, AC)
-    flux_ext = with_halo(flux_block, ATM_HALO)
+    flux_ext = with_halo_once(flux_block, ATM_HALO)
     ocean_flux = remap(
         flux_ext,
         src_ext,

time: 150 us -> 183 us (1.22)
  starting transfers between devices: 57.1 us -> 70.9 us
  waiting for transfers between devices: 10.4 us -> 21.1 us
  matrix products: 9.03 us -> 13.5 us
  other arithmetic: 17.7 us -> 21.6 us
    ppermute x0 -> x8, starting transfers between devices: none -> 27.6 us  [the longest x1 6.65 us: with_halo_once(): below_right = lax.ppermute(first_rows[..., :h], both, diagonal(-1, -1))]
    all_to_all x1, waiting for transfers between devices: 0.01 us -> 6.75 us  [per_device(): lax.all_to_all(outgoing, ('wide', 'narrow'), split_axis=0, concat_axis=0,...]
    ppermute x2 -> x1, starting transfers between devices: 11.4 us -> 5.75 us  [with_halo(): lax.ppermute(cells[..., :width, :], 'wide', shift_pairs(wide_count, -1))]
    pallas_call x0 -> x1, Pallas kernels: none -> 4.12 us  [unpack(): pl.pallas_call(unpack_kernel, out_shape=(jax.ShapeDtypeStruct((features,...]
    ppermute x2 -> x1, waiting for transfers between devices: 9.42 us -> 13.4 us  [with_halo(): lax.ppermute(cells[..., cols - width:], 'narrow', shift_pairs(narrow_coun...]
    ppermute x1, starting transfers between devices: 2.09 us -> 5.75 us  [plus_halo(): below = lax.ppermute(cells[:, :1, :], 'wide', shift_pairs(wide_count, -1))]
    unnamed x99 -> x62, local copies, waits for them, and re-layouts: 13.1 us -> 9.77 us
    add x1 -> x0, other arithmetic: 3.15 us -> none  [per_device(): atm_new = atm_state + tend_cols]
  transfers between devices with their start and end apart: 14 -> 18, of which waited for: 2 -> 3; matrix products, arithmetic and copies ran while one was open for 35% -> 31% of each run, Pallas kernels for 6% -> 3%
where the time goes in v3:
time: 183 us; the launch traced here: 182 us
  starting transfers between devices  70.9 us (39%)
  local copies, waits for them, and re-layouts  42.7 us (23%)
  other arithmetic  21.6 us (12%)
  waiting for transfers between devices  21.1 us (12%)
  matrix products  13.5 us (7%)
  Pallas kernels  10.3 us (6%)
    ppermute x1, waiting for transfers between devices, with_halo(): lax.ppermute(cells[..., cols - width:], 'narrow', shift_pairs(narrow_coun...  13.4 us
    gather x1, local copies, waits for them, and re-layouts, per_device(): returned = jnp.take(back, slots, axis=0, mode='clip')  10.3 us
    unnamed x62, local copies, waits for them, and re-layouts  9.77 us
    all_to_all x1, starting transfers between devices, per_device(): lax.all_to_all(outgoing, ('wide', 'narrow'), split_axis=0, concat_axis=0,...  8.56 us
    dot_general x8, matrix products, place_columns(): lax.dot_general(selector, source, (((1,), (1,)), ((), ())), preferred_ele...  7.84 us
    all_to_all x1, starting transfers between devices, per_device(): lax.all_to_all(physics(regime_ops[0], arrived, flux_map), ('wide', 'narro...  6.86 us
    all_to_all x1, waiting for transfers between devices, per_device(): lax.all_to_all(outgoing, ('wide', 'narrow'), split_axis=0, concat_axis=0,...  6.75 us
    ppermute x1, starting transfers between devices, with_halo_once(): below_right = lax.ppermute(first_rows[..., :h], both, diagonal(-1, -1))  6.65 us
  transfers between devices with their start and end apart: 18, of which 3 were waited for; matrix products, arithmetic and copies ran while one was open for 31% of the time, Pallas kernels for 3%

profile of v3, /device:TPU:34, one launch (start us, length us, event | category | flops | bytes accessed | tf_op | source)
XLA Modules:
  0.0 181.5 jit_solution(11672594113783555292)
XLA Ops:
  5.5 1.9 %collective-permute-start = (f32[12,4,256]{2,1,0:T(4,128)}, f32[12,4,256]{2,1,0:T(4,128)S(1)}, u32[]{:S(2)}, u32[]{:S(2)}) collective-permute-start(f32[12,4,256]{2,1,0:T(4,128)} %get-tuple-element.44), channel_id=1, source_target_pairs={{0,4},{4,8},{8,12},{12,16},{16,20},{20,24},{24,28},{28,32},{32,36}... | collective-permute-start | bytes 147464 | tf_op jit(solution)/shard_map/ppermute | solution.py:32
  7.4 5.8 %collective-permute-start.1 = (f32[12,4,256]{2,1,0:T(4,128)}, f32[12,4,256]{2,1,0:T(4,128)S(1)}, u32[]{:S(2)}, u32[]{:S(2)}) collective-permute-start(f32[12,4,256]{2,1,0:T(4,128)} %get-tuple-element.45), channel_id=1, source_target_pairs={{4,0},{8,4},{12,8},{16,12},{20,16},{24,20},{28,24},{32,28},{36,32}... | collective-permute-start | bytes 147464 | tf_op jit(solution)/shard_map/ppermute | solution.py:33
  25.6 2.4 %copy.21 = bf16[4096,144]{1,0:T(8,128)(2,1)} copy(bf16[4096,144]{0,1:T(8,128)(2,1)S(1)} %fusion.80) | data formatting | bytes 2359296 | tf_op jit(solution)/shard_map/concatenate | solution.py:106
  28.1 8.6 %all-to-all-start = ((bf16[128,32,144]{2,1,0:T(8,128)(2,1)}), bf16[128,32,144]{2,1,0:T(8,128)(2,1)}, u32[]{:S(2)}, u32[]{:S(2)}) async-start(bf16[128,32,144]{2,1,0:T(8,128)(2,1)} %bitcast.143), calls=%async_computation | async-start | bytes 4194304 | tf_op jit(solution)/shard_map/all_to_all | solution.py:329
  38.0 2.4 %copy.27 = f32[62,32,1]{0,1,2:T(8,128)} copy(f32[62,32,1]{2,1,0:T(8,128)} %get-tuple-element.33) | data formatting | bytes 15872
  40.4 2.4 %collective-permute-start.6 = (f32[62,32]{0,1:T(8,128)}, f32[62,32]{0,1:T(8,128)}, u32[]{:S(2)}, u32[]{:S(2)}) collective-permute-start(f32[62,32]{0,1:T(8,128)} %bitcast.162), channel_id=1, source_target_pairs={{1,0},{2,1},{3,2},{5,4},{6,5},{7,6},{9,8},{10,9},{11,10},{13,12},{... | collective-permute-start | bytes 23816 | tf_op jit(solution)/shard_map/ppermute | solution.py:80
  44.1 3.6 %collective-permute-start.7 = (f32[62,32]{0,1:T(8,128)}, f32[62,32]{0,1:T(8,128)S(1)}, u32[]{:S(2)}, u32[]{:S(2)}) collective-permute-start(f32[62,32]{0,1:T(8,128)} %bitcast.163), channel_id=1, source_target_pairs={{0,1},{1,2},{2,3},{4,5},{5,6},{6,7},{8,9},{9,10},{10,11},{12,13},{... | collective-permute-start | bytes 23816 | tf_op jit(solution)/shard_map/ppermute | solution.py:79
  53.2 2.8 %fusion.130 = (f32[62,32,255]{2,1,0:T(8,128)}, f32[62,32,255]{2,1,0:T(8,128)}) fusion(f32[62,32,256]{2,1,0:T(8,128)S(1)} %copy-done), kind=kLoop, calls=%fused_computation.214 | loop fusion | bytes 8094720 | tf_op jit(solution)/shard_map/slice | solution.py:235
  56.0 2.5 %fusion.132 = (f32[62,31,256]{2,1,0:T(8,128)}, f32[62,31,256]{2,1,0:T(8,128)}) fusion(f32[62,32,256]{2,1,0:T(8,128)S(1)} %copy-done), kind=kLoop, calls=%fused_computation.216 | loop fusion | bytes 7872512 | tf_op jit(solution)/shard_map/slice | solution.py:233
  58.4 6.8 %all-to-all-done = bf16[128,32,144]{2,1,0:T(8,128)(2,1)} async-done(((bf16[128,32,144]{2,1,0:T(8,128)(2,1)}), bf16[128,32,144]{2,1,0:T(8,128)(2,1)}, u32[]{:S(2)}, u32[]{:S(2)}) %all-to-all-start) | async-done | bytes 1179680 | tf_op jit(solution)/shard_map/all_to_all | solution.py:329
  65.2 6.1 %shard_map.129 = bf16[4096,148]{1,0:T(8,128)(2,1)} custom-call(bf16[4096,144]{1,0:T(8,128)(2,1)} %bitcast.6.x_ref, bf16[4,144,144]{2,1,0:T(8,128)(2,1)} %bitcast.156, bf16[144,4]{1,0:T(8,128)(2,1)} %copy.22.fm_ref), custom_call_target="tpu_custom_call" | custom-call | flops 684195840 | bytes 2557952 | tf_op jit(solution)/shard_map/pallas_call | solution.py:130
  71.3 6.9 %all-to-all-start.1 = ((bf16[128,32,148]{2,1,0:T(8,128)(2,1)}), bf16[128,32,148]{2,1,0:T(8,128)(2,1)}, u32[]{:S(2)}, u32[]{:S(2)}) async-start(bf16[128,32,148]{2,1,0:T(8,128)(2,1)} %bitcast.142), calls=%async_computation.1 | async-start | bytes 4194304 | tf_op jit(solution)/shard_map/all_to_all | solution.py:330
  81.1 3.4 %collective-permute-start.2 = (f32[12,40,4]{2,1,0:T(8,128)}, f32[12,40,4]{2,1,0:T(8,128)}, u32[]{:S(2)}, u32[]{:S(2)}) collective-permute-start(f32[12,40,4]{2,1,0:T(8,128)} %get-tuple-element.42), channel_id=1, source_target_pairs={{0,1},{1,2},{2,3},{4,5},{5,6},{6,7},{8,9},{9,10},{10,11},{12,13},{... | collective-permute-start | bytes 23048 | tf_op jit(solution)/shard_map/ppermute | solution.py:35
  84.5 3.1 %collective-permute-start.3 = (f32[12,40,4]{2,1,0:T(8,128)}, f32[12,40,4]{2,1,0:T(8,128)}, u32[]{:S(2)}, u32[]{:S(2)}) collective-permute-start(f32[12,40,4]{2,1,0:T(8,128)} %get-tuple-element.43), channel_id=1, source_target_pairs={{1,0},{2,1},{3,2},{5,4},{6,5},{7,6},{9,8},{10,9},{11,10},{13,12},{... | collective-permute-start | bytes 23048 | tf_op jit(solution)/shard_map/ppermute | solution.py:36
  88.9 1.7 copy.26
  90.6 2.5 %copy.24 = f32[62,32,1]{2,1,0:T(8,128)} copy(f32[62,32,1]{0,1,2:T(8,128)} %bitcast.19) | data formatting | bytes 15872 | tf_op jit(solution)/shard_map/broadcast_in_dim | solution.py:81
  93.1 13.4 %collective-permute-done.2 = f32[12,40,4]{2,1,0:T(8,128)} collective-permute-done((f32[12,40,4]{2,1,0:T(8,128)}, f32[12,40,4]{2,1,0:T(8,128)}, u32[]{:S(2)}, u32[]{:S(2)}) %collective-permute-start.2) | collective-permute-done | bytes 7712 | tf_op jit(solution)/shard_map/ppermute | solution.py:35
  110.0 10.3 %gather_fusion = bf16[2048,148]{1,0:T(8,128)(2,1)} fusion(bf16[4096,148]{1,0:T(8,128)(2,1)} %bitcast.9, s32[2048]{0:T(1024)S(1)} %broadcast_clamp_fusion), kind=kCustom, calls=%fused_computation | custom fusion | bytes 1220608 | tf_op jit(solution)/shard_map/jit(_take)/gather | solution.py:337
  120.3 4.1 %shard_map.130 = (f32[144,2048]{1,0:T(8,128)}, bf16[4,2048]{1,0:T(4,128)(2,1)}) custom-call(bf16[2048,148]{1,0:T(8,128)(2,1)} %gather_fusion, f32[144,2048]{1,0:T(8,128)} %atm_ref.1, bf16[148,148]{1,0:T(8,128)(2,1)} %fusion.101.eye_ref), custom_call_target="tpu_custom_call" | custom-call | flops 89718784 | bytes 3571712 | tf_op jit(solution)/shard_map/pallas_call | solution.py:162
  125.3 1.9 %collective-permute-start.9 = (bf16[4,3,128]{2,1,0:T(4,128)(2,1)S(1)}, bf16[4,3,128]{2,1,0:T(4,128)(2,1)S(1)}, u32[]{:S(2)}, u32[]{:S(2)}) collective-permute-start(bf16[4,3,128]{2,1,0:T(4,128)(2,1)S(1)} %get-tuple-element.73), channel_id=1, source_target_pairs={{0,4},{4,8},{8,12},{12,16},{16,20},{20,24},{24,28},{28,32},{32,36}... | collective-permute-start | bytes 9224 | tf_op jit(solution)/shard_map/ppermute | solution.py:58
  127.3 5.8 %collective-permute-start.14 = (bf16[4,3,128]{2,1,0:T(4,128)(2,1)S(1)}, bf16[4,3,128]{2,1,0:T(4,128)(2,1)S(1)}, u32[]{:S(2)}, u32[]{:S(2)}) collective-permute-start(bf16[4,3,128]{2,1,0:T(4,128)(2,1)S(1)} %get-tuple-element.74), channel_id=1, source_target_pairs={{4,0},{8,4},{12,8},{16,12},{20,16},{24,20},{28,24},{32,28},{36,32}... | collective-permute-start | bytes 9224 | tf_op jit(solution)/shard_map/ppermute | solution.py:59
  133.0 1.9 %collective-permute-start.8 = (bf16[4,3,3]{2,1,0:T(4,128)(2,1)S(1)}, bf16[4,3,3]{2,1,0:T(4,128)(2,1)S(1)}, u32[]{:S(2)}, u32[]{:S(2)}) collective-permute-start(bf16[4,3,3]{2,1,0:T(4,128)(2,1)S(1)} %get-tuple-element.69), channel_id=1, source_target_pairs={{0,5},{1,6},{2,7},{4,9},{5,10},{6,11},{8,13},{9,14},{10,15},{12,17... | collective-permute-start | bytes 224 | tf_op jit(solution)/shard_map/ppermute | solution.py:62
  134.9 6.6 %collective-permute-start.15 = (bf16[4,3,3]{2,1,0:T(4,128)(2,1)S(1)}, bf16[4,3,3]{2,1,0:T(4,128)(2,1)S(1)}, u32[]{:S(2)}, u32[]{:S(2)}) collective-permute-start(bf16[4,3,3]{2,1,0:T(4,128)(2,1)S(1)} %get-tuple-element.70), channel_id=1, source_target_pairs={{5,0},{6,1},{7,2},{9,4},{10,5},{11,6},{13,8},{14,9},{15,10},{17,12... | collective-permute-start | bytes 224 | tf_op jit(solution)/shard_map/ppermute | solution.py:65
  141.6 1.9 %collective-permute-start.13 = (bf16[4,3,3]{2,1,0:T(4,128)(2,1)S(1)}, bf16[4,3,3]{2,1,0:T(4,128)(2,1)S(1)}, u32[]{:S(2)}, u32[]{:S(2)}) collective-permute-start(bf16[4,3,3]{2,1,0:T(4,128)(2,1)S(1)} %get-tuple-element.71), channel_id=1, source_target_pairs={{4,1},{5,2},{6,3},{8,5},{9,6},{10,7},{12,9},{13,10},{14,11},{16,13... | collective-permute-start | bytes 224 | tf_op jit(solution)/shard_map/ppermute | solution.py:64
  143.5 3.6 %collective-permute-start.10 = (bf16[4,3,3]{2,1,0:T(4,128)(2,1)S(1)}, bf16[4,3,3]{2,1,0:T(4,128)(2,1)S(1)}, u32[]{:S(2)}, u32[]{:S(2)}) collective-permute-start(bf16[4,3,3]{2,1,0:T(4,128)(2,1)S(1)} %get-tuple-element.72), channel_id=1, source_target_pairs={{1,4},{2,5},{3,6},{5,8},{6,9},{7,10},{9,12},{10,13},{11,14},{13,16... | collective-permute-start | bytes 224 | tf_op jit(solution)/shard_map/ppermute | solution.py:63
  147.2 3.1 %collective-permute-start.11 = (bf16[4,16,3]{2,1,0:T(8,128)(2,1)S(1)}, bf16[4,16,3]{2,1,0:T(8,128)(2,1)S(1)}, u32[]{:S(2)}, u32[]{:S(2)}) collective-permute-start(bf16[4,16,3]{2,1,0:T(8,128)(2,1)S(1)} %get-tuple-element.75), channel_id=1, source_target_pairs={{0,1},{1,2},{2,3},{4,5},{5,6},{6,7},{8,9},{9,10},{10,11},{12,13},{... | collective-permute-start | bytes 1160 | tf_op jit(solution)/shard_map/ppermute | solution.py:60
  150.3 2.7 %collective-permute-start.12 = (bf16[4,16,3]{2,1,0:T(8,128)(2,1)S(1)}, bf16[4,16,3]{2,1,0:T(8,128)(2,1)S(1)}, u32[]{:S(2)}, u32[]{:S(2)}) collective-permute-start(bf16[4,16,3]{2,1,0:T(8,128)(2,1)S(1)} %get-tuple-element.76), channel_id=1, source_target_pairs={{1,0},{2,1},{3,2},{5,4},{6,5},{7,6},{9,8},{10,9},{11,10},{13,12},{... | collective-permute-start | bytes 1160 | tf_op jit(solution)/shard_map/ppermute | solution.py:61
  154.6 1.9 %collective-permute-start.5 = (f32[62,1,256]{2,1,0:T(1,128)}, f32[62,1,256]{2,1,0:T(1,128)}, u32[]{:S(2)}, u32[]{:S(2)}) collective-permute-start(f32[62,1,256]{2,1,0:T(1,128)} %get-tuple-element.36), channel_id=1, source_target_pairs={{0,4},{4,8},{8,12},{12,16},{16,20},{20,24},{24,28},{28,32},{32,36}... | collective-permute-start | bytes 190472 | tf_op jit(solution)/shard_map/ppermute | solution.py:77
  156.5 5.8 %collective-permute-start.4 = (f32[62,1,256]{2,1,0:T(1,128)}, f32[62,1,256]{2,1,0:T(1,128)}, u32[]{:S(2)}, u32[]{:S(2)}) collective-permute-start(f32[62,1,256]{2,1,0:T(1,128)} %get-tuple-element.37), channel_id=1, source_target_pairs={{4,0},{8,4},{12,8},{16,12},{20,16},{24,20},{28,24},{32,28},{36,32}... | collective-permute-start | bytes 190472 | tf_op jit(solution)/shard_map/ppermute | solution.py:78
  164.5 1.9 %convolution_convert_fusion = bf16[88,792]{1,0:T(8,128)(2,1)} fusion(bf16[88,134]{1,0:T(8,128)(2,1)} %reshape.208, pred[134,264]{1,0:T(8,128)(4,1)} %iota_compare_fusion.9, pred[134,264]{1,0:T(8,128)(4,1)} %iota_compare_fusion.10, pred[134,264]{1,0:T(8,128)(4,1)} %iota_compare_fusion.11), kind=kOutput, calls=%fused_computation.48 | convolution fusion | flops 18960480 | bytes 269104 | tf_op jit(solution)/shard_map/dot_general | solution.py:211
  166.4 1.6 reshape.209
  177.5 2.7 %fusion.35 = f32[62,32,256]{2,1,0:T(8,128)S(1)} fusion(f32[62,32,256]{2,1,0:T(8,128)S(1)} %copy-done, f32[62,1,256]{2,1,0:T(1,128)} %collective-permute-done.4, f32[62,31,256]{2,1,0:T(8,128)S(1)} %copy-done.4, f32[62,31,256]{2,1,0:T(8,128)S(1)} %copy-done.3, f32[62,1,256]{2,1,0:T(1,128)} %collective-permute-done.5, f32[62,32,1]{2,1,0:T(8,128)S(1)} %copy-done.5, ...), kind=kLoop, calls=%fused_computation.38 | loop fusion | flops 8634368 | bytes 12320768 | tf_op jit(solution)/shard_map/add | solution.py:243
  (158 shorter events, 48.0 us)
Async XLA Ops:
  5.5 74.6 %collective-permute-start = (f32[12,4,256]{2,1,0:T(4,128)}, f32[12,4,256]{2,1,0:T(4,128)S(1)}, u32[]{:S(2)}, u32[]{:S(2)}) collective-permute-start(f32[12,4,256]{2,1,0:T(4,128)} %get-tuple-element.44), channel_id=1, source_target_pairs={{0,4},{4,8},{8,12},{12,16},{16,20},{20,24},{24,28},{28,32},{32,36}... | collective-permute-start | bytes 147464 | tf_op jit(solution)/shard_map/ppermute | solution.py:32
  7.4 72.7 %collective-permute-start.1 = (f32[12,4,256]{2,1,0:T(4,128)}, f32[12,4,256]{2,1,0:T(4,128)S(1)}, u32[]{:S(2)}, u32[]{:S(2)}) collective-permute-start(f32[12,4,256]{2,1,0:T(4,128)} %get-tuple-element.45), channel_id=1, source_target_pairs={{4,0},{8,4},{12,8},{16,12},{20,16},{24,20},{28,24},{32,28},{36,32}... | collective-permute-start | bytes 147464 | tf_op jit(solution)/shard_map/ppermute | solution.py:33
  28.1 8.6 %copy-start = (f32[62,32,256]{2,1,0:T(8,128)S(1)}, f32[62,32,256]{2,1,0:T(8,128)}, u32[]{:S(2)}) copy-start(f32[62,32,256]{2,1,0:T(8,128)} %param.19) | copy-start | bytes 6094852
  28.1 37.1 %all-to-all-start = ((bf16[128,32,144]{2,1,0:T(8,128)(2,1)}), bf16[128,32,144]{2,1,0:T(8,128)(2,1)}, u32[]{:S(2)}, u32[]{:S(2)}) async-start(bf16[128,32,144]{2,1,0:T(8,128)(2,1)} %bitcast.143), calls=%async_computation | async-start | bytes 4194304 | tf_op jit(solution)/shard_map/all_to_all | solution.py:329
  38.0 10.5 %copy-start.27 = (bf16[144,4]{0,1:T(4,128)(2,1)S(1)}, bf16[144,4]{0,1:T(4,128)(2,1)}, u32[]{:S(2)}) copy-start(bf16[144,4]{0,1:T(4,128)(2,1)} %param.15) | copy-start | bytes 3460
  40.4 50.2 %collective-permute-start.6 = (f32[62,32]{0,1:T(8,128)}, f32[62,32]{0,1:T(8,128)}, u32[]{:S(2)}, u32[]{:S(2)}) collective-permute-start(f32[62,32]{0,1:T(8,128)} %bitcast.162), channel_id=1, source_target_pairs={{1,0},{2,1},{3,2},{5,4},{6,5},{7,6},{9,8},{10,9},{11,10},{13,12},{... | collective-permute-start | bytes 23816 | tf_op jit(solution)/shard_map/ppermute | solution.py:80
  44.1 44.2 %collective-permute-start.7 = (f32[62,32]{0,1:T(8,128)}, f32[62,32]{0,1:T(8,128)S(1)}, u32[]{:S(2)}, u32[]{:S(2)}) collective-permute-start(f32[62,32]{0,1:T(8,128)} %bitcast.163), channel_id=1, source_target_pairs={{0,1},{1,2},{2,3},{4,5},{5,6},{6,7},{8,9},{9,10},{10,11},{12,13},{... | collective-permute-start | bytes 23816 | tf_op jit(solution)/shard_map/ppermute | solution.py:79
  71.3 38.7 %all-to-all-start.1 = ((bf16[128,32,148]{2,1,0:T(8,128)(2,1)}), bf16[128,32,148]{2,1,0:T(8,128)(2,1)}, u32[]{:S(2)}, u32[]{:S(2)}) async-start(bf16[128,32,148]{2,1,0:T(8,128)(2,1)} %bitcast.142), calls=%async_computation.1 | async-start | bytes 4194304 | tf_op jit(solution)/shard_map/all_to_all | solution.py:330
  80.1 28.7 %copy-start.7 = (f32[12,4,256]{2,1,0:T(4,128)}, f32[12,4,256]{2,1,0:T(4,128)S(1)}, u32[]{:S(2)}) copy-start(f32[12,4,256]{2,1,0:T(4,128)S(1)} %collective-permute-done.1) | copy-start | bytes 147460
  81.1 25.3 %collective-permute-start.2 = (f32[12,40,4]{2,1,0:T(8,128)}, f32[12,40,4]{2,1,0:T(8,128)}, u32[]{:S(2)}, u32[]{:S(2)}) collective-permute-start(f32[12,40,4]{2,1,0:T(8,128)} %get-tuple-element.42), channel_id=1, source_target_pairs={{0,1},{1,2},{2,3},{4,5},{5,6},{6,7},{8,9},{9,10},{10,11},{12,13},{... | collective-permute-start | bytes 23048 | tf_op jit(solution)/shard_map/ppermute | solution.py:35
  84.5 22.9 %collective-permute-start.3 = (f32[12,40,4]{2,1,0:T(8,128)}, f32[12,40,4]{2,1,0:T(8,128)}, u32[]{:S(2)}, u32[]{:S(2)}) collective-permute-start(f32[12,40,4]{2,1,0:T(8,128)} %get-tuple-element.43), channel_id=1, source_target_pairs={{1,0},{2,1},{3,2},{5,4},{6,5},{7,6},{9,8},{10,9},{11,10},{13,12},{... | collective-permute-start | bytes 23048 | tf_op jit(solution)/shard_map/ppermute | solution.py:36
  125.3 37.0 %collective-permute-start.9 = (bf16[4,3,128]{2,1,0:T(4,128)(2,1)S(1)}, bf16[4,3,128]{2,1,0:T(4,128)(2,1)S(1)}, u32[]{:S(2)}, u32[]{:S(2)}) collective-permute-start(bf16[4,3,128]{2,1,0:T(4,128)(2,1)S(1)} %get-tuple-element.73), channel_id=1, source_target_pairs={{0,4},{4,8},{8,12},{12,16},{16,20},{20,24},{24,28},{28,32},{32,36}... | collective-permute-start | bytes 9224 | tf_op jit(solution)/shard_map/ppermute | solution.py:58
  127.3 35.1 %collective-permute-start.14 = (bf16[4,3,128]{2,1,0:T(4,128)(2,1)S(1)}, bf16[4,3,128]{2,1,0:T(4,128)(2,1)S(1)}, u32[]{:S(2)}, u32[]{:S(2)}) collective-permute-start(bf16[4,3,128]{2,1,0:T(4,128)(2,1)S(1)} %get-tuple-element.74), channel_id=1, source_target_pairs={{4,0},{8,4},{12,8},{16,12},{20,16},{24,20},{28,24},{32,28},{36,32}... | collective-permute-start | bytes 9224 | tf_op jit(solution)/shard_map/ppermute | solution.py:59
  133.0 10.5 %collective-permute-start.8 = (bf16[4,3,3]{2,1,0:T(4,128)(2,1)S(1)}, bf16[4,3,3]{2,1,0:T(4,128)(2,1)S(1)}, u32[]{:S(2)}, u32[]{:S(2)}) collective-permute-start(bf16[4,3,3]{2,1,0:T(4,128)(2,1)S(1)} %get-tuple-element.69), channel_id=1, source_target_pairs={{0,5},{1,6},{2,7},{4,9},{5,10},{6,11},{8,13},{9,14},{10,15},{12,17... | collective-permute-start | bytes 224 | tf_op jit(solution)/shard_map/ppermute | solution.py:62
  134.9 12.2 %collective-permute-start.15 = (bf16[4,3,3]{2,1,0:T(4,128)(2,1)S(1)}, bf16[4,3,3]{2,1,0:T(4,128)(2,1)S(1)}, u32[]{:S(2)}, u32[]{:S(2)}) collective-permute-start(bf16[4,3,3]{2,1,0:T(4,128)(2,1)S(1)} %get-tuple-element.70), channel_id=1, source_target_pairs={{5,0},{6,1},{7,2},{9,4},{10,5},{11,6},{13,8},{14,9},{15,10},{17,12... | collective-permute-start | bytes 224 | tf_op jit(solution)/shard_map/ppermute | solution.py:65
  141.6 8.7 %collective-permute-start.13 = (bf16[4,3,3]{2,1,0:T(4,128)(2,1)S(1)}, bf16[4,3,3]{2,1,0:T(4,128)(2,1)S(1)}, u32[]{:S(2)}, u32[]{:S(2)}) collective-permute-start(bf16[4,3,3]{2,1,0:T(4,128)(2,1)S(1)} %get-tuple-element.71), channel_id=1, source_target_pairs={{4,1},{5,2},{6,3},{8,5},{9,6},{10,7},{12,9},{13,10},{14,11},{16,13... | collective-permute-start | bytes 224 | tf_op jit(solution)/shard_map/ppermute | solution.py:64
  143.5 11.1 %collective-permute-start.10 = (bf16[4,3,3]{2,1,0:T(4,128)(2,1)S(1)}, bf16[4,3,3]{2,1,0:T(4,128)(2,1)S(1)}, u32[]{:S(2)}, u32[]{:S(2)}) collective-permute-start(bf16[4,3,3]{2,1,0:T(4,128)(2,1)S(1)} %get-tuple-element.72), channel_id=1, source_target_pairs={{1,4},{2,5},{3,6},{5,8},{6,9},{7,10},{9,12},{10,13},{11,14},{13,16... | collective-permute-start | bytes 224 | tf_op jit(solution)/shard_map/ppermute | solution.py:63
  147.2 9.3 %collective-permute-start.11 = (bf16[4,16,3]{2,1,0:T(8,128)(2,1)S(1)}, bf16[4,16,3]{2,1,0:T(8,128)(2,1)S(1)}, u32[]{:S(2)}, u32[]{:S(2)}) collective-permute-start(bf16[4,16,3]{2,1,0:T(8,128)(2,1)S(1)} %get-tuple-element.75), channel_id=1, source_target_pairs={{0,1},{1,2},{2,3},{4,5},{5,6},{6,7},{8,9},{9,10},{10,11},{12,13},{... | collective-permute-start | bytes 1160 | tf_op jit(solution)/shard_map/ppermute | solution.py:60
  150.3 12.0 %collective-permute-start.12 = (bf16[4,16,3]{2,1,0:T(8,128)(2,1)S(1)}, bf16[4,16,3]{2,1,0:T(8,128)(2,1)S(1)}, u32[]{:S(2)}, u32[]{:S(2)}) collective-permute-start(bf16[4,16,3]{2,1,0:T(8,128)(2,1)S(1)} %get-tuple-element.76), channel_id=1, source_target_pairs={{1,0},{2,1},{3,2},{5,4},{6,5},{7,6},{9,8},{10,9},{11,10},{13,12},{... | collective-permute-start | bytes 1160 | tf_op jit(solution)/shard_map/ppermute | solution.py:61
  154.6 22.6 %collective-permute-start.5 = (f32[62,1,256]{2,1,0:T(1,128)}, f32[62,1,256]{2,1,0:T(1,128)}, u32[]{:S(2)}, u32[]{:S(2)}) collective-permute-start(f32[62,1,256]{2,1,0:T(1,128)} %get-tuple-element.36), channel_id=1, source_target_pairs={{0,4},{4,8},{8,12},{12,16},{16,20},{20,24},{24,28},{28,32},{32,36}... | collective-permute-start | bytes 190472 | tf_op jit(solution)/shard_map/ppermute | solution.py:77
  156.5 20.7 %collective-permute-start.4 = (f32[62,1,256]{2,1,0:T(1,128)}, f32[62,1,256]{2,1,0:T(1,128)}, u32[]{:S(2)}, u32[]{:S(2)}) collective-permute-start(f32[62,1,256]{2,1,0:T(1,128)} %get-tuple-element.37), channel_id=1, source_target_pairs={{4,0},{8,4},{12,8},{16,12},{20,16},{24,20},{28,24},{32,28},{36,32}... | collective-permute-start | bytes 190472 | tf_op jit(solution)/shard_map/ppermute | solution.py:78
  168.0 3.8 %copy-start.10 = (f32[40,264]{1,0:T(8,128)S(1)}, f32[40,264]{1,0:T(8,128)}, u32[]{:S(2)}) copy-start(f32[40,264]{1,0:T(8,128)} %get-tuple-element.20) | copy-start | bytes 126724
  168.0 3.8 %copy-start.11 = (f32[40,264]{1,0:T(8,128)S(1)}, f32[40,264]{1,0:T(8,128)}, u32[]{:S(2)}) copy-start(f32[40,264]{1,0:T(8,128)} %get-tuple-element.21) | copy-start | bytes 126724
  168.0 3.8 %copy-start.12 = (f32[40,264]{1,0:T(8,128)S(1)}, f32[40,264]{1,0:T(8,128)}, u32[]{:S(2)}) copy-start(f32[40,264]{1,0:T(8,128)} %get-tuple-element.22) | copy-start | bytes 126724
  168.0 3.8 %copy-start.13 = (f32[40,264]{1,0:T(8,128)S(1)}, f32[40,264]{1,0:T(8,128)}, u32[]{:S(2)}) copy-start(f32[40,264]{1,0:T(8,128)} %get-tuple-element.23) | copy-start | bytes 126724
  168.0 3.9 %copy-start.14 = (f32[40,264]{1,0:T(8,128)S(1)}, f32[40,264]{1,0:T(8,128)}, u32[]{:S(2)}) copy-start(f32[40,264]{1,0:T(8,128)} %get-tuple-element.24) | copy-start | bytes 126724
  168.0 3.9 %copy-start.15 = (f32[40,264]{1,0:T(8,128)S(1)}, f32[40,264]{1,0:T(8,128)}, u32[]{:S(2)}) copy-start(f32[40,264]{1,0:T(8,128)} %get-tuple-element.25) | copy-start | bytes 126724
  168.0 3.9 %copy-start.16 = (f32[40,264]{1,0:T(8,128)S(1)}, f32[40,264]{1,0:T(8,128)}, u32[]{:S(2)}) copy-start(f32[40,264]{1,0:T(8,128)} %get-tuple-element.26) | copy-start | bytes 126724
  168.1 3.9 %copy-start.17 = (f32[40,264]{1,0:T(8,128)S(1)}, f32[40,264]{1,0:T(8,128)}, u32[]{:S(2)}) copy-start(f32[40,264]{1,0:T(8,128)} %get-tuple-element.27) | copy-start | bytes 126724
  168.1 3.9 %copy-start.18 = (f32[40,264]{1,0:T(8,128)S(1)}, f32[40,264]{1,0:T(8,128)}, u32[]{:S(2)}) copy-start(f32[40,264]{1,0:T(8,128)} %get-tuple-element.28) | copy-start | bytes 126724
  171.9 5.3 %copy-start.5 = (f32[62,32,1]{2,1,0:T(8,128)S(1)}, f32[62,32,1]{2,1,0:T(8,128)}, u32[]{:S(2)}) copy-start(f32[62,32,1]{2,1,0:T(8,128)} %copy.24) | copy-start | bytes 23812
  172.4 4.8 %copy-start.4 = (f32[62,31,256]{2,1,0:T(8,128)S(1)}, f32[62,31,256]{2,1,0:T(8,128)}, u32[]{:S(2)}) copy-start(f32[62,31,256]{2,1,0:T(8,128)} %get-tuple-element.39) | copy-start | bytes 5904388
  (14 other events, 21.7 us)

commit v4 on v3

--- a/solution.py
+++ b/solution.py
@@ -3,7 +3,6 @@
 from jax import lax
 from jax.sharding import PartitionSpec as P
 from jax.experimental import pallas as pl
-from jax.experimental.pallas import tpu as pltpu
 
 AC = 128
 NSUB = 4
@@ -35,38 +34,6 @@
     left = lax.ppermute(cells[..., cols - width :], "narrow", shift_pairs(narrow_count, 1))
     right = lax.ppermute(cells[..., :width], "narrow", shift_pairs(narrow_count, -1))
     return jnp.concatenate([left, cells, right], axis=-1)
-
-
-def with_halo_once(cells, width):
-    wide_count = lax.axis_size("wide")
-    narrow_count = lax.axis_size("narrow")
-    both = ("wide", "narrow")
-    rows = cells.shape[-2]
-    cols = cells.shape[-1]
-    h = width
-
-    def diagonal(dw, dn):
-        return [
-            (w * narrow_count + n, (w + dw) * narrow_count + n + dn)
-            for w in range(wide_count)
-            for n in range(narrow_count)
-            if 0 <= w + dw < wide_count and 0 <= n + dn < narrow_count
-        ]
-
-    first_rows = cells[..., :h, :]
-    last_rows = cells[..., rows - h :, :]
-    above = lax.ppermute(last_rows, "wide", shift_pairs(wide_count, 1))
-    below = lax.ppermute(first_rows, "wide", shift_pairs(wide_count, -1))
-    left = lax.ppermute(cells[..., cols - h :], "narrow", shift_pairs(narrow_count, 1))
-    right = lax.ppermute(cells[..., :h], "narrow", shift_pairs(narrow_count, -1))
-    above_left = lax.ppermute(last_rows[..., cols - h :], both, diagonal(1, 1))
-    above_right = lax.ppermute(last_rows[..., :h], both, diagonal(1, -1))
-    below_left = lax.ppermute(first_rows[..., cols - h :], both, diagonal(-1, 1))
-    below_right = lax.ppermute(first_rows[..., :h], both, diagonal(-1, -1))
-    top = jnp.concatenate([above_left, above, above_right], axis=-1)
-    middle = jnp.concatenate([left, cells, right], axis=-1)
-    bottom = jnp.concatenate([below_left, below, below_right], axis=-1)
-    return jnp.concatenate([top, middle, bottom], axis=-2)
 
 
 def plus_halo(cells):
@@ -284,7 +251,6 @@
     peers = lax.axis_size(("wide", "narrow"))
     wide_count = lax.axis_size("wide")
     narrow_count = lax.axis_size("narrow")
-    features = atm_state.shape[0]
     columns_here = atm_state.shape[1]
     nflux = flux_map.shape[1]
     capacity = 2 * columns_here // peers
@@ -307,38 +273,42 @@
         axis=0,
     )
     planes_ext = with_halo(planes, h)
+    t_above, t_below, t_left, t_right = plus_halo(tracer)
+    mask_ext = planes_ext[0]
+    m_above = mask_ext[None, h - 1 : h, h:-h]
+    m_below = mask_ext[None, h + ocean_rows : h + ocean_rows + 1, h:-h]
+    m_left = mask_ext[None, h:-h, h - 1 : h]
+    m_right = mask_ext[None, h:-h, h + ocean_cols : h + ocean_cols + 1]
+    tracer_mixed = diffuse(
+        tracer, t_above, t_below, t_left, t_right, mask[None], m_above, m_below, m_left, m_right
+    )
+
+    owners = group_owner[:, 0]
+    slots = owners * capacity + column_ranks(owners, peers)
+    initial = atm_state.astype(jnp.bfloat16)
+    outgoing = place_columns(initial, slots, total_slots)
+    arrived = lax.all_to_all(outgoing, ("wide", "narrow"), split_axis=0, concat_axis=0, tiled=True)
+    physics_out, tracer_mixed, planes_ext = lax.optimization_barrier(
+        (physics(regime_ops[0], arrived, flux_map), tracer_mixed, planes_ext)
+    )
+    back = lax.all_to_all(
+        physics_out,
+        ("wide", "narrow"),
+        split_axis=0,
+        concat_axis=0,
+        tiled=True,
+    )
+    returned = jnp.take(back, slots, axis=0, mode="clip")
+    atm_new, flux_cols = unpack(returned, atm_state)
     mask_ext = planes_ext[0]
     eta = planes_ext[1]
     flow_u = planes_ext[2]
     flow_v = planes_ext[3]
     src_ext = planes_ext[4 : 4 + kk].astype(jnp.int32)
     weight_ext = planes_ext[4 + kk : 4 + 2 * kk]
-    t_above, t_below, t_left, t_right = plus_halo(tracer)
-    m_above = mask_ext[None, h - 1 : h, h:-h]
-    m_below = mask_ext[None, h + ocean_rows : h + ocean_rows + 1, h:-h]
-    m_left = mask_ext[None, h:-h, h - 1 : h]
-    m_right = mask_ext[None, h:-h, h + ocean_cols : h + ocean_cols + 1]
-    tracer_mixed = diffuse(
-        tracer, t_above, t_below, t_left, t_right, mask[None], m_above, m_below, m_left, m_right
-    )
-
-    owners = group_owner[:, 0]
-    slots = owners * capacity + column_ranks(owners, peers)
-    initial = atm_state.astype(jnp.bfloat16)
-    outgoing = place_columns(initial, slots, total_slots)
-    arrived = lax.all_to_all(outgoing, ("wide", "narrow"), split_axis=0, concat_axis=0, tiled=True)
-    back = lax.all_to_all(
-        physics(regime_ops[0], arrived, flux_map),
-        ("wide", "narrow"),
-        split_axis=0,
-        concat_axis=0,
-        tiled=True,
-    )
-    returned = jnp.take(back, slots, axis=0, mode="clip")
-    atm_new, flux_cols = unpack(returned, atm_state)
 
     flux_block = flux_cols.astype(jnp.bfloat16).reshape(nflux, block_rows, AC)
-    flux_ext = with_halo_once(flux_block, ATM_HALO)
+    flux_ext = with_halo(flux_block, ATM_HALO)
     ocean_flux = remap(
         flux_ext,
         src_ext,
@@ -354,7 +324,7 @@
 
     mask_east = next_col(mask_ext)
     mask_north = next_row(mask_ext)
-    for substep in range(NSUB):
+    for _ in range(NSUB):
         flow_u = momentum(flow_u, eta, next_col(eta), mask_ext, mask_east, ocean_flux[2])
         flow_v = momentum(flow_v, eta, next_row(eta), mask_ext, mask_north, ocean_flux[3])
         eta = continuity(
@@ -382,6 +352,5 @@
         P("wide", "narrow"),
         P(None, "wide", "narrow"),
     )
-    return jax.shard_map(
-        per_device, mesh=mesh, in_specs=in_specs, out_specs=out_specs, check_vma=False
-    )
+
+    return jax.shard_map(per_device, mesh=mesh, in_specs=in_specs, out_specs=out_specs, check_vma=False)

time: 183 us -> 179 us (0.978)
  waiting for transfers between devices: 21.1 us -> 39 us
  starting transfers between devices: 70.9 us -> 56 us
  local copies, waits for them, and re-layouts: 42.7 us -> 37.8 us
  other arithmetic: 21.6 us -> 18.2 us
    all_to_all x1, waiting for transfers between devices: 0.01 us -> 28.7 us  [per_device(): lax.all_to_all(physics_out, ('wide', 'narrow'), split_axis=0, concat_axis...]
    ppermute x8 -> x0, starting transfers between devices: 27.6 us -> none  [the longest x1 6.65 us: with_halo_once(): below_right = lax.ppermute(first_rows[..., :h], both, diagonal(-1, -1))]
    all_to_all x1, waiting for transfers between devices: 6.75 us -> 0.01 us  [per_device(): lax.all_to_all(outgoing, ('wide', 'narrow'), split_axis=0, concat_axis=0,...]
    ppermute x1 -> x2, waiting for transfers between devices: 13.4 us -> 6.81 us  [with_halo(): lax.ppermute(cells[..., cols - width:], 'narrow', shift_pairs(narrow_coun...]
    ppermute x1 -> x2, starting transfers between devices: 5.75 us -> 11.4 us  [with_halo(): lax.ppermute(cells[..., :width, :], 'wide', shift_pairs(wide_count, -1))]
    dot_general x8, matrix products: 7.84 us -> 13.1 us  [place_columns(): lax.dot_general(selector, source, (((1,), (1,)), ((), ())), preferred_ele...]
    ppermute x1, starting transfers between devices: 5.75 us -> 1.91 us  [plus_halo(): below = lax.ppermute(cells[:, :1, :], 'wide', shift_pairs(wide_count, -1))]
    ppermute x1 -> x2, starting transfers between devices: 3.15 us -> 6.05 us  [with_halo(): lax.ppermute(cells[..., :width], 'narrow', shift_pairs(narrow_count, -1))]
  transfers between devices with their start and end apart: 18 -> 14, of which waited for: 3 -> 5; matrix products, arithmetic and copies ran while one was open for 31% -> 28% of each run, Pallas kernels for 3% -> 0%
where the time goes in v4:
time: 179 us; the launch traced here: 177 us
  starting transfers between devices  56 us (31%)
  waiting for transfers between devices  39 us (22%)
  local copies, waits for them, and re-layouts  37.8 us (21%)
  other arithmetic  18.2 us (10%)
  matrix products  14.3 us (8%)
  Pallas kernels  10.2 us (6%)
    all_to_all x1, waiting for transfers between devices, per_device(): lax.all_to_all(physics_out, ('wide', 'narrow'), split_axis=0, concat_axis...  28.7 us
    dot_general x8, matrix products, place_columns(): lax.dot_general(selector, source, (((1,), (1,)), ((), ())), preferred_ele...  13.1 us
    ppermute x2, starting transfers between devices, with_halo(): lax.ppermute(cells[..., :width, :], 'wide', shift_pairs(wide_count, -1))  11.4 us
    all_to_all x1, starting transfers between devices, per_device(): lax.all_to_all(outgoing, ('wide', 'narrow'), split_axis=0, concat_axis=0,...  9.67 us
    all_to_all x1, starting transfers between devices, per_device(): lax.all_to_all(physics_out, ('wide', 'narrow'), split_axis=0, concat_axis...  9.47 us
    gather x1, local copies, waits for them, and re-layouts, per_device(): returned = jnp.take(back, slots, axis=0, mode='clip')  9.02 us
    unnamed x30, local copies, waits for them, and re-layouts  7.86 us
    ppermute x2, waiting for transfers between devices, with_halo(): lax.ppermute(cells[..., cols - width:], 'narrow', shift_pairs(narrow_coun...  6.81 us
  transfers between devices with their start and end apart: 14, of which 5 were waited for; matrix products, arithmetic and copies ran while one was open for 28% of the time, Pallas kernels for 0%

profile of v4, /device:TPU:34, one launch (start us, length us, event | category | flops | bytes accessed | tf_op | source)
XLA Modules:
  0.0 176.8 jit_solution(10370152097669971305)
XLA Ops:
  5.5 1.9 %collective-permute-start = (f32[12,4,256]{2,1,0:T(4,128)}, f32[12,4,256]{2,1,0:T(4,128)}, u32[]{:S(2)}, u32[]{:S(2)}) collective-permute-start(f32[12,4,256]{2,1,0:T(4,128)} %get-tuple-element.55), channel_id=1, source_target_pairs={{0,4},{4,8},{8,12},{12,16},{16,20},{20,24},{24,28},{28,32},{32,36}... | collective-permute-start | bytes 147464 | tf_op jit(solution)/shard_map/ppermute | solution.py:31
  7.4 5.8 %collective-permute-start.1 = (f32[12,4,256]{2,1,0:T(4,128)}, f32[12,4,256]{2,1,0:T(4,128)}, u32[]{:S(2)}, u32[]{:S(2)}) collective-permute-start(f32[12,4,256]{2,1,0:T(4,128)} %get-tuple-element.56), channel_id=1, source_target_pairs={{4,0},{8,4},{12,8},{16,12},{20,16},{24,20},{28,24},{32,28},{36,32}... | collective-permute-start | bytes 147464 | tf_op jit(solution)/shard_map/ppermute | solution.py:32
  13.2 2.8 %fusion.127 = (f32[62,32,1]{2,1,0:T(8,128)S(1)}, f32[62,32,1]{2,1,0:T(8,128)}) fusion(f32[62,32,256]{2,1,0:T(8,128)} %param.19), kind=kLoop, calls=%fused_computation.221 | loop fusion | bytes 31744 | tf_op jit(solution)/shard_map/slice | solution.py:46
  16.0 2.5 %copy.27 = f32[62,32,1]{0,1,2:T(8,128)} copy(f32[62,32,1]{2,1,0:T(8,128)} %get-tuple-element.40) | data formatting | bytes 15872
  18.5 2.4 %collective-permute-start.6 = (f32[62,32]{0,1:T(8,128)}, f32[62,32]{0,1:T(8,128)}, u32[]{:S(2)}, u32[]{:S(2)}) collective-permute-start(f32[62,32]{0,1:T(8,128)} %bitcast.14), channel_id=1, source_target_pairs={{1,0},{2,1},{3,2},{5,4},{6,5},{7,6},{9,8},{10,9},{11,10},{13,12},{... | collective-permute-start | bytes 23816 | tf_op jit(solution)/shard_map/ppermute | solution.py:47
  22.3 3.4 %collective-permute-start.7 = (f32[62,32]{0,1:T(8,128)}, f32[62,32]{0,1:T(8,128)}, u32[]{:S(2)}, u32[]{:S(2)}) collective-permute-start(f32[62,32]{0,1:T(8,128)} %bitcast.17), channel_id=1, source_target_pairs={{0,1},{1,2},{2,3},{4,5},{5,6},{6,7},{8,9},{9,10},{10,11},{12,13},{... | collective-permute-start | bytes 23816 | tf_op jit(solution)/shard_map/ppermute | solution.py:46
  26.4 1.9 %collective-permute-start.4 = (f32[62,1,256]{2,1,0:T(1,128)}, f32[62,1,256]{2,1,0:T(1,128)}, u32[]{:S(2)}, u32[]{:S(2)}) collective-permute-start(f32[62,1,256]{2,1,0:T(1,128)} %get-tuple-element.44), channel_id=1, source_target_pairs={{4,0},{8,4},{12,8},{16,12},{20,16},{24,20},{28,24},{32,28},{36,32}... | collective-permute-start | bytes 190472 | tf_op jit(solution)/shard_map/ppermute | solution.py:45
  34.6 1.6 fusion.44
  36.3 1.6 fusion.50
  37.9 1.6 fusion.56
  42.9 1.6 fusion.74
  46.2 3.6 %copy.21 = bf16[4096,144]{1,0:T(8,128)(2,1)} copy(bf16[4096,144]{0,1:T(8,128)(2,1)} %fusion.80) | data formatting | bytes 2359296 | tf_op jit(solution)/shard_map/concatenate | solution.py:73
  49.8 9.7 %all-to-all-start = ((bf16[128,32,144]{2,1,0:T(8,128)(2,1)}), bf16[128,32,144]{2,1,0:T(8,128)(2,1)}, u32[]{:S(2)}, u32[]{:S(2)}) async-start(bf16[128,32,144]{2,1,0:T(8,128)(2,1)} %bitcast.158), calls=%async_computation | async-start | bytes 4194304 | tf_op jit(solution)/shard_map/all_to_all | solution.py:290
  59.6 2.7 %fusion.128 = (f32[62,32,255]{2,1,0:T(8,128)}, f32[62,32,255]{2,1,0:T(8,128)}) fusion(f32[62,32,256]{2,1,0:T(8,128)S(1)} %copy-done), kind=kLoop, calls=%fused_computation.222 | loop fusion | bytes 8094720 | tf_op jit(solution)/shard_map/slice | solution.py:202
  62.3 2.3 %fusion.130 = (f32[62,31,256]{2,1,0:T(8,128)}, f32[62,31,256]{2,1,0:T(8,128)}) fusion(f32[62,32,256]{2,1,0:T(8,128)S(1)} %copy-done), kind=kLoop, calls=%fused_computation.224 | loop fusion | bytes 7872512 | tf_op jit(solution)/shard_map/slice | solution.py:200
  67.1 3.4 %collective-permute-start.2 = (f32[12,40,4]{2,1,0:T(8,128)}, f32[12,40,4]{2,1,0:T(8,128)S(1)}, u32[]{:S(2)}, u32[]{:S(2)}) collective-permute-start(f32[12,40,4]{2,1,0:T(8,128)} %get-tuple-element.53), channel_id=1, source_target_pairs={{0,1},{1,2},{2,3},{4,5},{5,6},{6,7},{8,9},{9,10},{10,11},{12,13},{... | collective-permute-start | bytes 23048 | tf_op jit(solution)/shard_map/ppermute | solution.py:34
  70.5 2.6 %collective-permute-start.3 = (f32[12,40,4]{2,1,0:T(8,128)S(1)}, f32[12,40,4]{2,1,0:T(8,128)}, u32[]{:S(2)}, u32[]{:S(2)}) collective-permute-start(f32[12,40,4]{2,1,0:T(8,128)S(1)} %get-tuple-element.54), channel_id=1, source_target_pairs={{1,0},{2,1},{3,2},{5,4},{6,5},{7,6},{9,8},{10,9},{11,10},{13,12},{... | collective-permute-start | bytes 23048 | tf_op jit(solution)/shard_map/ppermute | solution.py:35
  73.9 1.9 %collective-permute-start.5 = (f32[62,1,256]{2,1,0:T(1,128)}, f32[62,1,256]{2,1,0:T(1,128)S(1)}, u32[]{:S(2)}, u32[]{:S(2)}) collective-permute-start(f32[62,1,256]{2,1,0:T(1,128)} %get-tuple-element.43), channel_id=1, source_target_pairs={{0,4},{4,8},{8,12},{12,16},{16,20},{20,24},{24,28},{28,32},{32,36}... | collective-permute-start | bytes 190472 | tf_op jit(solution)/shard_map/ppermute | solution.py:44
  75.8 2.5 %copy.24 = f32[62,32,1]{2,1,0:T(8,128)} copy(f32[62,32,1]{0,1,2:T(8,128)} %bitcast.15) | data formatting | bytes 15872 | tf_op jit(solution)/shard_map/broadcast_in_dim | solution.py:48
  78.3 2.5 %copy.26 = f32[62,32,1]{2,1,0:T(8,128)} copy(f32[62,32,1]{0,1,2:T(8,128)} %bitcast.18) | data formatting | bytes 15872 | tf_op jit(solution)/shard_map/broadcast_in_dim | solution.py:48
  80.8 6.8 %collective-permute-done.2 = f32[12,40,4]{2,1,0:T(8,128)S(1)} collective-permute-done((f32[12,40,4]{2,1,0:T(8,128)}, f32[12,40,4]{2,1,0:T(8,128)S(1)}, u32[]{:S(2)}, u32[]{:S(2)}) %collective-permute-start.2) | collective-permute-done | bytes 7712 | tf_op jit(solution)/shard_map/ppermute | solution.py:34
  90.5 5.1 %fusion.35 = f32[62,32,256]{2,1,0:T(8,128)} fusion(f32[62,32,256]{2,1,0:T(8,128)S(1)} %copy-done, f32[62,1,256]{2,1,0:T(1,128)} %collective-permute-done.4, f32[62,31,256]{2,1,0:T(8,128)} %get-tuple-element.46, f32[62,31,256]{2,1,0:T(8,128)} %get-tuple-element.45, f32[62,1,256]{2,1,0:T(1,128)S(1)} %collective-permute-done.5, f32[62,32,1]{2,1,0:T(8,128)} %copy.24, ...), kind=kLoop, calls=%fused_computation.38 | loop fusion | flops 8634368 | bytes 12320768 | tf_op jit(solution)/shard_map/add | solution.py:210
  95.6 6.1 %shard_map.129 = bf16[4096,148]{1,0:T(8,128)(2,1)} custom-call(bf16[4096,144]{1,0:T(8,128)(2,1)} %bitcast.6.x_ref, bf16[4,144,144]{2,1,0:T(8,128)(2,1)} %bitcast.167, bf16[144,4]{1,0:T(8,128)(2,1)} %copy.22.fm_ref), custom_call_target="tpu_custom_call" | custom-call | flops 684195840 | bytes 2557952 | tf_op jit(solution)/shard_map/pallas_call | solution.py:97
  101.7 9.5 %all-to-all-start.1 = ((bf16[128,32,148]{2,1,0:T(8,128)(2,1)}), bf16[128,32,148]{2,1,0:T(8,128)(2,1)S(1)}, u32[]{:S(2)}, u32[]{:S(2)}) async-start(bf16[128,32,148]{2,1,0:T(8,128)(2,1)} %bitcast.157), calls=%async_computation.1 | async-start | bytes 4194304 | tf_op jit(solution)/shard_map/all_to_all | solution.py:294
  111.4 28.7 %all-to-all-done.1 = bf16[128,32,148]{2,1,0:T(8,128)(2,1)S(1)} async-done(((bf16[128,32,148]{2,1,0:T(8,128)(2,1)}), bf16[128,32,148]{2,1,0:T(8,128)(2,1)S(1)}, u32[]{:S(2)}, u32[]{:S(2)}) %all-to-all-start.1) | async-done | bytes 1212448 | tf_op jit(solution)/shard_map/all_to_all | solution.py:294
  140.1 9.0 %gather_fusion = bf16[2048,148]{1,0:T(8,128)(2,1)} fusion(bf16[4096,148]{1,0:T(8,128)(2,1)S(1)} %bitcast.156, s32[2048]{0:T(1024)S(1)} %broadcast_clamp_fusion), kind=kCustom, calls=%fused_computation | custom fusion | bytes 1220608 | tf_op jit(solution)/shard_map/jit(_take)/gather | solution.py:301
  149.1 4.1 %shard_map.130 = (f32[144,2048]{1,0:T(8,128)}, bf16[4,2048]{1,0:T(4,128)(2,1)}) custom-call(bf16[2048,148]{1,0:T(8,128)(2,1)} %gather_fusion, f32[144,2048]{1,0:T(8,128)} %atm_ref.1, bf16[148,148]{1,0:T(8,128)(2,1)} %fusion.101.eye_ref), custom_call_target="tpu_custom_call" | custom-call | flops 89718784 | bytes 3571712 | tf_op jit(solution)/shard_map/pallas_call | solution.py:129
  154.0 2.1 %collective-permute-start.8 = (bf16[4,3,128]{2,1,0:T(4,128)(2,1)S(1)}, bf16[4,3,128]{2,1,0:T(4,128)(2,1)S(1)}, u32[]{:S(2)}, u32[]{:S(2)}) collective-permute-start(bf16[4,3,128]{2,1,0:T(4,128)(2,1)S(1)} %get-tuple-element.82), channel_id=1, source_target_pairs={{0,4},{4,8},{8,12},{12,16},{16,20},{20,24},{24,28},{28,32},{32,36}... | collective-permute-start | bytes 9224 | tf_op jit(solution)/shard_map/ppermute | solution.py:31
  156.0 5.6 %collective-permute-start.9 = (bf16[4,3,128]{2,1,0:T(4,128)(2,1)S(1)}, bf16[4,3,128]{2,1,0:T(4,128)(2,1)S(1)}, u32[]{:S(2)}, u32[]{:S(2)}) collective-permute-start(bf16[4,3,128]{2,1,0:T(4,128)(2,1)S(1)} %get-tuple-element.83), channel_id=1, source_target_pairs={{4,0},{8,4},{12,8},{16,12},{20,16},{24,20},{28,24},{32,28},{36,32}... | collective-permute-start | bytes 9224 | tf_op jit(solution)/shard_map/ppermute | solution.py:32
  163.0 2.4 %collective-permute-start.10 = (bf16[4,22,3]{2,1,0:T(8,128)(2,1)S(1)}, bf16[4,22,3]{2,1,0:T(8,128)(2,1)S(1)}, u32[]{:S(2)}, u32[]{:S(2)}) collective-permute-start(bf16[4,22,3]{2,1,0:T(8,128)(2,1)S(1)} %get-tuple-element.80), channel_id=1, source_target_pairs={{0,1},{1,2},{2,3},{4,5},{5,6},{6,7},{8,9},{9,10},{10,11},{12,13},{... | collective-permute-start | bytes 1592 | tf_op jit(solution)/shard_map/ppermute | solution.py:34
  165.5 3.4 %collective-permute-start.11 = (bf16[4,22,3]{2,1,0:T(8,128)(2,1)S(1)}, bf16[4,22,3]{2,1,0:T(8,128)(2,1)S(1)}, u32[]{:S(2)}, u32[]{:S(2)}) collective-permute-start(bf16[4,22,3]{2,1,0:T(8,128)(2,1)S(1)} %get-tuple-element.81), channel_id=1, source_target_pairs={{1,0},{2,1},{3,2},{5,4},{6,5},{7,6},{9,8},{10,9},{11,10},{13,12},{... | collective-permute-start | bytes 1592 | tf_op jit(solution)/shard_map/ppermute | solution.py:35
  169.3 1.9 %collective-permute-done.11 = bf16[4,22,3]{2,1,0:T(8,128)(2,1)S(1)} collective-permute-done((bf16[4,22,3]{2,1,0:T(8,128)(2,1)S(1)}, bf16[4,22,3]{2,1,0:T(8,128)(2,1)S(1)}, u32[]{:S(2)}, u32[]{:S(2)}) %collective-permute-start.11) | collective-permute-done | bytes 560 | tf_op jit(solution)/shard_map/ppermute | solution.py:35
  (119 shorter events, 32.3 us)
Async XLA Ops:
  5.5 59.8 %collective-permute-start = (f32[12,4,256]{2,1,0:T(4,128)}, f32[12,4,256]{2,1,0:T(4,128)}, u32[]{:S(2)}, u32[]{:S(2)}) collective-permute-start(f32[12,4,256]{2,1,0:T(4,128)} %get-tuple-element.55), channel_id=1, source_target_pairs={{0,4},{4,8},{8,12},{12,16},{16,20},{20,24},{24,28},{28,32},{32,36}... | collective-permute-start | bytes 147464 | tf_op jit(solution)/shard_map/ppermute | solution.py:31
  7.4 57.9 %collective-permute-start.1 = (f32[12,4,256]{2,1,0:T(4,128)}, f32[12,4,256]{2,1,0:T(4,128)}, u32[]{:S(2)}, u32[]{:S(2)}) collective-permute-start(f32[12,4,256]{2,1,0:T(4,128)} %get-tuple-element.56), channel_id=1, source_target_pairs={{4,0},{8,4},{12,8},{16,12},{20,16},{24,20},{28,24},{32,28},{36,32}... | collective-permute-start | bytes 147464 | tf_op jit(solution)/shard_map/ppermute | solution.py:32
  16.0 9.7 %copy-start = (f32[62,32,256]{2,1,0:T(8,128)S(1)}, f32[62,32,256]{2,1,0:T(8,128)}, u32[]{:S(2)}) copy-start(f32[62,32,256]{2,1,0:T(8,128)} %param.19) | copy-start | bytes 6094852
  16.0 15.1 %copy-start.5 = (s32[2048,1]{0,1:T(1,128)S(1)}, s32[2048,1]{0,1:T(1,128)}, u32[]{:S(2)}) copy-start(s32[2048,1]{0,1:T(1,128)} %param.13) | copy-start | bytes 24580
  18.5 55.3 %collective-permute-start.6 = (f32[62,32]{0,1:T(8,128)}, f32[62,32]{0,1:T(8,128)}, u32[]{:S(2)}, u32[]{:S(2)}) collective-permute-start(f32[62,32]{0,1:T(8,128)} %bitcast.14), channel_id=1, source_target_pairs={{1,0},{2,1},{3,2},{5,4},{6,5},{7,6},{9,8},{10,9},{11,10},{13,12},{... | collective-permute-start | bytes 23816 | tf_op jit(solution)/shard_map/ppermute | solution.py:47
  22.3 56.0 %collective-permute-start.7 = (f32[62,32]{0,1:T(8,128)}, f32[62,32]{0,1:T(8,128)}, u32[]{:S(2)}, u32[]{:S(2)}) collective-permute-start(f32[62,32]{0,1:T(8,128)} %bitcast.17), channel_id=1, source_target_pairs={{0,1},{1,2},{2,3},{4,5},{5,6},{6,7},{8,9},{9,10},{10,11},{12,13},{... | collective-permute-start | bytes 23816 | tf_op jit(solution)/shard_map/ppermute | solution.py:46
  26.4 64.0 %collective-permute-start.4 = (f32[62,1,256]{2,1,0:T(1,128)}, f32[62,1,256]{2,1,0:T(1,128)}, u32[]{:S(2)}, u32[]{:S(2)}) collective-permute-start(f32[62,1,256]{2,1,0:T(1,128)} %get-tuple-element.44), channel_id=1, source_target_pairs={{4,0},{8,4},{12,8},{16,12},{20,16},{24,20},{28,24},{32,28},{36,32}... | collective-permute-start | bytes 190472 | tf_op jit(solution)/shard_map/ppermute | solution.py:45
  31.6 1.3 copy-start.2
  32.9 1.7 copy-start.11
  33.0 3.3 %copy-start.10 = (s32[512]{0:T(512)S(1)}, s32[512]{0:T(512)}, u32[]{:S(2)}) copy-start(s32[512]{0:T(512)} %iota_add_fusion.6) | copy-start | bytes 6148
  34.6 3.3 %copy-start.9 = (s32[512]{0:T(512)S(1)}, s32[512]{0:T(512)}, u32[]{:S(2)}) copy-start(s32[512]{0:T(512)} %iota_add_fusion.5) | copy-start | bytes 6148
  36.3 3.3 %copy-start.8 = (s32[512]{0:T(512)S(1)}, s32[512]{0:T(512)}, u32[]{:S(2)}) copy-start(s32[512]{0:T(512)} %iota_add_fusion.4) | copy-start | bytes 6148
  37.9 3.3 %copy-start.7 = (s32[512]{0:T(512)S(1)}, s32[512]{0:T(512)}, u32[]{:S(2)}) copy-start(s32[512]{0:T(512)} %iota_add_fusion.3) | copy-start | bytes 6148
  49.8 9.7 %copy-start.3 = (s32[32,256]{1,0:T(8,128)S(1)}, s32[32,256]{1,0:T(8,128)}, u32[]{:S(2)}) copy-start(s32[32,256]{1,0:T(8,128)} %param.18) | copy-start | bytes 98308
  49.8 45.8 %all-to-all-start = ((bf16[128,32,144]{2,1,0:T(8,128)(2,1)}), bf16[128,32,144]{2,1,0:T(8,128)(2,1)}, u32[]{:S(2)}, u32[]{:S(2)}) async-start(bf16[128,32,144]{2,1,0:T(8,128)(2,1)} %bitcast.158), calls=%async_computation | async-start | bytes 4194304 | tf_op jit(solution)/shard_map/all_to_all | solution.py:290
  64.6 8.5 %copy-start.6 = (bf16[144,4]{0,1:T(4,128)(2,1)S(1)}, bf16[144,4]{0,1:T(4,128)(2,1)}, u32[]{:S(2)}) copy-start(bf16[144,4]{0,1:T(4,128)(2,1)} %param.15) | copy-start | bytes 3460
  67.1 20.5 %collective-permute-start.2 = (f32[12,40,4]{2,1,0:T(8,128)}, f32[12,40,4]{2,1,0:T(8,128)S(1)}, u32[]{:S(2)}, u32[]{:S(2)}) collective-permute-start(f32[12,40,4]{2,1,0:T(8,128)} %get-tuple-element.53), channel_id=1, source_target_pairs={{0,1},{1,2},{2,3},{4,5},{5,6},{6,7},{8,9},{9,10},{10,11},{12,13},{... | collective-permute-start | bytes 23048 | tf_op jit(solution)/shard_map/ppermute | solution.py:34
  70.5 18.2 %collective-permute-start.3 = (f32[12,40,4]{2,1,0:T(8,128)S(1)}, f32[12,40,4]{2,1,0:T(8,128)}, u32[]{:S(2)}, u32[]{:S(2)}) collective-permute-start(f32[12,40,4]{2,1,0:T(8,128)S(1)} %get-tuple-element.54), channel_id=1, source_target_pairs={{1,0},{2,1},{3,2},{5,4},{6,5},{7,6},{9,8},{10,9},{11,10},{13,12},{... | collective-permute-start | bytes 23048 | tf_op jit(solution)/shard_map/ppermute | solution.py:35
  73.9 16.6 %collective-permute-start.5 = (f32[62,1,256]{2,1,0:T(1,128)}, f32[62,1,256]{2,1,0:T(1,128)S(1)}, u32[]{:S(2)}, u32[]{:S(2)}) collective-permute-start(f32[62,1,256]{2,1,0:T(1,128)} %get-tuple-element.43), channel_id=1, source_target_pairs={{0,4},{4,8},{8,12},{12,16},{16,20},{20,24},{24,28},{28,32},{32,36}... | collective-permute-start | bytes 190472 | tf_op jit(solution)/shard_map/ppermute | solution.py:44
  80.8 9.7 %copy-start.1 = (f32[62,32,255]{2,1,0:T(8,128)S(1)}, f32[62,32,255]{2,1,0:T(8,128)}, u32[]{:S(2)}) copy-start(f32[62,32,255]{2,1,0:T(8,128)} %get-tuple-element.41) | copy-start | bytes 6071044
  87.6 0.7 copy-start.4
  101.7 38.4 %all-to-all-start.1 = ((bf16[128,32,148]{2,1,0:T(8,128)(2,1)}), bf16[128,32,148]{2,1,0:T(8,128)(2,1)S(1)}, u32[]{:S(2)}, u32[]{:S(2)}) async-start(bf16[128,32,148]{2,1,0:T(8,128)(2,1)} %bitcast.157), calls=%async_computation.1 | async-start | bytes 4194304 | tf_op jit(solution)/shard_map/all_to_all | solution.py:294
  154.0 7.7 %collective-permute-start.8 = (bf16[4,3,128]{2,1,0:T(4,128)(2,1)S(1)}, bf16[4,3,128]{2,1,0:T(4,128)(2,1)S(1)}, u32[]{:S(2)}, u32[]{:S(2)}) collective-permute-start(bf16[4,3,128]{2,1,0:T(4,128)(2,1)S(1)} %get-tuple-element.82), channel_id=1, source_target_pairs={{0,4},{4,8},{8,12},{12,16},{16,20},{20,24},{24,28},{28,32},{32,36}... | collective-permute-start | bytes 9224 | tf_op jit(solution)/shard_map/ppermute | solution.py:31
  156.0 6.9 %collective-permute-start.9 = (bf16[4,3,128]{2,1,0:T(4,128)(2,1)S(1)}, bf16[4,3,128]{2,1,0:T(4,128)(2,1)S(1)}, u32[]{:S(2)}, u32[]{:S(2)}) collective-permute-start(bf16[4,3,128]{2,1,0:T(4,128)(2,1)S(1)} %get-tuple-element.83), channel_id=1, source_target_pairs={{4,0},{8,4},{12,8},{16,12},{20,16},{24,20},{28,24},{32,28},{36,32}... | collective-permute-start | bytes 9224 | tf_op jit(solution)/shard_map/ppermute | solution.py:32
  163.0 6.3 %collective-permute-start.10 = (bf16[4,22,3]{2,1,0:T(8,128)(2,1)S(1)}, bf16[4,22,3]{2,1,0:T(8,128)(2,1)S(1)}, u32[]{:S(2)}, u32[]{:S(2)}) collective-permute-start(bf16[4,22,3]{2,1,0:T(8,128)(2,1)S(1)} %get-tuple-element.80), channel_id=1, source_target_pairs={{0,1},{1,2},{2,3},{4,5},{5,6},{6,7},{8,9},{9,10},{10,11},{12,13},{... | collective-permute-start | bytes 1592 | tf_op jit(solution)/shard_map/ppermute | solution.py:34
  165.5 5.7 %collective-permute-start.11 = (bf16[4,22,3]{2,1,0:T(8,128)(2,1)S(1)}, bf16[4,22,3]{2,1,0:T(8,128)(2,1)S(1)}, u32[]{:S(2)}, u32[]{:S(2)}) collective-permute-start(bf16[4,22,3]{2,1,0:T(8,128)(2,1)S(1)} %get-tuple-element.81), channel_id=1, source_target_pairs={{1,0},{2,1},{3,2},{5,4},{6,5},{7,6},{9,8},{10,9},{11,10},{13,12},{... | collective-permute-start | bytes 1592 | tf_op jit(solution)/shard_map/ppermute | solution.py:35

commit v5 on v4

--- a/solution.py
+++ b/solution.py
@@ -288,11 +288,8 @@
     initial = atm_state.astype(jnp.bfloat16)
     outgoing = place_columns(initial, slots, total_slots)
     arrived = lax.all_to_all(outgoing, ("wide", "narrow"), split_axis=0, concat_axis=0, tiled=True)
-    physics_out, tracer_mixed, planes_ext = lax.optimization_barrier(
-        (physics(regime_ops[0], arrived, flux_map), tracer_mixed, planes_ext)
-    )
     back = lax.all_to_all(
-        physics_out,
+        physics(regime_ops[0], arrived, flux_map),
         ("wide", "narrow"),
         split_axis=0,
         concat_axis=0,

time: 179 us -> 167 us (0.933)
  waiting for transfers between devices: 39 us -> 20.2 us
  local copies, waits for them, and re-layouts: 37.8 us -> 43.3 us
  other arithmetic: 18.2 us -> 22.2 us
    all_to_all x1, waiting for transfers between devices: 28.7 us -> 0.01 us  [per_device(): lax.all_to_all(physics(regime_ops[0], arrived, flux_map), ('wide', 'narro...]
    all_to_all x1, waiting for transfers between devices: 0.01 us -> 9.15 us  [per_device(): lax.all_to_all(outgoing, ('wide', 'narrow'), split_axis=0, concat_axis=0,...]
    dot_general x8, matrix products: 13.1 us -> 7.84 us  [place_columns(): lax.dot_general(selector, source, (((1,), (1,)), ((), ())), preferred_ele...]
    dot_general x3, matrix products: 0.84 us -> 3.71 us  [remap(): jnp.einsum('ap,fpx->fax', row_sel, by_cols, preferred_element_type=jnp.fl...]
    add x7, other arithmetic: 2.73 us -> 0.03 us  [place_columns(): start + jnp.arange(width, dtype=jnp.int32)]
    all_to_all x1, starting transfers between devices: 9.47 us -> 6.86 us  [per_device(): lax.all_to_all(physics(regime_ops[0], arrived, flux_map), ('wide', 'narro...]
    add x1, other arithmetic: 5.14 us -> 2.66 us  [diffuse(): return centre + kappa_mix * summed]
    mul x4 -> x5, other arithmetic: 0.21 us -> 2.28 us  [momentum(): mask * mask_next]
  transfers between devices with their start and end apart: 14 -> 14, of which waited for: 5 -> 4; matrix products, arithmetic and copies ran while one was open for 28% -> 43% of each run, Pallas kernels for 0% -> 6%
where the time goes in v5:
time: 167 us; the launch traced here: 165 us
  starting transfers between devices  54.7 us (33%)
  local copies, waits for them, and re-layouts  43.3 us (26%)
  other arithmetic  22.2 us (13%)
  waiting for transfers between devices  20.2 us (12%)
  matrix products  13.5 us (8%)
  Pallas kernels  10.2 us (6%)
    gather x1, local copies, waits for them, and re-layouts, per_device(): returned = jnp.take(back, slots, axis=0, mode='clip')  10.3 us
    ppermute x2, starting transfers between devices, with_halo(): lax.ppermute(cells[..., :width, :], 'wide', shift_pairs(wide_count, -1))  9.84 us
    unnamed x64, local copies, waits for them, and re-layouts  9.17 us
    all_to_all x1, waiting for transfers between devices, per_device(): lax.all_to_all(outgoing, ('wide', 'narrow'), split_axis=0, concat_axis=0,...  9.15 us
    ppermute x2, waiting for transfers between devices, with_halo(): lax.ppermute(cells[..., cols - width:], 'narrow', shift_pairs(narrow_coun...  8.65 us
    all_to_all x1, starting transfers between devices, per_device(): lax.all_to_all(outgoing, ('wide', 'narrow'), split_axis=0, concat_axis=0,...  8.56 us
    dot_general x8, matrix products, place_columns(): lax.dot_general(selector, source, (((1,), (1,)), ((), ())), preferred_ele...  7.84 us
    all_to_all x1, starting transfers between devices, per_device(): lax.all_to_all(physics(regime_ops[0], arrived, flux_map), ('wide', 'narro...  6.86 us
  transfers between devices with their start and end apart: 14, of which 4 were waited for; matrix products, arithmetic and copies ran while one was open for 43% of the time, Pallas kernels for 6%

profile of v5, /device:TPU:34, one launch (start us, length us, event | category | flops | bytes accessed | tf_op | source)
XLA Modules:
  0.0 165.4 jit_solution(13200748346809127575)
XLA Ops:
  0.6 2.0 %fusion.131 = (f32[62,1,256]{2,1,0:T(1,128)}, f32[62,1,256]{2,1,0:T(1,128)}) fusion(f32[62,32,256]{2,1,0:T(8,128)} %param.19), kind=kLoop, calls=%fused_computation.216 | loop fusion | bytes 253952 | tf_op jit(solution)/shard_map/slice | solution.py:44
  2.7 1.9 %collective-permute-start.5 = (f32[62,1,256]{2,1,0:T(1,128)}, f32[62,1,256]{2,1,0:T(1,128)}, u32[]{:S(2)}, u32[]{:S(2)}) collective-permute-start(f32[62,1,256]{2,1,0:T(1,128)} %get-tuple-element.36), channel_id=1, source_target_pairs={{0,4},{4,8},{8,12},{12,16},{16,20},{20,24},{24,28},{28,32},{32,36}... | collective-permute-start | bytes 190472 | tf_op jit(solution)/shard_map/ppermute | solution.py:44
  9.5 3.6 %collective-permute-start = (f32[12,4,256]{2,1,0:T(4,128)}, f32[12,4,256]{2,1,0:T(4,128)S(1)}, u32[]{:S(2)}, u32[]{:S(2)}) collective-permute-start(f32[12,4,256]{2,1,0:T(4,128)} %get-tuple-element.44), channel_id=1, source_target_pairs={{0,4},{4,8},{8,12},{12,16},{16,20},{20,24},{24,28},{28,32},{32,36}... | collective-permute-start | bytes 147464 | tf_op jit(solution)/shard_map/ppermute | solution.py:31
  13.0 4.1 %collective-permute-start.1 = (f32[12,4,256]{2,1,0:T(4,128)}, f32[12,4,256]{2,1,0:T(4,128)S(1)}, u32[]{:S(2)}, u32[]{:S(2)}) collective-permute-start(f32[12,4,256]{2,1,0:T(4,128)} %get-tuple-element.45), channel_id=1, source_target_pairs={{4,0},{8,4},{12,8},{16,12},{20,16},{24,20},{28,24},{32,28},{36,32}... | collective-permute-start | bytes 147464 | tf_op jit(solution)/shard_map/ppermute | solution.py:32
  28.3 2.4 %copy.21 = bf16[4096,144]{1,0:T(8,128)(2,1)} copy(bf16[4096,144]{0,1:T(8,128)(2,1)S(1)} %fusion.80) | data formatting | bytes 2359296 | tf_op jit(solution)/shard_map/concatenate | solution.py:73
  30.7 8.6 %all-to-all-start = ((bf16[128,32,144]{2,1,0:T(8,128)(2,1)}), bf16[128,32,144]{2,1,0:T(8,128)(2,1)}, u32[]{:S(2)}, u32[]{:S(2)}) async-start(bf16[128,32,144]{2,1,0:T(8,128)(2,1)} %bitcast.143), calls=%async_computation | async-start | bytes 4194304 | tf_op jit(solution)/shard_map/all_to_all | solution.py:290
  40.6 2.4 %copy.27 = f32[62,32,1]{0,1,2:T(8,128)} copy(f32[62,32,1]{2,1,0:T(8,128)} %get-tuple-element.33) | data formatting | bytes 15872
  43.0 2.4 %collective-permute-start.6 = (f32[62,32]{0,1:T(8,128)}, f32[62,32]{0,1:T(8,128)}, u32[]{:S(2)}, u32[]{:S(2)}) collective-permute-start(f32[62,32]{0,1:T(8,128)} %bitcast.161), channel_id=1, source_target_pairs={{1,0},{2,1},{3,2},{5,4},{6,5},{7,6},{9,8},{10,9},{11,10},{13,12},{... | collective-permute-start | bytes 23816 | tf_op jit(solution)/shard_map/ppermute | solution.py:47
  46.7 3.6 %collective-permute-start.7 = (f32[62,32]{0,1:T(8,128)}, f32[62,32]{0,1:T(8,128)S(1)}, u32[]{:S(2)}, u32[]{:S(2)}) collective-permute-start(f32[62,32]{0,1:T(8,128)} %bitcast.163), channel_id=1, source_target_pairs={{0,1},{1,2},{2,3},{4,5},{5,6},{6,7},{8,9},{9,10},{10,11},{12,13},{... | collective-permute-start | bytes 23816 | tf_op jit(solution)/shard_map/ppermute | solution.py:46
  55.9 2.8 %fusion.130 = (f32[62,32,255]{2,1,0:T(8,128)}, f32[62,32,255]{2,1,0:T(8,128)}) fusion(f32[62,32,256]{2,1,0:T(8,128)S(1)} %copy-done), kind=kLoop, calls=%fused_computation.215 | loop fusion | bytes 8094720 | tf_op jit(solution)/shard_map/slice | solution.py:202
  58.7 9.2 %all-to-all-done = bf16[128,32,144]{2,1,0:T(8,128)(2,1)} async-done(((bf16[128,32,144]{2,1,0:T(8,128)(2,1)}), bf16[128,32,144]{2,1,0:T(8,128)(2,1)}, u32[]{:S(2)}, u32[]{:S(2)}) %all-to-all-start) | async-done | bytes 1179680 | tf_op jit(solution)/shard_map/all_to_all | solution.py:290
  67.8 6.1 %shard_map.129 = bf16[4096,148]{1,0:T(8,128)(2,1)} custom-call(bf16[4096,144]{1,0:T(8,128)(2,1)} %bitcast.6.x_ref, bf16[4,144,144]{2,1,0:T(8,128)(2,1)} %bitcast.152, bf16[144,4]{1,0:T(8,128)(2,1)} %copy.22.fm_ref), custom_call_target="tpu_custom_call" | custom-call | flops 684195840 | bytes 2557952 | tf_op jit(solution)/shard_map/pallas_call | solution.py:97
  73.9 6.9 %all-to-all-start.1 = ((bf16[128,32,148]{2,1,0:T(8,128)(2,1)}), bf16[128,32,148]{2,1,0:T(8,128)(2,1)}, u32[]{:S(2)}, u32[]{:S(2)}) async-start(bf16[128,32,148]{2,1,0:T(8,128)(2,1)} %bitcast.142), calls=%async_computation.1 | async-start | bytes 4194304 | tf_op jit(solution)/shard_map/all_to_all | solution.py:291
  81.4 2.5 %fusion.132 = (f32[62,31,256]{2,1,0:T(8,128)}, f32[62,31,256]{2,1,0:T(8,128)}) fusion(f32[62,32,256]{2,1,0:T(8,128)S(1)} %copy-done), kind=kLoop, calls=%fused_computation.217 | loop fusion | bytes 7872512 | tf_op jit(solution)/shard_map/slice | solution.py:200
  85.4 3.4 %collective-permute-start.2 = (f32[12,40,4]{2,1,0:T(8,128)}, f32[12,40,4]{2,1,0:T(8,128)}, u32[]{:S(2)}, u32[]{:S(2)}) collective-permute-start(f32[12,40,4]{2,1,0:T(8,128)} %get-tuple-element.42), channel_id=1, source_target_pairs={{0,1},{1,2},{2,3},{4,5},{5,6},{6,7},{8,9},{9,10},{10,11},{12,13},{... | collective-permute-start | bytes 23048 | tf_op jit(solution)/shard_map/ppermute | solution.py:34
  88.8 3.1 %collective-permute-start.3 = (f32[12,40,4]{2,1,0:T(8,128)}, f32[12,40,4]{2,1,0:T(8,128)}, u32[]{:S(2)}, u32[]{:S(2)}) collective-permute-start(f32[12,40,4]{2,1,0:T(8,128)} %get-tuple-element.43), channel_id=1, source_target_pairs={{1,0},{2,1},{3,2},{5,4},{6,5},{7,6},{9,8},{10,9},{11,10},{13,12},{... | collective-permute-start | bytes 23048 | tf_op jit(solution)/shard_map/ppermute | solution.py:35
  92.5 3.7 %collective-permute-start.4 = (f32[62,1,256]{2,1,0:T(1,128)}, f32[62,1,256]{2,1,0:T(1,128)}, u32[]{:S(2)}, u32[]{:S(2)}) collective-permute-start(f32[62,1,256]{2,1,0:T(1,128)} %get-tuple-element.37), channel_id=1, source_target_pairs={{4,0},{8,4},{12,8},{16,12},{20,16},{24,20},{28,24},{32,28},{36,32}... | collective-permute-start | bytes 190472 | tf_op jit(solution)/shard_map/ppermute | solution.py:45
  96.2 1.7 %copy.26 = f32[62,32,1]{2,1,0:T(8,128)S(1)} copy(f32[62,32,1]{0,1,2:T(8,128)} %bitcast.162) | data formatting | bytes 15872 | tf_op jit(solution)/shard_map/broadcast_in_dim | solution.py:48
  97.9 2.5 %copy.24 = f32[62,32,1]{2,1,0:T(8,128)} copy(f32[62,32,1]{0,1,2:T(8,128)} %bitcast.19) | data formatting | bytes 15872 | tf_op jit(solution)/shard_map/broadcast_in_dim | solution.py:48
  100.4 8.6 %collective-permute-done.2 = f32[12,40,4]{2,1,0:T(8,128)} collective-permute-done((f32[12,40,4]{2,1,0:T(8,128)}, f32[12,40,4]{2,1,0:T(8,128)}, u32[]{:S(2)}, u32[]{:S(2)}) %collective-permute-start.2) | collective-permute-done | bytes 7712 | tf_op jit(solution)/shard_map/ppermute | solution.py:34
  109.9 2.4 %pad_maximum_fusion = f32[12,40,264]{2,1,0:T(8,128)} fusion(f32[12,40,4]{2,1,0:T(8,128)} %collective-permute-done.3, f32[12,4,256]{2,1,0:T(4,128)S(1)} %collective-permute-done.1, f32[12,32,256]{2,1,0:T(8,128)S(1)} %constant_dynamic-update-slice_fusion, f32[12,4,256]{2,1,0:T(4,128)S(1)} %collective-permute-done, f32[12,40,4]{2,1,0:T(8,128)} %collective-permute-done.2), kind=kLoop, calls=%fused_computation.72 | loop fusion | flops 506880 | bytes 1013760 | tf_op jit(solution)/shard_map/concatenate | solution.py:36
  112.3 10.3 %gather_fusion = bf16[2048,148]{1,0:T(8,128)(2,1)} fusion(bf16[4096,148]{1,0:T(8,128)(2,1)} %bitcast.9, s32[2048]{0:T(1024)S(1)} %broadcast_clamp_fusion), kind=kCustom, calls=%fused_computation | custom fusion | bytes 1220608 | tf_op jit(solution)/shard_map/jit(_take)/gather | solution.py:298
  122.6 4.1 %shard_map.130 = (f32[144,2048]{1,0:T(8,128)}, bf16[4,2048]{1,0:T(4,128)(2,1)}) custom-call(bf16[2048,148]{1,0:T(8,128)(2,1)} %gather_fusion, f32[144,2048]{1,0:T(8,128)} %atm_ref.1, bf16[148,148]{1,0:T(8,128)(2,1)} %fusion.101.eye_ref), custom_call_target="tpu_custom_call" | custom-call | flops 89718784 | bytes 3571712 | tf_op jit(solution)/shard_map/pallas_call | solution.py:129
  127.5 1.9 %collective-permute-start.8 = (bf16[4,3,128]{2,1,0:T(4,128)(2,1)S(1)}, bf16[4,3,128]{2,1,0:T(4,128)(2,1)S(1)}, u32[]{:S(2)}, u32[]{:S(2)}) collective-permute-start(bf16[4,3,128]{2,1,0:T(4,128)(2,1)S(1)} %get-tuple-element.71), channel_id=1, source_target_pairs={{0,4},{4,8},{8,12},{12,16},{16,20},{20,24},{24,28},{28,32},{32,36}... | collective-permute-start | bytes 9224 | tf_op jit(solution)/shard_map/ppermute | solution.py:31
  129.4 5.8 %collective-permute-start.9 = (bf16[4,3,128]{2,1,0:T(4,128)(2,1)S(1)}, bf16[4,3,128]{2,1,0:T(4,128)(2,1)S(1)}, u32[]{:S(2)}, u32[]{:S(2)}) collective-permute-start(bf16[4,3,128]{2,1,0:T(4,128)(2,1)S(1)} %get-tuple-element.72), channel_id=1, source_target_pairs={{4,0},{8,4},{12,8},{16,12},{20,16},{24,20},{28,24},{32,28},{36,32}... | collective-permute-start | bytes 9224 | tf_op jit(solution)/shard_map/ppermute | solution.py:32
  135.1 2.2 %select_reduce_fusion.8 = (f32[40,264]{1,0:T(8,128)}, f32[40,264]{1,0:T(8,128)}, f32[40,264]{1,0:T(8,128)}, f32[40,264]{1,0:T(8,128)}, f32[40,264]{1,0:T(8,128)}...) fusion(f32[12,40,264]{2,1,0:T(8,128)} %pad_maximum_fusion), kind=kLoop, calls=%fused_computation.107 | loop fusion | flops 1087680 | bytes 718080 | tf_op jit(solution)/shard_map/reduce_sum | solution.py:192
  137.5 3.1 %collective-permute-start.10 = (bf16[4,22,3]{2,1,0:T(8,128)(2,1)S(1)}, bf16[4,22,3]{2,1,0:T(8,128)(2,1)S(1)}, u32[]{:S(2)}, u32[]{:S(2)}) collective-permute-start(bf16[4,22,3]{2,1,0:T(8,128)(2,1)S(1)} %get-tuple-element.69), channel_id=1, source_target_pairs={{0,1},{1,2},{2,3},{4,5},{5,6},{6,7},{8,9},{9,10},{10,11},{12,13},{... | collective-permute-start | bytes 1592 | tf_op jit(solution)/shard_map/ppermute | solution.py:34
  140.5 2.7 %collective-permute-start.11 = (bf16[4,22,3]{2,1,0:T(8,128)(2,1)S(1)}, bf16[4,22,3]{2,1,0:T(8,128)(2,1)S(1)}, u32[]{:S(2)}, u32[]{:S(2)}) collective-permute-start(bf16[4,22,3]{2,1,0:T(8,128)(2,1)S(1)} %get-tuple-element.70), channel_id=1, source_target_pairs={{1,0},{2,1},{3,2},{5,4},{6,5},{7,6},{9,8},{10,9},{11,10},{13,12},{... | collective-permute-start | bytes 1592 | tf_op jit(solution)/shard_map/ppermute | solution.py:35
  143.3 1.5 maximum_bitcast_fusion.2
  148.4 1.9 %convolution_convert_fusion = bf16[88,792]{1,0:T(8,128)(2,1)} fusion(bf16[88,134]{1,0:T(8,128)(2,1)} %reshape.208, pred[134,264]{1,0:T(8,128)(4,1)} %iota_compare_fusion.9, pred[134,264]{1,0:T(8,128)(4,1)} %iota_compare_fusion.10, pred[134,264]{1,0:T(8,128)(4,1)} %iota_compare_fusion.11), kind=kOutput, calls=%fused_computation.48 | convolution fusion | flops 18960480 | bytes 269104 | tf_op jit(solution)/shard_map/dot_general | solution.py:178
  150.3 1.6 reshape.209
  161.4 2.7 %fusion.35 = f32[62,32,256]{2,1,0:T(8,128)S(1)} fusion(f32[62,32,256]{2,1,0:T(8,128)S(1)} %copy-done, f32[62,1,256]{2,1,0:T(1,128)} %collective-permute-done.4, f32[62,31,256]{2,1,0:T(8,128)S(1)} %copy-done.4, f32[62,31,256]{2,1,0:T(8,128)S(1)} %copy-done.3, f32[62,1,256]{2,1,0:T(1,128)} %collective-permute-done.5, f32[62,32,1]{2,1,0:T(8,128)S(1)} %copy-done.6, ...), kind=kLoop, calls=%fused_computation.38 | loop fusion | flops 8634368 | bytes 12320768 | tf_op jit(solution)/shard_map/add | solution.py:210
  (152 shorter events, 42.4 us)
Async XLA Ops:
  0.6 17.4 %copy-start.5 = (f32[144,2048]{1,0:T(8,128)S(1)}, f32[144,2048]{1,0:T(8,128)}, u32[]{:S(2)}) copy-start(f32[144,2048]{1,0:T(8,128)} %atm_ref.1) | copy-start | bytes 3538948
  2.7 158.5 %collective-permute-start.5 = (f32[62,1,256]{2,1,0:T(1,128)}, f32[62,1,256]{2,1,0:T(1,128)}, u32[]{:S(2)}, u32[]{:S(2)}) collective-permute-start(f32[62,1,256]{2,1,0:T(1,128)} %get-tuple-element.36), channel_id=1, source_target_pairs={{0,4},{4,8},{8,12},{12,16},{16,20},{20,24},{24,28},{28,32},{32,36}... | collective-permute-start | bytes 190472 | tf_op jit(solution)/shard_map/ppermute | solution.py:44
  9.5 75.0 %collective-permute-start = (f32[12,4,256]{2,1,0:T(4,128)}, f32[12,4,256]{2,1,0:T(4,128)S(1)}, u32[]{:S(2)}, u32[]{:S(2)}) collective-permute-start(f32[12,4,256]{2,1,0:T(4,128)} %get-tuple-element.44), channel_id=1, source_target_pairs={{0,4},{4,8},{8,12},{12,16},{16,20},{20,24},{24,28},{28,32},{32,36}... | collective-permute-start | bytes 147464 | tf_op jit(solution)/shard_map/ppermute | solution.py:31
  13.0 71.4 %collective-permute-start.1 = (f32[12,4,256]{2,1,0:T(4,128)}, f32[12,4,256]{2,1,0:T(4,128)S(1)}, u32[]{:S(2)}, u32[]{:S(2)}) collective-permute-start(f32[12,4,256]{2,1,0:T(4,128)} %get-tuple-element.45), channel_id=1, source_target_pairs={{4,0},{8,4},{12,8},{16,12},{20,16},{24,20},{28,24},{32,28},{36,32}... | collective-permute-start | bytes 147464 | tf_op jit(solution)/shard_map/ppermute | solution.py:32
  30.7 8.6 %copy-start = (f32[62,32,256]{2,1,0:T(8,128)S(1)}, f32[62,32,256]{2,1,0:T(8,128)}, u32[]{:S(2)}) copy-start(f32[62,32,256]{2,1,0:T(8,128)} %param.19) | copy-start | bytes 6094852
  30.7 37.1 %all-to-all-start = ((bf16[128,32,144]{2,1,0:T(8,128)(2,1)}), bf16[128,32,144]{2,1,0:T(8,128)(2,1)}, u32[]{:S(2)}, u32[]{:S(2)}) async-start(bf16[128,32,144]{2,1,0:T(8,128)(2,1)} %bitcast.143), calls=%async_computation | async-start | bytes 4194304 | tf_op jit(solution)/shard_map/all_to_all | solution.py:290
  40.6 9.8 %copy-start.28 = (bf16[144,4]{0,1:T(4,128)(2,1)S(1)}, bf16[144,4]{0,1:T(4,128)(2,1)}, u32[]{:S(2)}) copy-start(bf16[144,4]{0,1:T(4,128)(2,1)} %param.15) | copy-start | bytes 3460
  43.0 54.8 %collective-permute-start.6 = (f32[62,32]{0,1:T(8,128)}, f32[62,32]{0,1:T(8,128)}, u32[]{:S(2)}, u32[]{:S(2)}) collective-permute-start(f32[62,32]{0,1:T(8,128)} %bitcast.161), channel_id=1, source_target_pairs={{1,0},{2,1},{3,2},{5,4},{6,5},{7,6},{9,8},{10,9},{11,10},{13,12},{... | collective-permute-start | bytes 23816 | tf_op jit(solution)/shard_map/ppermute | solution.py:47
  46.7 45.7 %collective-permute-start.7 = (f32[62,32]{0,1:T(8,128)}, f32[62,32]{0,1:T(8,128)S(1)}, u32[]{:S(2)}, u32[]{:S(2)}) collective-permute-start(f32[62,32]{0,1:T(8,128)} %bitcast.163), channel_id=1, source_target_pairs={{0,1},{1,2},{2,3},{4,5},{5,6},{6,7},{8,9},{9,10},{10,11},{12,13},{... | collective-permute-start | bytes 23816 | tf_op jit(solution)/shard_map/ppermute | solution.py:46
  73.9 38.4 %all-to-all-start.1 = ((bf16[128,32,148]{2,1,0:T(8,128)(2,1)}), bf16[128,32,148]{2,1,0:T(8,128)(2,1)}, u32[]{:S(2)}, u32[]{:S(2)}) async-start(bf16[128,32,148]{2,1,0:T(8,128)(2,1)} %bitcast.142), calls=%async_computation.1 | async-start | bytes 4194304 | tf_op jit(solution)/shard_map/all_to_all | solution.py:291
  84.5 27.8 %copy-start.8 = (f32[12,4,256]{2,1,0:T(4,128)}, f32[12,4,256]{2,1,0:T(4,128)S(1)}, u32[]{:S(2)}) copy-start(f32[12,4,256]{2,1,0:T(4,128)S(1)} %collective-permute-done.1) | copy-start | bytes 147460
  85.4 23.6 %collective-permute-start.2 = (f32[12,40,4]{2,1,0:T(8,128)}, f32[12,40,4]{2,1,0:T(8,128)}, u32[]{:S(2)}, u32[]{:S(2)}) collective-permute-start(f32[12,40,4]{2,1,0:T(8,128)} %get-tuple-element.42), channel_id=1, source_target_pairs={{0,1},{1,2},{2,3},{4,5},{5,6},{6,7},{8,9},{9,10},{10,11},{12,13},{... | collective-permute-start | bytes 23048 | tf_op jit(solution)/shard_map/ppermute | solution.py:34
  88.8 21.2 %collective-permute-start.3 = (f32[12,40,4]{2,1,0:T(8,128)}, f32[12,40,4]{2,1,0:T(8,128)}, u32[]{:S(2)}, u32[]{:S(2)}) collective-permute-start(f32[12,40,4]{2,1,0:T(8,128)} %get-tuple-element.43), channel_id=1, source_target_pairs={{1,0},{2,1},{3,2},{5,4},{6,5},{7,6},{9,8},{10,9},{11,10},{13,12},{... | collective-permute-start | bytes 23048 | tf_op jit(solution)/shard_map/ppermute | solution.py:35
  92.5 3.7 %copy-start.27 = (f32[62,32]{0,1:T(8,128)}, f32[62,32]{0,1:T(8,128)S(1)}, u32[]{:S(2)}) copy-start(f32[62,32]{0,1:T(8,128)S(1)} %collective-permute-done.7) | copy-start | bytes 23812
  92.5 68.7 %collective-permute-start.4 = (f32[62,1,256]{2,1,0:T(1,128)}, f32[62,1,256]{2,1,0:T(1,128)}, u32[]{:S(2)}, u32[]{:S(2)}) collective-permute-start(f32[62,1,256]{2,1,0:T(1,128)} %get-tuple-element.37), channel_id=1, source_target_pairs={{4,0},{8,4},{12,8},{16,12},{20,16},{24,20},{28,24},{32,28},{36,32}... | collective-permute-start | bytes 190472 | tf_op jit(solution)/shard_map/ppermute | solution.py:45
  127.5 9.9 %collective-permute-start.8 = (bf16[4,3,128]{2,1,0:T(4,128)(2,1)S(1)}, bf16[4,3,128]{2,1,0:T(4,128)(2,1)S(1)}, u32[]{:S(2)}, u32[]{:S(2)}) collective-permute-start(bf16[4,3,128]{2,1,0:T(4,128)(2,1)S(1)} %get-tuple-element.71), channel_id=1, source_target_pairs={{0,4},{4,8},{8,12},{12,16},{16,20},{20,24},{24,28},{28,32},{32,36}... | collective-permute-start | bytes 9224 | tf_op jit(solution)/shard_map/ppermute | solution.py:31
  129.4 8.0 %collective-permute-start.9 = (bf16[4,3,128]{2,1,0:T(4,128)(2,1)S(1)}, bf16[4,3,128]{2,1,0:T(4,128)(2,1)S(1)}, u32[]{:S(2)}, u32[]{:S(2)}) collective-permute-start(bf16[4,3,128]{2,1,0:T(4,128)(2,1)S(1)} %get-tuple-element.72), channel_id=1, source_target_pairs={{4,0},{8,4},{12,8},{16,12},{20,16},{24,20},{28,24},{32,28},{36,32}... | collective-permute-start | bytes 9224 | tf_op jit(solution)/shard_map/ppermute | solution.py:32
  137.5 7.4 %collective-permute-start.10 = (bf16[4,22,3]{2,1,0:T(8,128)(2,1)S(1)}, bf16[4,22,3]{2,1,0:T(8,128)(2,1)S(1)}, u32[]{:S(2)}, u32[]{:S(2)}) collective-permute-start(bf16[4,22,3]{2,1,0:T(8,128)(2,1)S(1)} %get-tuple-element.69), channel_id=1, source_target_pairs={{0,1},{1,2},{2,3},{4,5},{5,6},{6,7},{8,9},{9,10},{10,11},{12,13},{... | collective-permute-start | bytes 1592 | tf_op jit(solution)/shard_map/ppermute | solution.py:34
  140.5 5.7 %collective-permute-start.11 = (bf16[4,22,3]{2,1,0:T(8,128)(2,1)S(1)}, bf16[4,22,3]{2,1,0:T(8,128)(2,1)S(1)}, u32[]{:S(2)}, u32[]{:S(2)}) collective-permute-start(bf16[4,22,3]{2,1,0:T(8,128)(2,1)S(1)} %get-tuple-element.70), channel_id=1, source_target_pairs={{1,0},{2,1},{3,2},{5,4},{6,5},{7,6},{9,8},{10,9},{11,10},{13,12},{... | collective-permute-start | bytes 1592 | tf_op jit(solution)/shard_map/ppermute | solution.py:35
  152.0 3.8 %copy-start.11 = (f32[40,264]{1,0:T(8,128)S(1)}, f32[40,264]{1,0:T(8,128)}, u32[]{:S(2)}) copy-start(f32[40,264]{1,0:T(8,128)} %get-tuple-element.20) | copy-start | bytes 126724
  152.0 3.8 %copy-start.12 = (f32[40,264]{1,0:T(8,128)S(1)}, f32[40,264]{1,0:T(8,128)}, u32[]{:S(2)}) copy-start(f32[40,264]{1,0:T(8,128)} %get-tuple-element.21) | copy-start | bytes 126724
  152.0 3.8 %copy-start.13 = (f32[40,264]{1,0:T(8,128)S(1)}, f32[40,264]{1,0:T(8,128)}, u32[]{:S(2)}) copy-start(f32[40,264]{1,0:T(8,128)} %get-tuple-element.22) | copy-start | bytes 126724
  152.0 3.8 %copy-start.14 = (f32[40,264]{1,0:T(8,128)S(1)}, f32[40,264]{1,0:T(8,128)}, u32[]{:S(2)}) copy-start(f32[40,264]{1,0:T(8,128)} %get-tuple-element.23) | copy-start | bytes 126724
  152.0 3.8 %copy-start.15 = (f32[40,264]{1,0:T(8,128)S(1)}, f32[40,264]{1,0:T(8,128)}, u32[]{:S(2)}) copy-start(f32[40,264]{1,0:T(8,128)} %get-tuple-element.24) | copy-start | bytes 126724
  152.0 3.8 %copy-start.16 = (f32[40,264]{1,0:T(8,128)S(1)}, f32[40,264]{1,0:T(8,128)}, u32[]{:S(2)}) copy-start(f32[40,264]{1,0:T(8,128)} %get-tuple-element.25) | copy-start | bytes 126724
  152.0 3.8 %copy-start.17 = (f32[40,264]{1,0:T(8,128)S(1)}, f32[40,264]{1,0:T(8,128)}, u32[]{:S(2)}) copy-start(f32[40,264]{1,0:T(8,128)} %get-tuple-element.26) | copy-start | bytes 126724
  152.0 3.8 %copy-start.18 = (f32[40,264]{1,0:T(8,128)S(1)}, f32[40,264]{1,0:T(8,128)}, u32[]{:S(2)}) copy-start(f32[40,264]{1,0:T(8,128)} %get-tuple-element.27) | copy-start | bytes 126724
  152.0 3.8 %copy-start.19 = (f32[40,264]{1,0:T(8,128)S(1)}, f32[40,264]{1,0:T(8,128)}, u32[]{:S(2)}) copy-start(f32[40,264]{1,0:T(8,128)} %get-tuple-element.28) | copy-start | bytes 126724
  155.9 5.3 %copy-start.6 = (f32[62,32,1]{2,1,0:T(8,128)S(1)}, f32[62,32,1]{2,1,0:T(8,128)}, u32[]{:S(2)}) copy-start(f32[62,32,1]{2,1,0:T(8,128)} %copy.24) | copy-start | bytes 23812
  156.4 4.8 %copy-start.4 = (f32[62,31,256]{2,1,0:T(8,128)S(1)}, f32[62,31,256]{2,1,0:T(8,128)}, u32[]{:S(2)}) copy-start(f32[62,31,256]{2,1,0:T(8,128)} %get-tuple-element.39) | copy-start | bytes 5904388
  157.8 3.4 %copy-start.3 = (f32[62,31,256]{2,1,0:T(8,128)S(1)}, f32[62,31,256]{2,1,0:T(8,128)}, u32[]{:S(2)}) copy-start(f32[62,31,256]{2,1,0:T(8,128)} %get-tuple-element.38) | copy-start | bytes 5904388
  159.1 2.3 %copy-start.2 = (f32[62,32,255]{2,1,0:T(8,128)S(1)}, f32[62,32,255]{2,1,0:T(8,128)}, u32[]{:S(2)}) copy-start(f32[62,32,255]{2,1,0:T(8,128)} %get-tuple-element.35) | copy-start | bytes 6071044
  (11 other events, 15.4 us)

commit v6 on v5

--- a/solution.py
+++ b/solution.py
@@ -263,13 +263,7 @@
 
     mask = ocean_mask.astype(jnp.float32)
     planes = jnp.concatenate(
-        [
-            mask[None],
-            surface_height[None],
-            transports,
-            remap_src.astype(jnp.float32),
-            remap_weight,
-        ],
+        [mask[None], surface_height[None], transports, remap_src.astype(jnp.float32), remap_weight],
         axis=0,
     )
     planes_ext = with_halo(planes, h)

time: 167 us -> 167 us (level)
  no operation moved by 1% of the time
where the time goes in v6:
time: 167 us; the launch traced here: 165 us
  starting transfers between devices  54.7 us (33%)
  local copies, waits for them, and re-layouts  43.3 us (26%)
  other arithmetic  22.2 us (13%)
  waiting for transfers between devices  20.2 us (12%)
  matrix products  13.5 us (8%)
  Pallas kernels  10.2 us (6%)
    gather x1, local copies, waits for them, and re-layouts, per_device(): returned = jnp.take(back, slots, axis=0, mode='clip')  10.3 us
    ppermute x2, starting transfers between devices, with_halo(): lax.ppermute(cells[..., :width, :], 'wide', shift_pairs(wide_count, -1))  9.84 us
    unnamed x64, local copies, waits for them, and re-layouts  9.17 us
    all_to_all x1, waiting for transfers between devices, per_device(): lax.all_to_all(outgoing, ('wide', 'narrow'), split_axis=0, concat_axis=0,...  9.15 us
    ppermute x2, waiting for transfers between devices, with_halo(): lax.ppermute(cells[..., cols - width:], 'narrow', shift_pairs(narrow_coun...  8.65 us
    all_to_all x1, starting transfers between devices, per_device(): lax.all_to_all(outgoing, ('wide', 'narrow'), split_axis=0, concat_axis=0,...  8.56 us
    dot_general x8, matrix products, place_columns(): lax.dot_general(selector, source, (((1,), (1,)), ((), ())), preferred_ele...  7.84 us
    all_to_all x1, starting transfers between devices, per_device(): lax.all_to_all(physics(regime_ops[0], arrived, flux_map), ('wide', 'narro...  6.86 us
  transfers between devices with their start and end apart: 14, of which 4 were waited for; matrix products, arithmetic and copies ran while one was open for 43% of the time, Pallas kernels for 6%

profile of v6, /device:TPU:34, one launch (start us, length us, event | category | flops | bytes accessed | tf_op | source)
XLA Modules:
  0.0 165.4 jit_solution(13200748346809127575)
XLA Ops:
  0.6 2.0 %fusion.131 = (f32[62,1,256]{2,1,0:T(1,128)}, f32[62,1,256]{2,1,0:T(1,128)}) fusion(f32[62,32,256]{2,1,0:T(8,128)} %param.19), kind=kLoop, calls=%fused_computation.216 | loop fusion | bytes 253952 | tf_op jit(solution)/shard_map/slice | solution.py:44
  2.7 1.9 %collective-permute-start.5 = (f32[62,1,256]{2,1,0:T(1,128)}, f32[62,1,256]{2,1,0:T(1,128)}, u32[]{:S(2)}, u32[]{:S(2)}) collective-permute-start(f32[62,1,256]{2,1,0:T(1,128)} %get-tuple-element.36), channel_id=1, source_target_pairs={{0,4},{4,8},{8,12},{12,16},{16,20},{20,24},{24,28},{28,32},{32,36}... | collective-permute-start | bytes 190472 | tf_op jit(solution)/shard_map/ppermute | solution.py:44
  9.5 3.6 %collective-permute-start = (f32[12,4,256]{2,1,0:T(4,128)}, f32[12,4,256]{2,1,0:T(4,128)S(1)}, u32[]{:S(2)}, u32[]{:S(2)}) collective-permute-start(f32[12,4,256]{2,1,0:T(4,128)} %get-tuple-element.44), channel_id=1, source_target_pairs={{0,4},{4,8},{8,12},{12,16},{16,20},{20,24},{24,28},{28,32},{32,36}... | collective-permute-start | bytes 147464 | tf_op jit(solution)/shard_map/ppermute | solution.py:31
  13.0 4.1 %collective-permute-start.1 = (f32[12,4,256]{2,1,0:T(4,128)}, f32[12,4,256]{2,1,0:T(4,128)S(1)}, u32[]{:S(2)}, u32[]{:S(2)}) collective-permute-start(f32[12,4,256]{2,1,0:T(4,128)} %get-tuple-element.45), channel_id=1, source_target_pairs={{4,0},{8,4},{12,8},{16,12},{20,16},{24,20},{28,24},{32,28},{36,32}... | collective-permute-start | bytes 147464 | tf_op jit(solution)/shard_map/ppermute | solution.py:32
  28.3 2.4 %copy.21 = bf16[4096,144]{1,0:T(8,128)(2,1)} copy(bf16[4096,144]{0,1:T(8,128)(2,1)S(1)} %fusion.80) | data formatting | bytes 2359296 | tf_op jit(solution)/shard_map/concatenate | solution.py:73
  30.7 8.6 %all-to-all-start = ((bf16[128,32,144]{2,1,0:T(8,128)(2,1)}), bf16[128,32,144]{2,1,0:T(8,128)(2,1)}, u32[]{:S(2)}, u32[]{:S(2)}) async-start(bf16[128,32,144]{2,1,0:T(8,128)(2,1)} %bitcast.143), calls=%async_computation | async-start | bytes 4194304 | tf_op jit(solution)/shard_map/all_to_all | solution.py:284
  40.6 2.4 %copy.27 = f32[62,32,1]{0,1,2:T(8,128)} copy(f32[62,32,1]{2,1,0:T(8,128)} %get-tuple-element.33) | data formatting | bytes 15872
  43.0 2.4 %collective-permute-start.6 = (f32[62,32]{0,1:T(8,128)}, f32[62,32]{0,1:T(8,128)}, u32[]{:S(2)}, u32[]{:S(2)}) collective-permute-start(f32[62,32]{0,1:T(8,128)} %bitcast.161), channel_id=1, source_target_pairs={{1,0},{2,1},{3,2},{5,4},{6,5},{7,6},{9,8},{10,9},{11,10},{13,12},{... | collective-permute-start | bytes 23816 | tf_op jit(solution)/shard_map/ppermute | solution.py:47
  46.7 3.6 %collective-permute-start.7 = (f32[62,32]{0,1:T(8,128)}, f32[62,32]{0,1:T(8,128)S(1)}, u32[]{:S(2)}, u32[]{:S(2)}) collective-permute-start(f32[62,32]{0,1:T(8,128)} %bitcast.163), channel_id=1, source_target_pairs={{0,1},{1,2},{2,3},{4,5},{5,6},{6,7},{8,9},{9,10},{10,11},{12,13},{... | collective-permute-start | bytes 23816 | tf_op jit(solution)/shard_map/ppermute | solution.py:46
  55.9 2.8 %fusion.130 = (f32[62,32,255]{2,1,0:T(8,128)}, f32[62,32,255]{2,1,0:T(8,128)}) fusion(f32[62,32,256]{2,1,0:T(8,128)S(1)} %copy-done), kind=kLoop, calls=%fused_computation.215 | loop fusion | bytes 8094720 | tf_op jit(solution)/shard_map/slice | solution.py:202
  58.7 9.2 %all-to-all-done = bf16[128,32,144]{2,1,0:T(8,128)(2,1)} async-done(((bf16[128,32,144]{2,1,0:T(8,128)(2,1)}), bf16[128,32,144]{2,1,0:T(8,128)(2,1)}, u32[]{:S(2)}, u32[]{:S(2)}) %all-to-all-start) | async-done | bytes 1179680 | tf_op jit(solution)/shard_map/all_to_all | solution.py:284
  67.8 6.1 %shard_map.129 = bf16[4096,148]{1,0:T(8,128)(2,1)} custom-call(bf16[4096,144]{1,0:T(8,128)(2,1)} %bitcast.6.x_ref, bf16[4,144,144]{2,1,0:T(8,128)(2,1)} %bitcast.152, bf16[144,4]{1,0:T(8,128)(2,1)} %copy.22.fm_ref), custom_call_target="tpu_custom_call" | custom-call | flops 684195840 | bytes 2557952 | tf_op jit(solution)/shard_map/pallas_call | solution.py:97
  73.9 6.9 %all-to-all-start.1 = ((bf16[128,32,148]{2,1,0:T(8,128)(2,1)}), bf16[128,32,148]{2,1,0:T(8,128)(2,1)}, u32[]{:S(2)}, u32[]{:S(2)}) async-start(bf16[128,32,148]{2,1,0:T(8,128)(2,1)} %bitcast.142), calls=%async_computation.1 | async-start | bytes 4194304 | tf_op jit(solution)/shard_map/all_to_all | solution.py:285
  81.4 2.5 %fusion.132 = (f32[62,31,256]{2,1,0:T(8,128)}, f32[62,31,256]{2,1,0:T(8,128)}) fusion(f32[62,32,256]{2,1,0:T(8,128)S(1)} %copy-done), kind=kLoop, calls=%fused_computation.217 | loop fusion | bytes 7872512 | tf_op jit(solution)/shard_map/slice | solution.py:200
  85.4 3.4 %collective-permute-start.2 = (f32[12,40,4]{2,1,0:T(8,128)}, f32[12,40,4]{2,1,0:T(8,128)}, u32[]{:S(2)}, u32[]{:S(2)}) collective-permute-start(f32[12,40,4]{2,1,0:T(8,128)} %get-tuple-element.42), channel_id=1, source_target_pairs={{0,1},{1,2},{2,3},{4,5},{5,6},{6,7},{8,9},{9,10},{10,11},{12,13},{... | collective-permute-start | bytes 23048 | tf_op jit(solution)/shard_map/ppermute | solution.py:34
  88.8 3.1 %collective-permute-start.3 = (f32[12,40,4]{2,1,0:T(8,128)}, f32[12,40,4]{2,1,0:T(8,128)}, u32[]{:S(2)}, u32[]{:S(2)}) collective-permute-start(f32[12,40,4]{2,1,0:T(8,128)} %get-tuple-element.43), channel_id=1, source_target_pairs={{1,0},{2,1},{3,2},{5,4},{6,5},{7,6},{9,8},{10,9},{11,10},{13,12},{... | collective-permute-start | bytes 23048 | tf_op jit(solution)/shard_map/ppermute | solution.py:35
  92.5 3.7 %collective-permute-start.4 = (f32[62,1,256]{2,1,0:T(1,128)}, f32[62,1,256]{2,1,0:T(1,128)}, u32[]{:S(2)}, u32[]{:S(2)}) collective-permute-start(f32[62,1,256]{2,1,0:T(1,128)} %get-tuple-element.37), channel_id=1, source_target_pairs={{4,0},{8,4},{12,8},{16,12},{20,16},{24,20},{28,24},{32,28},{36,32}... | collective-permute-start | bytes 190472 | tf_op jit(solution)/shard_map/ppermute | solution.py:45
  96.2 1.7 %copy.26 = f32[62,32,1]{2,1,0:T(8,128)S(1)} copy(f32[62,32,1]{0,1,2:T(8,128)} %bitcast.162) | data formatting | bytes 15872 | tf_op jit(solution)/shard_map/broadcast_in_dim | solution.py:48
  97.9 2.5 %copy.24 = f32[62,32,1]{2,1,0:T(8,128)} copy(f32[62,32,1]{0,1,2:T(8,128)} %bitcast.19) | data formatting | bytes 15872 | tf_op jit(solution)/shard_map/broadcast_in_dim | solution.py:48
  100.4 8.6 %collective-permute-done.2 = f32[12,40,4]{2,1,0:T(8,128)} collective-permute-done((f32[12,40,4]{2,1,0:T(8,128)}, f32[12,40,4]{2,1,0:T(8,128)}, u32[]{:S(2)}, u32[]{:S(2)}) %collective-permute-start.2) | collective-permute-done | bytes 7712 | tf_op jit(solution)/shard_map/ppermute | solution.py:34
  109.9 2.4 %pad_maximum_fusion = f32[12,40,264]{2,1,0:T(8,128)} fusion(f32[12,40,4]{2,1,0:T(8,128)} %collective-permute-done.3, f32[12,4,256]{2,1,0:T(4,128)S(1)} %collective-permute-done.1, f32[12,32,256]{2,1,0:T(8,128)S(1)} %constant_dynamic-update-slice_fusion, f32[12,4,256]{2,1,0:T(4,128)S(1)} %collective-permute-done, f32[12,40,4]{2,1,0:T(8,128)} %collective-permute-done.2), kind=kLoop, calls=%fused_computation.72 | loop fusion | flops 506880 | bytes 1013760 | tf_op jit(solution)/shard_map/concatenate | solution.py:36
  112.3 10.3 %gather_fusion = bf16[2048,148]{1,0:T(8,128)(2,1)} fusion(bf16[4096,148]{1,0:T(8,128)(2,1)} %bitcast.9, s32[2048]{0:T(1024)S(1)} %broadcast_clamp_fusion), kind=kCustom, calls=%fused_computation | custom fusion | bytes 1220608 | tf_op jit(solution)/shard_map/jit(_take)/gather | solution.py:292
  122.6 4.1 %shard_map.130 = (f32[144,2048]{1,0:T(8,128)}, bf16[4,2048]{1,0:T(4,128)(2,1)}) custom-call(bf16[2048,148]{1,0:T(8,128)(2,1)} %gather_fusion, f32[144,2048]{1,0:T(8,128)} %atm_ref.1, bf16[148,148]{1,0:T(8,128)(2,1)} %fusion.101.eye_ref), custom_call_target="tpu_custom_call" | custom-call | flops 89718784 | bytes 3571712 | tf_op jit(solution)/shard_map/pallas_call | solution.py:129
  127.5 1.9 %collective-permute-start.8 = (bf16[4,3,128]{2,1,0:T(4,128)(2,1)S(1)}, bf16[4,3,128]{2,1,0:T(4,128)(2,1)S(1)}, u32[]{:S(2)}, u32[]{:S(2)}) collective-permute-start(bf16[4,3,128]{2,1,0:T(4,128)(2,1)S(1)} %get-tuple-element.71), channel_id=1, source_target_pairs={{0,4},{4,8},{8,12},{12,16},{16,20},{20,24},{24,28},{28,32},{32,36}... | collective-permute-start | bytes 9224 | tf_op jit(solution)/shard_map/ppermute | solution.py:31
  129.4 5.8 %collective-permute-start.9 = (bf16[4,3,128]{2,1,0:T(4,128)(2,1)S(1)}, bf16[4,3,128]{2,1,0:T(4,128)(2,1)S(1)}, u32[]{:S(2)}, u32[]{:S(2)}) collective-permute-start(bf16[4,3,128]{2,1,0:T(4,128)(2,1)S(1)} %get-tuple-element.72), channel_id=1, source_target_pairs={{4,0},{8,4},{12,8},{16,12},{20,16},{24,20},{28,24},{32,28},{36,32}... | collective-permute-start | bytes 9224 | tf_op jit(solution)/shard_map/ppermute | solution.py:32
  135.1 2.2 %select_reduce_fusion.8 = (f32[40,264]{1,0:T(8,128)}, f32[40,264]{1,0:T(8,128)}, f32[40,264]{1,0:T(8,128)}, f32[40,264]{1,0:T(8,128)}, f32[40,264]{1,0:T(8,128)}...) fusion(f32[12,40,264]{2,1,0:T(8,128)} %pad_maximum_fusion), kind=kLoop, calls=%fused_computation.107 | loop fusion | flops 1087680 | bytes 718080 | tf_op jit(solution)/shard_map/reduce_sum | solution.py:192
  137.5 3.1 %collective-permute-start.10 = (bf16[4,22,3]{2,1,0:T(8,128)(2,1)S(1)}, bf16[4,22,3]{2,1,0:T(8,128)(2,1)S(1)}, u32[]{:S(2)}, u32[]{:S(2)}) collective-permute-start(bf16[4,22,3]{2,1,0:T(8,128)(2,1)S(1)} %get-tuple-element.69), channel_id=1, source_target_pairs={{0,1},{1,2},{2,3},{4,5},{5,6},{6,7},{8,9},{9,10},{10,11},{12,13},{... | collective-permute-start | bytes 1592 | tf_op jit(solution)/shard_map/ppermute | solution.py:34
  140.5 2.7 %collective-permute-start.11 = (bf16[4,22,3]{2,1,0:T(8,128)(2,1)S(1)}, bf16[4,22,3]{2,1,0:T(8,128)(2,1)S(1)}, u32[]{:S(2)}, u32[]{:S(2)}) collective-permute-start(bf16[4,22,3]{2,1,0:T(8,128)(2,1)S(1)} %get-tuple-element.70), channel_id=1, source_target_pairs={{1,0},{2,1},{3,2},{5,4},{6,5},{7,6},{9,8},{10,9},{11,10},{13,12},{... | collective-permute-start | bytes 1592 | tf_op jit(solution)/shard_map/ppermute | solution.py:35
  143.3 1.5 maximum_bitcast_fusion.2
  148.4 1.9 %convolution_convert_fusion = bf16[88,792]{1,0:T(8,128)(2,1)} fusion(bf16[88,134]{1,0:T(8,128)(2,1)} %reshape.208, pred[134,264]{1,0:T(8,128)(4,1)} %iota_compare_fusion.9, pred[134,264]{1,0:T(8,128)(4,1)} %iota_compare_fusion.10, pred[134,264]{1,0:T(8,128)(4,1)} %iota_compare_fusion.11), kind=kOutput, calls=%fused_computation.48 | convolution fusion | flops 18960480 | bytes 269104 | tf_op jit(solution)/shard_map/dot_general | solution.py:178
  150.3 1.6 reshape.209
  161.4 2.7 %fusion.35 = f32[62,32,256]{2,1,0:T(8,128)S(1)} fusion(f32[62,32,256]{2,1,0:T(8,128)S(1)} %copy-done, f32[62,1,256]{2,1,0:T(1,128)} %collective-permute-done.4, f32[62,31,256]{2,1,0:T(8,128)S(1)} %copy-done.4, f32[62,31,256]{2,1,0:T(8,128)S(1)} %copy-done.3, f32[62,1,256]{2,1,0:T(1,128)} %collective-permute-done.5, f32[62,32,1]{2,1,0:T(8,128)S(1)} %copy-done.6, ...), kind=kLoop, calls=%fused_computation.38 | loop fusion | flops 8634368 | bytes 12320768 | tf_op jit(solution)/shard_map/add | solution.py:210
  (152 shorter events, 42.4 us)
Async XLA Ops:
  0.6 17.4 %copy-start.5 = (f32[144,2048]{1,0:T(8,128)S(1)}, f32[144,2048]{1,0:T(8,128)}, u32[]{:S(2)}) copy-start(f32[144,2048]{1,0:T(8,128)} %atm_ref.1) | copy-start | bytes 3538948
  2.7 158.5 %collective-permute-start.5 = (f32[62,1,256]{2,1,0:T(1,128)}, f32[62,1,256]{2,1,0:T(1,128)}, u32[]{:S(2)}, u32[]{:S(2)}) collective-permute-start(f32[62,1,256]{2,1,0:T(1,128)} %get-tuple-element.36), channel_id=1, source_target_pairs={{0,4},{4,8},{8,12},{12,16},{16,20},{20,24},{24,28},{28,32},{32,36}... | collective-permute-start | bytes 190472 | tf_op jit(solution)/shard_map/ppermute | solution.py:44
  9.5 75.0 %collective-permute-start = (f32[12,4,256]{2,1,0:T(4,128)}, f32[12,4,256]{2,1,0:T(4,128)S(1)}, u32[]{:S(2)}, u32[]{:S(2)}) collective-permute-start(f32[12,4,256]{2,1,0:T(4,128)} %get-tuple-element.44), channel_id=1, source_target_pairs={{0,4},{4,8},{8,12},{12,16},{16,20},{20,24},{24,28},{28,32},{32,36}... | collective-permute-start | bytes 147464 | tf_op jit(solution)/shard_map/ppermute | solution.py:31
  13.0 71.4 %collective-permute-start.1 = (f32[12,4,256]{2,1,0:T(4,128)}, f32[12,4,256]{2,1,0:T(4,128)S(1)}, u32[]{:S(2)}, u32[]{:S(2)}) collective-permute-start(f32[12,4,256]{2,1,0:T(4,128)} %get-tuple-element.45), channel_id=1, source_target_pairs={{4,0},{8,4},{12,8},{16,12},{20,16},{24,20},{28,24},{32,28},{36,32}... | collective-permute-start | bytes 147464 | tf_op jit(solution)/shard_map/ppermute | solution.py:32
  30.7 8.6 %copy-start = (f32[62,32,256]{2,1,0:T(8,128)S(1)}, f32[62,32,256]{2,1,0:T(8,128)}, u32[]{:S(2)}) copy-start(f32[62,32,256]{2,1,0:T(8,128)} %param.19) | copy-start | bytes 6094852
  30.7 37.1 %all-to-all-start = ((bf16[128,32,144]{2,1,0:T(8,128)(2,1)}), bf16[128,32,144]{2,1,0:T(8,128)(2,1)}, u32[]{:S(2)}, u32[]{:S(2)}) async-start(bf16[128,32,144]{2,1,0:T(8,128)(2,1)} %bitcast.143), calls=%async_computation | async-start | bytes 4194304 | tf_op jit(solution)/shard_map/all_to_all | solution.py:284
  40.6 9.8 %copy-start.28 = (bf16[144,4]{0,1:T(4,128)(2,1)S(1)}, bf16[144,4]{0,1:T(4,128)(2,1)}, u32[]{:S(2)}) copy-start(bf16[144,4]{0,1:T(4,128)(2,1)} %param.15) | copy-start | bytes 3460
  43.0 54.8 %collective-permute-start.6 = (f32[62,32]{0,1:T(8,128)}, f32[62,32]{0,1:T(8,128)}, u32[]{:S(2)}, u32[]{:S(2)}) collective-permute-start(f32[62,32]{0,1:T(8,128)} %bitcast.161), channel_id=1, source_target_pairs={{1,0},{2,1},{3,2},{5,4},{6,5},{7,6},{9,8},{10,9},{11,10},{13,12},{... | collective-permute-start | bytes 23816 | tf_op jit(solution)/shard_map/ppermute | solution.py:47
  46.7 45.7 %collective-permute-start.7 = (f32[62,32]{0,1:T(8,128)}, f32[62,32]{0,1:T(8,128)S(1)}, u32[]{:S(2)}, u32[]{:S(2)}) collective-permute-start(f32[62,32]{0,1:T(8,128)} %bitcast.163), channel_id=1, source_target_pairs={{0,1},{1,2},{2,3},{4,5},{5,6},{6,7},{8,9},{9,10},{10,11},{12,13},{... | collective-permute-start | bytes 23816 | tf_op jit(solution)/shard_map/ppermute | solution.py:46
  73.9 38.4 %all-to-all-start.1 = ((bf16[128,32,148]{2,1,0:T(8,128)(2,1)}), bf16[128,32,148]{2,1,0:T(8,128)(2,1)}, u32[]{:S(2)}, u32[]{:S(2)}) async-start(bf16[128,32,148]{2,1,0:T(8,128)(2,1)} %bitcast.142), calls=%async_computation.1 | async-start | bytes 4194304 | tf_op jit(solution)/shard_map/all_to_all | solution.py:285
  84.5 27.8 %copy-start.8 = (f32[12,4,256]{2,1,0:T(4,128)}, f32[12,4,256]{2,1,0:T(4,128)S(1)}, u32[]{:S(2)}) copy-start(f32[12,4,256]{2,1,0:T(4,128)S(1)} %collective-permute-done.1) | copy-start | bytes 147460
  85.4 23.6 %collective-permute-start.2 = (f32[12,40,4]{2,1,0:T(8,128)}, f32[12,40,4]{2,1,0:T(8,128)}, u32[]{:S(2)}, u32[]{:S(2)}) collective-permute-start(f32[12,40,4]{2,1,0:T(8,128)} %get-tuple-element.42), channel_id=1, source_target_pairs={{0,1},{1,2},{2,3},{4,5},{5,6},{6,7},{8,9},{9,10},{10,11},{12,13},{... | collective-permute-start | bytes 23048 | tf_op jit(solution)/shard_map/ppermute | solution.py:34
  88.8 21.2 %collective-permute-start.3 = (f32[12,40,4]{2,1,0:T(8,128)}, f32[12,40,4]{2,1,0:T(8,128)}, u32[]{:S(2)}, u32[]{:S(2)}) collective-permute-start(f32[12,40,4]{2,1,0:T(8,128)} %get-tuple-element.43), channel_id=1, source_target_pairs={{1,0},{2,1},{3,2},{5,4},{6,5},{7,6},{9,8},{10,9},{11,10},{13,12},{... | collective-permute-start | bytes 23048 | tf_op jit(solution)/shard_map/ppermute | solution.py:35
  92.5 3.7 %copy-start.27 = (f32[62,32]{0,1:T(8,128)}, f32[62,32]{0,1:T(8,128)S(1)}, u32[]{:S(2)}) copy-start(f32[62,32]{0,1:T(8,128)S(1)} %collective-permute-done.7) | copy-start | bytes 23812
  92.5 68.7 %collective-permute-start.4 = (f32[62,1,256]{2,1,0:T(1,128)}, f32[62,1,256]{2,1,0:T(1,128)}, u32[]{:S(2)}, u32[]{:S(2)}) collective-permute-start(f32[62,1,256]{2,1,0:T(1,128)} %get-tuple-element.37), channel_id=1, source_target_pairs={{4,0},{8,4},{12,8},{16,12},{20,16},{24,20},{28,24},{32,28},{36,32}... | collective-permute-start | bytes 190472 | tf_op jit(solution)/shard_map/ppermute | solution.py:45
  127.5 9.9 %collective-permute-start.8 = (bf16[4,3,128]{2,1,0:T(4,128)(2,1)S(1)}, bf16[4,3,128]{2,1,0:T(4,128)(2,1)S(1)}, u32[]{:S(2)}, u32[]{:S(2)}) collective-permute-start(bf16[4,3,128]{2,1,0:T(4,128)(2,1)S(1)} %get-tuple-element.71), channel_id=1, source_target_pairs={{0,4},{4,8},{8,12},{12,16},{16,20},{20,24},{24,28},{28,32},{32,36}... | collective-permute-start | bytes 9224 | tf_op jit(solution)/shard_map/ppermute | solution.py:31
  129.4 8.0 %collective-permute-start.9 = (bf16[4,3,128]{2,1,0:T(4,128)(2,1)S(1)}, bf16[4,3,128]{2,1,0:T(4,128)(2,1)S(1)}, u32[]{:S(2)}, u32[]{:S(2)}) collective-permute-start(bf16[4,3,128]{2,1,0:T(4,128)(2,1)S(1)} %get-tuple-element.72), channel_id=1, source_target_pairs={{4,0},{8,4},{12,8},{16,12},{20,16},{24,20},{28,24},{32,28},{36,32}... | collective-permute-start | bytes 9224 | tf_op jit(solution)/shard_map/ppermute | solution.py:32
  137.5 7.4 %collective-permute-start.10 = (bf16[4,22,3]{2,1,0:T(8,128)(2,1)S(1)}, bf16[4,22,3]{2,1,0:T(8,128)(2,1)S(1)}, u32[]{:S(2)}, u32[]{:S(2)}) collective-permute-start(bf16[4,22,3]{2,1,0:T(8,128)(2,1)S(1)} %get-tuple-element.69), channel_id=1, source_target_pairs={{0,1},{1,2},{2,3},{4,5},{5,6},{6,7},{8,9},{9,10},{10,11},{12,13},{... | collective-permute-start | bytes 1592 | tf_op jit(solution)/shard_map/ppermute | solution.py:34
  140.5 5.7 %collective-permute-start.11 = (bf16[4,22,3]{2,1,0:T(8,128)(2,1)S(1)}, bf16[4,22,3]{2,1,0:T(8,128)(2,1)S(1)}, u32[]{:S(2)}, u32[]{:S(2)}) collective-permute-start(bf16[4,22,3]{2,1,0:T(8,128)(2,1)S(1)} %get-tuple-element.70), channel_id=1, source_target_pairs={{1,0},{2,1},{3,2},{5,4},{6,5},{7,6},{9,8},{10,9},{11,10},{13,12},{... | collective-permute-start | bytes 1592 | tf_op jit(solution)/shard_map/ppermute | solution.py:35
  152.0 3.8 %copy-start.11 = (f32[40,264]{1,0:T(8,128)S(1)}, f32[40,264]{1,0:T(8,128)}, u32[]{:S(2)}) copy-start(f32[40,264]{1,0:T(8,128)} %get-tuple-element.20) | copy-start | bytes 126724
  152.0 3.8 %copy-start.12 = (f32[40,264]{1,0:T(8,128)S(1)}, f32[40,264]{1,0:T(8,128)}, u32[]{:S(2)}) copy-start(f32[40,264]{1,0:T(8,128)} %get-tuple-element.21) | copy-start | bytes 126724
  152.0 3.8 %copy-start.13 = (f32[40,264]{1,0:T(8,128)S(1)}, f32[40,264]{1,0:T(8,128)}, u32[]{:S(2)}) copy-start(f32[40,264]{1,0:T(8,128)} %get-tuple-element.22) | copy-start | bytes 126724
  152.0 3.8 %copy-start.14 = (f32[40,264]{1,0:T(8,128)S(1)}, f32[40,264]{1,0:T(8,128)}, u32[]{:S(2)}) copy-start(f32[40,264]{1,0:T(8,128)} %get-tuple-element.23) | copy-start | bytes 126724
  152.0 3.8 %copy-start.15 = (f32[40,264]{1,0:T(8,128)S(1)}, f32[40,264]{1,0:T(8,128)}, u32[]{:S(2)}) copy-start(f32[40,264]{1,0:T(8,128)} %get-tuple-element.24) | copy-start | bytes 126724
  152.0 3.8 %copy-start.16 = (f32[40,264]{1,0:T(8,128)S(1)}, f32[40,264]{1,0:T(8,128)}, u32[]{:S(2)}) copy-start(f32[40,264]{1,0:T(8,128)} %get-tuple-element.25) | copy-start | bytes 126724
  152.0 3.8 %copy-start.17 = (f32[40,264]{1,0:T(8,128)S(1)}, f32[40,264]{1,0:T(8,128)}, u32[]{:S(2)}) copy-start(f32[40,264]{1,0:T(8,128)} %get-tuple-element.26) | copy-start | bytes 126724
  152.0 3.8 %copy-start.18 = (f32[40,264]{1,0:T(8,128)S(1)}, f32[40,264]{1,0:T(8,128)}, u32[]{:S(2)}) copy-start(f32[40,264]{1,0:T(8,128)} %get-tuple-element.27) | copy-start | bytes 126724
  152.0 3.8 %copy-start.19 = (f32[40,264]{1,0:T(8,128)S(1)}, f32[40,264]{1,0:T(8,128)}, u32[]{:S(2)}) copy-start(f32[40,264]{1,0:T(8,128)} %get-tuple-element.28) | copy-start | bytes 126724
  155.9 5.3 %copy-start.6 = (f32[62,32,1]{2,1,0:T(8,128)S(1)}, f32[62,32,1]{2,1,0:T(8,128)}, u32[]{:S(2)}) copy-start(f32[62,32,1]{2,1,0:T(8,128)} %copy.24) | copy-start | bytes 23812
  156.4 4.8 %copy-start.4 = (f32[62,31,256]{2,1,0:T(8,128)S(1)}, f32[62,31,256]{2,1,0:T(8,128)}, u32[]{:S(2)}) copy-start(f32[62,31,256]{2,1,0:T(8,128)} %get-tuple-element.39) | copy-start | bytes 5904388
  157.8 3.4 %copy-start.3 = (f32[62,31,256]{2,1,0:T(8,128)S(1)}, f32[62,31,256]{2,1,0:T(8,128)}, u32[]{:S(2)}) copy-start(f32[62,31,256]{2,1,0:T(8,128)} %get-tuple-element.38) | copy-start | bytes 5904388
  159.1 2.3 %copy-start.2 = (f32[62,32,255]{2,1,0:T(8,128)S(1)}, f32[62,32,255]{2,1,0:T(8,128)}, u32[]{:S(2)}) copy-start(f32[62,32,255]{2,1,0:T(8,128)} %get-tuple-element.35) | copy-start | bytes 6071044
  (11 other events, 15.4 us)

commit v7 on v6

--- a/solution.py
+++ b/solution.py
@@ -175,12 +175,9 @@
         ],
         axis=1,
     )
-    by_cols = jnp.dot(
-        flux_ext.reshape(nflux * flux_ext.shape[1], flux_ext.shape[2]),
-        col_sel,
-        preferred_element_type=jnp.float32,
+    by_cols = jnp.einsum(
+        "fpt,tx->fpx", flux_ext, col_sel, preferred_element_type=jnp.float32
     ).astype(jnp.bfloat16)
-    by_cols = by_cols.reshape(nflux, flux_ext.shape[1], 3 * ext_c)
     ocean_flux = jnp.zeros((nflux, ext_r, ext_c), jnp.float32)
     for dr in (-1, 0, 1):
         row_sel = selector(ext_r, row0, dr, atm_rows, arow0, flux_ext.shape[1])

time: 167 us -> 158 us (0.946)
  matrix products: 13.5 us -> 9.05 us
  other arithmetic: 22.2 us -> 18.8 us
  local copies, waits for them, and re-layouts: 43.3 us -> 40.3 us
    reshape x2 -> x0, local copies, waits for them, and re-layouts: 3.07 us -> none  [the longest x1 1.63 us: remap(): by_cols = by_cols.reshape(nflux, flux_ext.shape[1], 3 * ext_c)]
    dot_general x3, matrix products: 3.71 us -> 0.84 us  [remap(): jnp.einsum('ap,fpx->fax', row_sel, by_cols, preferred_element_type=jnp.fl...]
    unnamed x64 -> x44, local copies, waits for them, and re-layouts: 9.17 us -> 9.25 us
  transfers between devices with their start and end apart: 14 -> 14, of which waited for: 4 -> 4; matrix products, arithmetic and copies ran while one was open for 43% -> 40% of each run, Pallas kernels for 6% -> 7%
where the time goes in v7:
time: 158 us; the launch traced here: 156 us
  starting transfers between devices  54.7 us (35%)
  local copies, waits for them, and re-layouts  40.3 us (26%)
  waiting for transfers between devices  21.4 us (14%)
  other arithmetic  18.8 us (12%)
  Pallas kernels  10.2 us (6%)
  matrix products  9.05 us (6%)
    gather x1, local copies, waits for them, and re-layouts, per_device(): returned = jnp.take(back, slots, axis=0, mode='clip')  10.3 us
    ppermute x2, starting transfers between devices, with_halo(): lax.ppermute(cells[..., :width, :], 'wide', shift_pairs(wide_count, -1))  9.84 us
    unnamed x44, local copies, waits for them, and re-layouts  9.25 us
    all_to_all x1, waiting for transfers between devices, per_device(): lax.all_to_all(outgoing, ('wide', 'narrow'), split_axis=0, concat_axis=0,...  9.22 us
    ppermute x2, waiting for transfers between devices, with_halo(): lax.ppermute(cells[..., cols - width:], 'narrow', shift_pairs(narrow_coun...  9.18 us
    all_to_all x1, starting transfers between devices, per_device(): lax.all_to_all(outgoing, ('wide', 'narrow'), split_axis=0, concat_axis=0,...  8.57 us
    dot_general x8, matrix products, place_columns(): lax.dot_general(selector, source, (((1,), (1,)), ((), ())), preferred_ele...  7.83 us
    all_to_all x1, starting transfers between devices, per_device(): lax.all_to_all(physics(regime_ops[0], arrived, flux_map), ('wide', 'narro...  6.85 us
  transfers between devices with their start and end apart: 14, of which 4 were waited for; matrix products, arithmetic and copies ran while one was open for 40% of the time, Pallas kernels for 7%

profile of v7, /device:TPU:34, one launch (start us, length us, event | category | flops | bytes accessed | tf_op | source)
XLA Modules:
  0.0 155.7 jit_solution(16626590969812107998)
XLA Ops:
  0.6 2.0 %fusion.140 = (f32[62,1,256]{2,1,0:T(1,128)}, f32[62,1,256]{2,1,0:T(1,128)}) fusion(f32[62,32,256]{2,1,0:T(8,128)} %param.19), kind=kLoop, calls=%fused_computation.225 | loop fusion | bytes 253952 | tf_op jit(solution)/shard_map/slice | solution.py:44
  2.7 1.9 %collective-permute-start.5 = (f32[62,1,256]{2,1,0:T(1,128)}, f32[62,1,256]{2,1,0:T(1,128)}, u32[]{:S(2)}, u32[]{:S(2)}) collective-permute-start(f32[62,1,256]{2,1,0:T(1,128)} %get-tuple-element.36), channel_id=1, source_target_pairs={{0,4},{4,8},{8,12},{12,16},{16,20},{20,24},{24,28},{28,32},{32,36}... | collective-permute-start | bytes 190472 | tf_op jit(solution)/shard_map/ppermute | solution.py:44
  9.5 3.6 %collective-permute-start = (f32[12,4,256]{2,1,0:T(4,128)}, f32[12,4,256]{2,1,0:T(4,128)S(1)}, u32[]{:S(2)}, u32[]{:S(2)}) collective-permute-start(f32[12,4,256]{2,1,0:T(4,128)} %get-tuple-element.44), channel_id=1, source_target_pairs={{0,4},{4,8},{8,12},{12,16},{16,20},{20,24},{24,28},{28,32},{32,36}... | collective-permute-start | bytes 147464 | tf_op jit(solution)/shard_map/ppermute | solution.py:31
  13.0 4.1 %collective-permute-start.1 = (f32[12,4,256]{2,1,0:T(4,128)}, f32[12,4,256]{2,1,0:T(4,128)S(1)}, u32[]{:S(2)}, u32[]{:S(2)}) collective-permute-start(f32[12,4,256]{2,1,0:T(4,128)} %get-tuple-element.45), channel_id=1, source_target_pairs={{4,0},{8,4},{12,8},{16,12},{20,16},{24,20},{28,24},{32,28},{36,32}... | collective-permute-start | bytes 147464 | tf_op jit(solution)/shard_map/ppermute | solution.py:32
  27.7 2.4 %copy.21 = bf16[4096,144]{1,0:T(8,128)(2,1)} copy(bf16[4096,144]{0,1:T(8,128)(2,1)S(1)} %fusion.80) | data formatting | bytes 2359296 | tf_op jit(solution)/shard_map/concatenate | solution.py:73
  30.1 8.6 %all-to-all-start = ((bf16[128,32,144]{2,1,0:T(8,128)(2,1)}), bf16[128,32,144]{2,1,0:T(8,128)(2,1)}, u32[]{:S(2)}, u32[]{:S(2)}) async-start(bf16[128,32,144]{2,1,0:T(8,128)(2,1)} %bitcast.145), calls=%async_computation | async-start | bytes 4194304 | tf_op jit(solution)/shard_map/all_to_all | solution.py:281
  38.7 1.3 fusion.138
  40.0 2.4 %copy.27 = f32[62,32,1]{0,1,2:T(8,128)} copy(f32[62,32,1]{2,1,0:T(8,128)} %get-tuple-element.33) | data formatting | bytes 15872
  42.4 2.4 %collective-permute-start.6 = (f32[62,32]{0,1:T(8,128)}, f32[62,32]{0,1:T(8,128)}, u32[]{:S(2)}, u32[]{:S(2)}) collective-permute-start(f32[62,32]{0,1:T(8,128)} %bitcast.163), channel_id=1, source_target_pairs={{1,0},{2,1},{3,2},{5,4},{6,5},{7,6},{9,8},{10,9},{11,10},{13,12},{... | collective-permute-start | bytes 23816 | tf_op jit(solution)/shard_map/ppermute | solution.py:47
  46.1 3.6 %collective-permute-start.7 = (f32[62,32]{0,1:T(8,128)}, f32[62,32]{0,1:T(8,128)S(1)}, u32[]{:S(2)}, u32[]{:S(2)}) collective-permute-start(f32[62,32]{0,1:T(8,128)} %bitcast.165), channel_id=1, source_target_pairs={{0,1},{1,2},{2,3},{4,5},{5,6},{6,7},{8,9},{9,10},{10,11},{12,13},{... | collective-permute-start | bytes 23816 | tf_op jit(solution)/shard_map/ppermute | solution.py:46
  49.8 1.4 copy.22.fm_ref
  55.2 2.8 %fusion.139 = (f32[62,32,255]{2,1,0:T(8,128)}, f32[62,32,255]{2,1,0:T(8,128)}) fusion(f32[62,32,256]{2,1,0:T(8,128)S(1)} %copy-done), kind=kLoop, calls=%fused_computation.224 | loop fusion | bytes 8094720 | tf_op jit(solution)/shard_map/slice | solution.py:199
  58.0 9.2 %all-to-all-done = bf16[128,32,144]{2,1,0:T(8,128)(2,1)} async-done(((bf16[128,32,144]{2,1,0:T(8,128)(2,1)}), bf16[128,32,144]{2,1,0:T(8,128)(2,1)}, u32[]{:S(2)}, u32[]{:S(2)}) %all-to-all-start) | async-done | bytes 1179680 | tf_op jit(solution)/shard_map/all_to_all | solution.py:281
  67.2 6.1 %shard_map.129 = bf16[4096,148]{1,0:T(8,128)(2,1)} custom-call(bf16[4096,144]{1,0:T(8,128)(2,1)} %bitcast.6.x_ref, bf16[4,144,144]{2,1,0:T(8,128)(2,1)} %bitcast.154, bf16[144,4]{1,0:T(8,128)(2,1)} %copy.22.fm_ref), custom_call_target="tpu_custom_call" | custom-call | flops 684195840 | bytes 2557952 | tf_op jit(solution)/shard_map/pallas_call | solution.py:97
  73.3 6.9 %all-to-all-start.1 = ((bf16[128,32,148]{2,1,0:T(8,128)(2,1)}), bf16[128,32,148]{2,1,0:T(8,128)(2,1)}, u32[]{:S(2)}, u32[]{:S(2)}) async-start(bf16[128,32,148]{2,1,0:T(8,128)(2,1)} %bitcast.144), calls=%async_computation.1 | async-start | bytes 4194304 | tf_op jit(solution)/shard_map/all_to_all | solution.py:282
  80.8 2.5 %fusion.141 = (f32[62,31,256]{2,1,0:T(8,128)}, f32[62,31,256]{2,1,0:T(8,128)}) fusion(f32[62,32,256]{2,1,0:T(8,128)S(1)} %copy-done), kind=kLoop, calls=%fused_computation.226 | loop fusion | bytes 7872512 | tf_op jit(solution)/shard_map/slice | solution.py:197
  84.2 3.4 %collective-permute-start.2 = (f32[12,40,4]{2,1,0:T(8,128)}, f32[12,40,4]{2,1,0:T(8,128)}, u32[]{:S(2)}, u32[]{:S(2)}) collective-permute-start(f32[12,40,4]{2,1,0:T(8,128)} %get-tuple-element.42), channel_id=1, source_target_pairs={{0,1},{1,2},{2,3},{4,5},{5,6},{6,7},{8,9},{9,10},{10,11},{12,13},{... | collective-permute-start | bytes 23048 | tf_op jit(solution)/shard_map/ppermute | solution.py:34
  87.6 3.2 %collective-permute-start.3 = (f32[12,40,4]{2,1,0:T(8,128)}, f32[12,40,4]{2,1,0:T(8,128)}, u32[]{:S(2)}, u32[]{:S(2)}) collective-permute-start(f32[12,40,4]{2,1,0:T(8,128)} %get-tuple-element.43), channel_id=1, source_target_pairs={{1,0},{2,1},{3,2},{5,4},{6,5},{7,6},{9,8},{10,9},{11,10},{13,12},{... | collective-permute-start | bytes 23048 | tf_op jit(solution)/shard_map/ppermute | solution.py:35
  91.3 3.7 %collective-permute-start.4 = (f32[62,1,256]{2,1,0:T(1,128)}, f32[62,1,256]{2,1,0:T(1,128)}, u32[]{:S(2)}, u32[]{:S(2)}) collective-permute-start(f32[62,1,256]{2,1,0:T(1,128)} %get-tuple-element.37), channel_id=1, source_target_pairs={{4,0},{8,4},{12,8},{16,12},{20,16},{24,20},{28,24},{32,28},{36,32}... | collective-permute-start | bytes 190472 | tf_op jit(solution)/shard_map/ppermute | solution.py:45
  95.0 1.7 %copy.26 = f32[62,32,1]{2,1,0:T(8,128)S(1)} copy(f32[62,32,1]{0,1,2:T(8,128)} %bitcast.164) | data formatting | bytes 15872 | tf_op jit(solution)/shard_map/broadcast_in_dim | solution.py:48
  96.7 2.5 %copy.24 = f32[62,32,1]{2,1,0:T(8,128)} copy(f32[62,32,1]{0,1,2:T(8,128)} %bitcast.19) | data formatting | bytes 15872 | tf_op jit(solution)/shard_map/broadcast_in_dim | solution.py:48
  99.2 9.2 %collective-permute-done.2 = f32[12,40,4]{2,1,0:T(8,128)} collective-permute-done((f32[12,40,4]{2,1,0:T(8,128)}, f32[12,40,4]{2,1,0:T(8,128)}, u32[]{:S(2)}, u32[]{:S(2)}) %collective-permute-start.2) | collective-permute-done | bytes 7712 | tf_op jit(solution)/shard_map/ppermute | solution.py:34
  109.3 2.3 %pad_maximum_fusion = f32[12,40,264]{2,1,0:T(8,128)} fusion(f32[12,40,4]{2,1,0:T(8,128)} %collective-permute-done.3, f32[12,4,256]{2,1,0:T(4,128)S(1)} %collective-permute-done.1, f32[12,32,256]{2,1,0:T(8,128)S(1)} %constant_dynamic-update-slice_fusion, f32[12,4,256]{2,1,0:T(4,128)S(1)} %collective-permute-done, f32[12,40,4]{2,1,0:T(8,128)} %collective-permute-done.2), kind=kLoop, calls=%fused_computation.72 | loop fusion | flops 506880 | bytes 1013760 | tf_op jit(solution)/shard_map/concatenate | solution.py:36
  111.7 10.3 %gather_fusion = bf16[2048,148]{1,0:T(8,128)(2,1)} fusion(bf16[4096,148]{1,0:T(8,128)(2,1)} %bitcast.9, s32[2048]{0:T(1024)S(1)} %broadcast_clamp_fusion), kind=kCustom, calls=%fused_computation | custom fusion | bytes 1220608 | tf_op jit(solution)/shard_map/jit(_take)/gather | solution.py:289
  122.0 4.1 %shard_map.130 = (f32[144,2048]{1,0:T(8,128)}, bf16[4,2048]{1,0:T(4,128)(2,1)}) custom-call(bf16[2048,148]{1,0:T(8,128)(2,1)} %gather_fusion, f32[144,2048]{1,0:T(8,128)} %atm_ref.1, bf16[148,148]{1,0:T(8,128)(2,1)} %fusion.100.eye_ref), custom_call_target="tpu_custom_call" | custom-call | flops 89718784 | bytes 3571712 | tf_op jit(solution)/shard_map/pallas_call | solution.py:129
  126.9 1.9 %collective-permute-start.8 = (bf16[4,3,128]{2,1,0:T(4,128)(2,1)S(1)}, bf16[4,3,128]{2,1,0:T(4,128)(2,1)S(1)}, u32[]{:S(2)}, u32[]{:S(2)}) collective-permute-start(bf16[4,3,128]{2,1,0:T(4,128)(2,1)S(1)} %get-tuple-element.71), channel_id=1, source_target_pairs={{0,4},{4,8},{8,12},{12,16},{16,20},{20,24},{24,28},{28,32},{32,36}... | collective-permute-start | bytes 9224 | tf_op jit(solution)/shard_map/ppermute | solution.py:31
  128.8 5.8 %collective-permute-start.9 = (bf16[4,3,128]{2,1,0:T(4,128)(2,1)S(1)}, bf16[4,3,128]{2,1,0:T(4,128)(2,1)S(1)}, u32[]{:S(2)}, u32[]{:S(2)}) collective-permute-start(bf16[4,3,128]{2,1,0:T(4,128)(2,1)S(1)} %get-tuple-element.72), channel_id=1, source_target_pairs={{4,0},{8,4},{12,8},{16,12},{20,16},{24,20},{28,24},{32,28},{36,32}... | collective-permute-start | bytes 9224 | tf_op jit(solution)/shard_map/ppermute | solution.py:32
  134.6 1.4 select_reduce_fusion.8
  136.1 3.1 %collective-permute-start.10 = (bf16[4,22,3]{2,1,0:T(8,128)(2,1)S(1)}, bf16[4,22,3]{2,1,0:T(8,128)(2,1)S(1)}, u32[]{:S(2)}, u32[]{:S(2)}) collective-permute-start(bf16[4,22,3]{2,1,0:T(8,128)(2,1)S(1)} %get-tuple-element.69), channel_id=1, source_target_pairs={{0,1},{1,2},{2,3},{4,5},{5,6},{6,7},{8,9},{9,10},{10,11},{12,13},{... | collective-permute-start | bytes 1592 | tf_op jit(solution)/shard_map/ppermute | solution.py:34
  139.2 2.7 %collective-permute-start.11 = (bf16[4,22,3]{2,1,0:T(8,128)(2,1)S(1)}, bf16[4,22,3]{2,1,0:T(8,128)(2,1)S(1)}, u32[]{:S(2)}, u32[]{:S(2)}) collective-permute-start(bf16[4,22,3]{2,1,0:T(8,128)(2,1)S(1)} %get-tuple-element.70), channel_id=1, source_target_pairs={{1,0},{2,1},{3,2},{5,4},{6,5},{7,6},{9,8},{10,9},{11,10},{13,12},{... | collective-permute-start | bytes 1592 | tf_op jit(solution)/shard_map/ppermute | solution.py:35
  142.9 2.0 %collective-permute-done.11 = bf16[4,22,3]{2,1,0:T(8,128)(2,1)S(1)} collective-permute-done((bf16[4,22,3]{2,1,0:T(8,128)(2,1)S(1)}, bf16[4,22,3]{2,1,0:T(8,128)(2,1)S(1)}, u32[]{:S(2)}, u32[]{:S(2)}) %collective-permute-start.11) | collective-permute-done | bytes 560 | tf_op jit(solution)/shard_map/ppermute | solution.py:35
  151.7 2.7 %fusion.35 = f32[62,32,256]{2,1,0:T(8,128)S(1)} fusion(f32[62,32,256]{2,1,0:T(8,128)S(1)} %copy-done, f32[62,1,256]{2,1,0:T(1,128)} %collective-permute-done.4, f32[62,31,256]{2,1,0:T(8,128)S(1)} %copy-done.4, f32[62,31,256]{2,1,0:T(8,128)S(1)} %copy-done.3, f32[62,1,256]{2,1,0:T(1,128)} %collective-permute-done.5, f32[62,32,1]{2,1,0:T(8,128)S(1)} %copy-done.6, ...), kind=kLoop, calls=%fused_computation.38 | loop fusion | flops 8634368 | bytes 12320768 | tf_op jit(solution)/shard_map/add | solution.py:207
  (129 shorter events, 33.3 us)
Async XLA Ops:
  0.6 17.4 %copy-start.5 = (f32[144,2048]{1,0:T(8,128)S(1)}, f32[144,2048]{1,0:T(8,128)}, u32[]{:S(2)}) copy-start(f32[144,2048]{1,0:T(8,128)} %atm_ref.1) | copy-start | bytes 3538948
  2.7 148.8 %collective-permute-start.5 = (f32[62,1,256]{2,1,0:T(1,128)}, f32[62,1,256]{2,1,0:T(1,128)}, u32[]{:S(2)}, u32[]{:S(2)}) collective-permute-start(f32[62,1,256]{2,1,0:T(1,128)} %get-tuple-element.36), channel_id=1, source_target_pairs={{0,4},{4,8},{8,12},{12,16},{16,20},{20,24},{24,28},{28,32},{32,36}... | collective-permute-start | bytes 190472 | tf_op jit(solution)/shard_map/ppermute | solution.py:44
  9.5 73.9 %collective-permute-start = (f32[12,4,256]{2,1,0:T(4,128)}, f32[12,4,256]{2,1,0:T(4,128)S(1)}, u32[]{:S(2)}, u32[]{:S(2)}) collective-permute-start(f32[12,4,256]{2,1,0:T(4,128)} %get-tuple-element.44), channel_id=1, source_target_pairs={{0,4},{4,8},{8,12},{12,16},{16,20},{20,24},{24,28},{28,32},{32,36}... | collective-permute-start | bytes 147464 | tf_op jit(solution)/shard_map/ppermute | solution.py:31
  13.0 70.3 %collective-permute-start.1 = (f32[12,4,256]{2,1,0:T(4,128)}, f32[12,4,256]{2,1,0:T(4,128)S(1)}, u32[]{:S(2)}, u32[]{:S(2)}) collective-permute-start(f32[12,4,256]{2,1,0:T(4,128)} %get-tuple-element.45), channel_id=1, source_target_pairs={{4,0},{8,4},{12,8},{16,12},{20,16},{24,20},{28,24},{32,28},{36,32}... | collective-permute-start | bytes 147464 | tf_op jit(solution)/shard_map/ppermute | solution.py:32
  30.1 8.6 %copy-start = (f32[62,32,256]{2,1,0:T(8,128)S(1)}, f32[62,32,256]{2,1,0:T(8,128)}, u32[]{:S(2)}) copy-start(f32[62,32,256]{2,1,0:T(8,128)} %param.19) | copy-start | bytes 6094852
  30.1 37.1 %all-to-all-start = ((bf16[128,32,144]{2,1,0:T(8,128)(2,1)}), bf16[128,32,144]{2,1,0:T(8,128)(2,1)}, u32[]{:S(2)}, u32[]{:S(2)}) async-start(bf16[128,32,144]{2,1,0:T(8,128)(2,1)} %bitcast.145), calls=%async_computation | async-start | bytes 4194304 | tf_op jit(solution)/shard_map/all_to_all | solution.py:281
  42.4 54.3 %collective-permute-start.6 = (f32[62,32]{0,1:T(8,128)}, f32[62,32]{0,1:T(8,128)}, u32[]{:S(2)}, u32[]{:S(2)}) collective-permute-start(f32[62,32]{0,1:T(8,128)} %bitcast.163), channel_id=1, source_target_pairs={{1,0},{2,1},{3,2},{5,4},{6,5},{7,6},{9,8},{10,9},{11,10},{13,12},{... | collective-permute-start | bytes 23816 | tf_op jit(solution)/shard_map/ppermute | solution.py:47
  46.1 45.2 %collective-permute-start.7 = (f32[62,32]{0,1:T(8,128)}, f32[62,32]{0,1:T(8,128)S(1)}, u32[]{:S(2)}, u32[]{:S(2)}) collective-permute-start(f32[62,32]{0,1:T(8,128)} %bitcast.165), channel_id=1, source_target_pairs={{0,1},{1,2},{2,3},{4,5},{5,6},{6,7},{8,9},{9,10},{10,11},{12,13},{... | collective-permute-start | bytes 23816 | tf_op jit(solution)/shard_map/ppermute | solution.py:46
  73.3 38.4 %all-to-all-start.1 = ((bf16[128,32,148]{2,1,0:T(8,128)(2,1)}), bf16[128,32,148]{2,1,0:T(8,128)(2,1)}, u32[]{:S(2)}, u32[]{:S(2)}) async-start(bf16[128,32,148]{2,1,0:T(8,128)(2,1)} %bitcast.144), calls=%async_computation.1 | async-start | bytes 4194304 | tf_op jit(solution)/shard_map/all_to_all | solution.py:282
  84.2 24.2 %collective-permute-start.2 = (f32[12,40,4]{2,1,0:T(8,128)}, f32[12,40,4]{2,1,0:T(8,128)}, u32[]{:S(2)}, u32[]{:S(2)}) collective-permute-start(f32[12,40,4]{2,1,0:T(8,128)} %get-tuple-element.42), channel_id=1, source_target_pairs={{0,1},{1,2},{2,3},{4,5},{5,6},{6,7},{8,9},{9,10},{10,11},{12,13},{... | collective-permute-start | bytes 23048 | tf_op jit(solution)/shard_map/ppermute | solution.py:34
  87.6 21.7 %collective-permute-start.3 = (f32[12,40,4]{2,1,0:T(8,128)}, f32[12,40,4]{2,1,0:T(8,128)}, u32[]{:S(2)}, u32[]{:S(2)}) collective-permute-start(f32[12,40,4]{2,1,0:T(8,128)} %get-tuple-element.43), channel_id=1, source_target_pairs={{1,0},{2,1},{3,2},{5,4},{6,5},{7,6},{9,8},{10,9},{11,10},{13,12},{... | collective-permute-start | bytes 23048 | tf_op jit(solution)/shard_map/ppermute | solution.py:35
  91.3 3.7 %copy-start.17 = (f32[62,32]{0,1:T(8,128)}, f32[62,32]{0,1:T(8,128)S(1)}, u32[]{:S(2)}) copy-start(f32[62,32]{0,1:T(8,128)S(1)} %collective-permute-done.7) | copy-start | bytes 23812
  91.3 60.1 %collective-permute-start.4 = (f32[62,1,256]{2,1,0:T(1,128)}, f32[62,1,256]{2,1,0:T(1,128)}, u32[]{:S(2)}, u32[]{:S(2)}) collective-permute-start(f32[62,1,256]{2,1,0:T(1,128)} %get-tuple-element.37), channel_id=1, source_target_pairs={{4,0},{8,4},{12,8},{16,12},{20,16},{24,20},{28,24},{32,28},{36,32}... | collective-permute-start | bytes 190472 | tf_op jit(solution)/shard_map/ppermute | solution.py:45
  126.1 18.8 %copy-start.14 = (pred[134,264]{1,0:T(8,128)(4,1)S(1)}, pred[134,264]{1,0:T(8,128)(4,1)}, u32[]{:S(2)}) copy-start(pred[134,264]{1,0:T(8,128)(4,1)} %iota_compare_fusion.9) | copy-start | bytes 106132
  126.1 18.8 %copy-start.15 = (pred[134,264]{1,0:T(8,128)(4,1)S(1)}, pred[134,264]{1,0:T(8,128)(4,1)}, u32[]{:S(2)}) copy-start(pred[134,264]{1,0:T(8,128)(4,1)} %iota_compare_fusion.11) | copy-start | bytes 106132
  126.1 18.8 %copy-start.16 = (pred[134,264]{1,0:T(8,128)(4,1)S(1)}, pred[134,264]{1,0:T(8,128)(4,1)}, u32[]{:S(2)}) copy-start(pred[134,264]{1,0:T(8,128)(4,1)} %iota_compare_fusion.10) | copy-start | bytes 106132
  126.9 9.1 %collective-permute-start.8 = (bf16[4,3,128]{2,1,0:T(4,128)(2,1)S(1)}, bf16[4,3,128]{2,1,0:T(4,128)(2,1)S(1)}, u32[]{:S(2)}, u32[]{:S(2)}) collective-permute-start(bf16[4,3,128]{2,1,0:T(4,128)(2,1)S(1)} %get-tuple-element.71), channel_id=1, source_target_pairs={{0,4},{4,8},{8,12},{12,16},{16,20},{20,24},{24,28},{28,32},{32,36}... | collective-permute-start | bytes 9224 | tf_op jit(solution)/shard_map/ppermute | solution.py:31
  128.8 7.2 %collective-permute-start.9 = (bf16[4,3,128]{2,1,0:T(4,128)(2,1)S(1)}, bf16[4,3,128]{2,1,0:T(4,128)(2,1)S(1)}, u32[]{:S(2)}, u32[]{:S(2)}) collective-permute-start(bf16[4,3,128]{2,1,0:T(4,128)(2,1)S(1)} %get-tuple-element.72), channel_id=1, source_target_pairs={{4,0},{8,4},{12,8},{16,12},{20,16},{24,20},{28,24},{32,28},{36,32}... | collective-permute-start | bytes 9224 | tf_op jit(solution)/shard_map/ppermute | solution.py:32
  136.0 9.9 %copy-start.18 = (s32[40]{0:T(128)S(1)}, s32[40]{0:T(128)}, u32[]{:S(2)}) copy-start(s32[40]{0:T(128)} %clamp_subtract_fusion.5) | copy-start | bytes 484
  136.1 6.8 %collective-permute-start.10 = (bf16[4,22,3]{2,1,0:T(8,128)(2,1)S(1)}, bf16[4,22,3]{2,1,0:T(8,128)(2,1)S(1)}, u32[]{:S(2)}, u32[]{:S(2)}) collective-permute-start(bf16[4,22,3]{2,1,0:T(8,128)(2,1)S(1)} %get-tuple-element.69), channel_id=1, source_target_pairs={{0,1},{1,2},{2,3},{4,5},{5,6},{6,7},{8,9},{9,10},{10,11},{12,13},{... | collective-permute-start | bytes 1592 | tf_op jit(solution)/shard_map/ppermute | solution.py:34
  139.2 5.7 %collective-permute-start.11 = (bf16[4,22,3]{2,1,0:T(8,128)(2,1)S(1)}, bf16[4,22,3]{2,1,0:T(8,128)(2,1)S(1)}, u32[]{:S(2)}, u32[]{:S(2)}) collective-permute-start(bf16[4,22,3]{2,1,0:T(8,128)(2,1)S(1)} %get-tuple-element.70), channel_id=1, source_target_pairs={{1,0},{2,1},{3,2},{5,4},{6,5},{7,6},{9,8},{10,9},{11,10},{13,12},{... | collective-permute-start | bytes 1592 | tf_op jit(solution)/shard_map/ppermute | solution.py:35
  146.2 5.3 %copy-start.6 = (f32[62,32,1]{2,1,0:T(8,128)S(1)}, f32[62,32,1]{2,1,0:T(8,128)}, u32[]{:S(2)}) copy-start(f32[62,32,1]{2,1,0:T(8,128)} %copy.24) | copy-start | bytes 23812
  146.7 4.8 %copy-start.4 = (f32[62,31,256]{2,1,0:T(8,128)S(1)}, f32[62,31,256]{2,1,0:T(8,128)}, u32[]{:S(2)}) copy-start(f32[62,31,256]{2,1,0:T(8,128)} %get-tuple-element.39) | copy-start | bytes 5904388
  148.1 3.4 %copy-start.3 = (f32[62,31,256]{2,1,0:T(8,128)S(1)}, f32[62,31,256]{2,1,0:T(8,128)}, u32[]{:S(2)}) copy-start(f32[62,31,256]{2,1,0:T(8,128)} %get-tuple-element.38) | copy-start | bytes 5904388
  149.3 1.4 copy-start.8
  149.3 1.4 copy-start.10
  149.3 1.4 copy-start.11
  149.3 1.4 copy-start.12
  149.3 1.4 copy-start.13
  149.4 2.1 %copy-start.1 = (f32[62,32,255]{2,1,0:T(8,128)S(1)}, f32[62,32,255]{2,1,0:T(8,128)}, u32[]{:S(2)}) copy-start(f32[62,32,255]{2,1,0:T(8,128)} %get-tuple-element.34) | copy-start | bytes 6071044
  149.4 2.3 %copy-start.2 = (f32[62,32,255]{2,1,0:T(8,128)S(1)}, f32[62,32,255]{2,1,0:T(8,128)}, u32[]{:S(2)}) copy-start(f32[62,32,255]{2,1,0:T(8,128)} %get-tuple-element.35) | copy-start | bytes 6071044
  154.4 1.3 copy-start.7
  (1 other events, 0.7 us)

commit v8 on v7

--- a/solution.py
+++ b/solution.py
@@ -112,42 +112,46 @@
     )(columns, operators, flux_map)
 
 
-def unpack_kernel(got_ref, atm_ref, eye_ref, atm_out_ref, flux_out_ref):
+def fetch_kernel(slots_ref, back_ref, atm_ref, atm_out_ref, flux_out_ref):
     features = atm_ref.shape[0]
-    turned = lax.dot_general(
-        eye_ref[...], got_ref[...], (((1,), (1,)), ((), ())), preferred_element_type=jnp.float32
-    )
-    atm_out_ref[...] = atm_ref[...] + turned[:features]
-    flux_out_ref[...] = turned[features:].astype(flux_out_ref.dtype)
-
-
-def unpack(got, atm_state):
-    columns, width = got.shape
-    features = atm_state.shape[0]
-    tile = min(columns, 512)
-    eye = jnp.eye(width, dtype=jnp.bfloat16)
+    count = back_ref.shape[0]
+    tile = slots_ref.shape[1]
+    picked = (lax.broadcasted_iota(jnp.int32, (count, tile), 0) == slots_ref[...]).astype(
+        jnp.bfloat16
+    )
+    got = lax.dot_general(
+        back_ref[...], picked, (((0,), (0,)), ((), ())), preferred_element_type=jnp.float32
+    )
+    atm_out_ref[...] = atm_ref[...] + got[:features]
+    flux_out_ref[...] = got[features:].astype(flux_out_ref.dtype)
+
+
+def fetch(back, slots, atm_state):
+    count, width = back.shape
+    features, columns = atm_state.shape
+    tile = min(columns, 256)
     return pl.pallas_call(
-        unpack_kernel,
+        fetch_kernel,
         out_shape=(
             jax.ShapeDtypeStruct((features, columns), jnp.float32),
             jax.ShapeDtypeStruct((width - features, columns), jnp.bfloat16),
         ),
         grid=(columns // tile,),
         in_specs=[
-            pl.BlockSpec((tile, width), lambda i: (i, 0)),
+            pl.BlockSpec((1, tile), lambda i: (0, i)),
+            pl.BlockSpec((count, width), lambda i: (0, 0)),
             pl.BlockSpec((features, tile), lambda i: (0, i)),
-            pl.BlockSpec((width, width), lambda i: (0, 0)),
         ],
         out_specs=(
             pl.BlockSpec((features, tile), lambda i: (0, i)),
             pl.BlockSpec((width - features, tile), lambda i: (0, i)),
         ),
         cost_estimate=pl.CostEstimate(
-            flops=2 * columns * width * width,
+            flops=2 * count * width * columns,
             transcendentals=0,
-            bytes_accessed=2 * columns * width + 8 * columns * features + 2 * columns * width,
+            bytes_accessed=2 * count * width + 8 * columns * features + 2 * columns * width,
         ),
-    )(got, atm_state, eye)
+    )(slots.reshape(1, columns), back, atm_state)
 
 
 def selector(count, origin, offset, limit, base, size):
@@ -286,8 +290,7 @@
         concat_axis=0,
         tiled=True,
     )
-    returned = jnp.take(back, slots, axis=0, mode="clip")
-    atm_new, flux_cols = unpack(returned, atm_state)
+    atm_new, flux_cols = fetch(back, slots, atm_state)
     mask_ext = planes_ext[0]
     eta = planes_ext[1]
     flow_u = planes_ext[2]

time: 158 us -> 153 us (0.968)
  local copies, waits for them, and re-layouts: 40.3 us -> 30 us
  Pallas kernels: 10.2 us -> 15.4 us
    gather x1 -> x0, local copies, waits for them, and re-layouts: 10.3 us -> none  [per_device(): returned = jnp.take(back, slots, axis=0, mode='clip')]
    pallas_call x1, Pallas kernels: 4.12 us -> 9.34 us  [fetch(): pl.pallas_call(fetch_kernel, out_shape=(jax.ShapeDtypeStruct((features, c...]
    ppermute x2, waiting for transfers between devices: 9.18 us -> 11.6 us  [with_halo(): lax.ppermute(cells[..., cols - width:], 'narrow', shift_pairs(narrow_coun...]
    all_to_all x1, waiting for transfers between devices: 9.22 us -> 7.45 us  [per_device(): lax.all_to_all(outgoing, ('wide', 'narrow'), split_axis=0, concat_axis=0,...]
    unnamed x44 -> x42, local copies, waits for them, and re-layouts: 9.25 us -> 9.25 us
  transfers between devices with their start and end apart: 14 -> 14, of which waited for: 4 -> 4; matrix products, arithmetic and copies ran while one was open for 40% -> 34% of each run, Pallas kernels for 7% -> 10%
where the time goes in v8:
time: 153 us; the launch traced here: 151 us
  starting transfers between devices  54.7 us (36%)
  local copies, waits for them, and re-layouts  30 us (20%)
  waiting for transfers between devices  22 us (14%)
  other arithmetic  18.2 us (12%)
  Pallas kernels  15.4 us (10%)
  matrix products  9.05 us (6%)
    ppermute x2, waiting for transfers between devices, with_halo(): lax.ppermute(cells[..., cols - width:], 'narrow', shift_pairs(narrow_coun...  11.6 us
    ppermute x2, starting transfers between devices, with_halo(): lax.ppermute(cells[..., :width, :], 'wide', shift_pairs(wide_count, -1))  9.84 us
    pallas_call x1, Pallas kernels, fetch(): pl.pallas_call(fetch_kernel, out_shape=(jax.ShapeDtypeStruct((features, c...  9.34 us
    unnamed x42, local copies, waits for them, and re-layouts  9.25 us
    all_to_all x1, starting transfers between devices, per_device(): lax.all_to_all(outgoing, ('wide', 'narrow'), split_axis=0, concat_axis=0,...  8.57 us
    dot_general x8, matrix products, place_columns(): lax.dot_general(selector, source, (((1,), (1,)), ((), ())), preferred_ele...  7.83 us
    all_to_all x1, waiting for transfers between devices, per_device(): lax.all_to_all(outgoing, ('wide', 'narrow'), split_axis=0, concat_axis=0,...  7.45 us
    all_to_all x1, starting transfers between devices, per_device(): lax.all_to_all(physics(regime_ops[0], arrived, flux_map), ('wide', 'narro...  6.85 us
  transfers between devices with their start and end apart: 14, of which 4 were waited for; matrix products, arithmetic and copies ran while one was open for 34% of the time, Pallas kernels for 10%

profile of v8, /device:TPU:34, one launch (start us, length us, event | category | flops | bytes accessed | tf_op | source)
XLA Modules:
  0.0 150.7 jit_solution(11239964067369609894)
XLA Ops:
  0.6 2.0 %fusion.139 = (f32[62,1,256]{2,1,0:T(1,128)}, f32[62,1,256]{2,1,0:T(1,128)}) fusion(f32[62,32,256]{2,1,0:T(8,128)} %param.19), kind=kLoop, calls=%fused_computation.221 | loop fusion | bytes 253952 | tf_op jit(solution)/shard_map/slice | solution.py:44
  2.7 1.9 %collective-permute-start.5 = (f32[62,1,256]{2,1,0:T(1,128)}, f32[62,1,256]{2,1,0:T(1,128)}, u32[]{:S(2)}, u32[]{:S(2)}) collective-permute-start(f32[62,1,256]{2,1,0:T(1,128)} %get-tuple-element.36), channel_id=1, source_target_pairs={{0,4},{4,8},{8,12},{12,16},{16,20},{20,24},{24,28},{28,32},{32,36}... | collective-permute-start | bytes 190472 | tf_op jit(solution)/shard_map/ppermute | solution.py:44
  9.5 3.6 %collective-permute-start = (f32[12,4,256]{2,1,0:T(4,128)}, f32[12,4,256]{2,1,0:T(4,128)S(1)}, u32[]{:S(2)}, u32[]{:S(2)}) collective-permute-start(f32[12,4,256]{2,1,0:T(4,128)} %get-tuple-element.44), channel_id=1, source_target_pairs={{0,4},{4,8},{8,12},{12,16},{16,20},{20,24},{24,28},{28,32},{32,36}... | collective-permute-start | bytes 147464 | tf_op jit(solution)/shard_map/ppermute | solution.py:31
  13.0 4.1 %collective-permute-start.1 = (f32[12,4,256]{2,1,0:T(4,128)}, f32[12,4,256]{2,1,0:T(4,128)S(1)}, u32[]{:S(2)}, u32[]{:S(2)}) collective-permute-start(f32[12,4,256]{2,1,0:T(4,128)} %get-tuple-element.45), channel_id=1, source_target_pairs={{4,0},{8,4},{12,8},{16,12},{20,16},{24,20},{28,24},{32,28},{36,32}... | collective-permute-start | bytes 147464 | tf_op jit(solution)/shard_map/ppermute | solution.py:32
  27.7 2.4 %copy.21 = bf16[4096,144]{1,0:T(8,128)(2,1)} copy(bf16[4096,144]{0,1:T(8,128)(2,1)S(1)} %fusion.80) | data formatting | bytes 2359296 | tf_op jit(solution)/shard_map/concatenate | solution.py:73
  30.1 8.6 %all-to-all-start = ((bf16[128,32,144]{2,1,0:T(8,128)(2,1)}), bf16[128,32,144]{2,1,0:T(8,128)(2,1)}, u32[]{:S(2)}, u32[]{:S(2)}) async-start(bf16[128,32,144]{2,1,0:T(8,128)(2,1)} %bitcast.146), calls=%async_computation | async-start | bytes 4194304 | tf_op jit(solution)/shard_map/all_to_all | solution.py:285
  38.7 1.3 fusion.137
  40.0 2.4 %copy.27 = f32[62,32,1]{0,1,2:T(8,128)} copy(f32[62,32,1]{2,1,0:T(8,128)} %get-tuple-element.33) | data formatting | bytes 15872
  42.4 2.4 %collective-permute-start.6 = (f32[62,32]{0,1:T(8,128)}, f32[62,32]{0,1:T(8,128)}, u32[]{:S(2)}, u32[]{:S(2)}) collective-permute-start(f32[62,32]{0,1:T(8,128)} %bitcast.163), channel_id=1, source_target_pairs={{1,0},{2,1},{3,2},{5,4},{6,5},{7,6},{9,8},{10,9},{11,10},{13,12},{... | collective-permute-start | bytes 23816 | tf_op jit(solution)/shard_map/ppermute | solution.py:47
  44.9 1.3 copy.28
  46.2 3.6 %collective-permute-start.7 = (f32[62,32]{0,1:T(8,128)}, f32[62,32]{0,1:T(8,128)S(1)}, u32[]{:S(2)}, u32[]{:S(2)}) collective-permute-start(f32[62,32]{0,1:T(8,128)} %bitcast.165), channel_id=1, source_target_pairs={{0,1},{1,2},{2,3},{4,5},{5,6},{6,7},{8,9},{9,10},{10,11},{12,13},{... | collective-permute-start | bytes 23816 | tf_op jit(solution)/shard_map/ppermute | solution.py:46
  50.6 1.4 copy.22.fm_ref
  54.6 2.8 %fusion.138 = (f32[62,32,255]{2,1,0:T(8,128)}, f32[62,32,255]{2,1,0:T(8,128)}) fusion(f32[62,32,256]{2,1,0:T(8,128)S(1)} %copy-done), kind=kLoop, calls=%fused_computation.220 | loop fusion | bytes 8094720 | tf_op jit(solution)/shard_map/slice | solution.py:203
  57.3 2.5 %fusion.140 = (f32[62,31,256]{2,1,0:T(8,128)}, f32[62,31,256]{2,1,0:T(8,128)}) fusion(f32[62,32,256]{2,1,0:T(8,128)S(1)} %copy-done), kind=kLoop, calls=%fused_computation.222 | loop fusion | bytes 7872512 | tf_op jit(solution)/shard_map/slice | solution.py:201
  59.8 7.4 %all-to-all-done = bf16[128,32,144]{2,1,0:T(8,128)(2,1)} async-done(((bf16[128,32,144]{2,1,0:T(8,128)(2,1)}), bf16[128,32,144]{2,1,0:T(8,128)(2,1)}, u32[]{:S(2)}, u32[]{:S(2)}) %all-to-all-start) | async-done | bytes 1179680 | tf_op jit(solution)/shard_map/all_to_all | solution.py:285
  67.3 6.1 %shard_map.129 = bf16[4096,148]{1,0:T(8,128)(2,1)} custom-call(bf16[4096,144]{1,0:T(8,128)(2,1)} %bitcast.8.x_ref, bf16[4,144,144]{2,1,0:T(8,128)(2,1)} %bitcast.155, bf16[144,4]{1,0:T(8,128)(2,1)} %copy.22.fm_ref), custom_call_target="tpu_custom_call" | custom-call | flops 684195840 | bytes 2557952 | tf_op jit(solution)/shard_map/pallas_call | solution.py:97
  73.3 6.9 %all-to-all-start.1 = ((bf16[128,32,148]{2,1,0:T(8,128)(2,1)}), bf16[128,32,148]{2,1,0:T(8,128)(2,1)}, u32[]{:S(2)}, u32[]{:S(2)}) async-start(bf16[128,32,148]{2,1,0:T(8,128)(2,1)} %bitcast.145), calls=%async_computation.1 | async-start | bytes 4194304 | tf_op jit(solution)/shard_map/all_to_all | solution.py:286
  82.4 3.4 %collective-permute-start.2 = (f32[12,40,4]{2,1,0:T(8,128)}, f32[12,40,4]{2,1,0:T(8,128)}, u32[]{:S(2)}, u32[]{:S(2)}) collective-permute-start(f32[12,40,4]{2,1,0:T(8,128)} %get-tuple-element.42), channel_id=1, source_target_pairs={{0,1},{1,2},{2,3},{4,5},{5,6},{6,7},{8,9},{9,10},{10,11},{12,13},{... | collective-permute-start | bytes 23048 | tf_op jit(solution)/shard_map/ppermute | solution.py:34
  85.8 3.1 %collective-permute-start.3 = (f32[12,40,4]{2,1,0:T(8,128)}, f32[12,40,4]{2,1,0:T(8,128)}, u32[]{:S(2)}, u32[]{:S(2)}) collective-permute-start(f32[12,40,4]{2,1,0:T(8,128)} %get-tuple-element.43), channel_id=1, source_target_pairs={{1,0},{2,1},{3,2},{5,4},{6,5},{7,6},{9,8},{10,9},{11,10},{13,12},{... | collective-permute-start | bytes 23048 | tf_op jit(solution)/shard_map/ppermute | solution.py:35
  89.0 3.7 %collective-permute-start.4 = (f32[62,1,256]{2,1,0:T(1,128)}, f32[62,1,256]{2,1,0:T(1,128)}, u32[]{:S(2)}, u32[]{:S(2)}) collective-permute-start(f32[62,1,256]{2,1,0:T(1,128)} %get-tuple-element.37), channel_id=1, source_target_pairs={{4,0},{8,4},{12,8},{16,12},{20,16},{24,20},{28,24},{32,28},{36,32}... | collective-permute-start | bytes 190472 | tf_op jit(solution)/shard_map/ppermute | solution.py:45
  92.7 1.7 %copy.26 = f32[62,32,1]{2,1,0:T(8,128)S(1)} copy(f32[62,32,1]{0,1,2:T(8,128)} %bitcast.164) | data formatting | bytes 15872 | tf_op jit(solution)/shard_map/broadcast_in_dim | solution.py:48
  94.4 2.5 %copy.24 = f32[62,32,1]{2,1,0:T(8,128)} copy(f32[62,32,1]{0,1,2:T(8,128)} %bitcast.19) | data formatting | bytes 15872 | tf_op jit(solution)/shard_map/broadcast_in_dim | solution.py:48
  96.9 11.5 %collective-permute-done.2 = f32[12,40,4]{2,1,0:T(8,128)} collective-permute-done((f32[12,40,4]{2,1,0:T(8,128)}, f32[12,40,4]{2,1,0:T(8,128)}, u32[]{:S(2)}, u32[]{:S(2)}) %collective-permute-start.2) | collective-permute-done | bytes 7712 | tf_op jit(solution)/shard_map/ppermute | solution.py:34
  109.4 2.3 %pad_maximum_fusion = f32[12,40,264]{2,1,0:T(8,128)} fusion(f32[12,40,4]{2,1,0:T(8,128)} %collective-permute-done.3, f32[12,4,256]{2,1,0:T(4,128)S(1)} %collective-permute-done.1, f32[12,32,256]{2,1,0:T(8,128)S(1)} %constant_dynamic-update-slice_fusion, f32[12,4,256]{2,1,0:T(4,128)S(1)} %collective-permute-done, f32[12,40,4]{2,1,0:T(8,128)} %collective-permute-done.2), kind=kLoop, calls=%fused_computation.71 | loop fusion | flops 506880 | bytes 1013760 | tf_op jit(solution)/shard_map/concatenate | solution.py:36
  111.7 9.3 %shard_map.130 = (f32[144,2048]{1,0:T(8,128)}, bf16[4,2048]{1,0:T(4,128)(2,1)}) custom-call(s32[1,2048]{1,0:T(1,128)} %bitcast_add_fusion.slots_ref, bf16[4096,148]{1,0:T(8,128)(2,1)} %bitcast.11.back_ref, f32[144,2048]{1,0:T(8,128)} %atm_ref.1), custom_call_target="tpu_custom_call" | custom-call | flops 2483027968 | bytes 4177920 | tf_op jit(solution)/shard_map/pallas_call | solution.py:133
  121.8 1.9 %collective-permute-start.8 = (bf16[4,3,128]{2,1,0:T(4,128)(2,1)S(1)}, bf16[4,3,128]{2,1,0:T(4,128)(2,1)S(1)}, u32[]{:S(2)}, u32[]{:S(2)}) collective-permute-start(bf16[4,3,128]{2,1,0:T(4,128)(2,1)S(1)} %get-tuple-element.71), channel_id=1, source_target_pairs={{0,4},{4,8},{8,12},{12,16},{16,20},{20,24},{24,28},{28,32},{32,36}... | collective-permute-start | bytes 9224 | tf_op jit(solution)/shard_map/ppermute | solution.py:31
  123.8 5.8 %collective-permute-start.9 = (bf16[4,3,128]{2,1,0:T(4,128)(2,1)S(1)}, bf16[4,3,128]{2,1,0:T(4,128)(2,1)S(1)}, u32[]{:S(2)}, u32[]{:S(2)}) collective-permute-start(bf16[4,3,128]{2,1,0:T(4,128)(2,1)S(1)} %get-tuple-element.72), channel_id=1, source_target_pairs={{4,0},{8,4},{12,8},{16,12},{20,16},{24,20},{28,24},{32,28},{36,32}... | collective-permute-start | bytes 9224 | tf_op jit(solution)/shard_map/ppermute | solution.py:32
  129.5 1.4 select_reduce_fusion.8
  131.0 3.1 %collective-permute-start.10 = (bf16[4,22,3]{2,1,0:T(8,128)(2,1)S(1)}, bf16[4,22,3]{2,1,0:T(8,128)(2,1)S(1)}, u32[]{:S(2)}, u32[]{:S(2)}) collective-permute-start(bf16[4,22,3]{2,1,0:T(8,128)(2,1)S(1)} %get-tuple-element.69), channel_id=1, source_target_pairs={{0,1},{1,2},{2,3},{4,5},{5,6},{6,7},{8,9},{9,10},{10,11},{12,13},{... | collective-permute-start | bytes 1592 | tf_op jit(solution)/shard_map/ppermute | solution.py:34
  134.1 2.7 %collective-permute-start.11 = (bf16[4,22,3]{2,1,0:T(8,128)(2,1)S(1)}, bf16[4,22,3]{2,1,0:T(8,128)(2,1)S(1)}, u32[]{:S(2)}, u32[]{:S(2)}) collective-permute-start(bf16[4,22,3]{2,1,0:T(8,128)(2,1)S(1)} %get-tuple-element.70), channel_id=1, source_target_pairs={{1,0},{2,1},{3,2},{5,4},{6,5},{7,6},{9,8},{10,9},{11,10},{13,12},{... | collective-permute-start | bytes 1592 | tf_op jit(solution)/shard_map/ppermute | solution.py:35
  137.8 2.0 %collective-permute-done.11 = bf16[4,22,3]{2,1,0:T(8,128)(2,1)S(1)} collective-permute-done((bf16[4,22,3]{2,1,0:T(8,128)(2,1)S(1)}, bf16[4,22,3]{2,1,0:T(8,128)(2,1)S(1)}, u32[]{:S(2)}, u32[]{:S(2)}) %collective-permute-start.11) | collective-permute-done | bytes 560 | tf_op jit(solution)/shard_map/ppermute | solution.py:35
  146.6 2.7 %fusion.35 = f32[62,32,256]{2,1,0:T(8,128)S(1)} fusion(f32[62,32,256]{2,1,0:T(8,128)S(1)} %copy-done, f32[62,1,256]{2,1,0:T(1,128)} %collective-permute-done.4, f32[62,31,256]{2,1,0:T(8,128)S(1)} %copy-done.4, f32[62,31,256]{2,1,0:T(8,128)S(1)} %copy-done.3, f32[62,1,256]{2,1,0:T(1,128)} %collective-permute-done.5, f32[62,32,1]{2,1,0:T(8,128)S(1)} %copy-done.5, ...), kind=kLoop, calls=%fused_computation.37 | loop fusion | flops 8634368 | bytes 12320768 | tf_op jit(solution)/shard_map/add | solution.py:211
  (124 shorter events, 31.5 us)
Async XLA Ops:
  0.6 17.4 %copy-start.7 = (f32[144,2048]{1,0:T(8,128)S(1)}, f32[144,2048]{1,0:T(8,128)}, u32[]{:S(2)}) copy-start(f32[144,2048]{1,0:T(8,128)} %atm_ref.1) | copy-start | bytes 3538948
  2.7 143.7 %collective-permute-start.5 = (f32[62,1,256]{2,1,0:T(1,128)}, f32[62,1,256]{2,1,0:T(1,128)}, u32[]{:S(2)}, u32[]{:S(2)}) collective-permute-start(f32[62,1,256]{2,1,0:T(1,128)} %get-tuple-element.36), channel_id=1, source_target_pairs={{0,4},{4,8},{8,12},{12,16},{16,20},{20,24},{24,28},{28,32},{32,36}... | collective-permute-start | bytes 190472 | tf_op jit(solution)/shard_map/ppermute | solution.py:44
  9.5 72.0 %collective-permute-start = (f32[12,4,256]{2,1,0:T(4,128)}, f32[12,4,256]{2,1,0:T(4,128)S(1)}, u32[]{:S(2)}, u32[]{:S(2)}) collective-permute-start(f32[12,4,256]{2,1,0:T(4,128)} %get-tuple-element.44), channel_id=1, source_target_pairs={{0,4},{4,8},{8,12},{12,16},{16,20},{20,24},{24,28},{28,32},{32,36}... | collective-permute-start | bytes 147464 | tf_op jit(solution)/shard_map/ppermute | solution.py:31
  13.0 68.4 %collective-permute-start.1 = (f32[12,4,256]{2,1,0:T(4,128)}, f32[12,4,256]{2,1,0:T(4,128)S(1)}, u32[]{:S(2)}, u32[]{:S(2)}) collective-permute-start(f32[12,4,256]{2,1,0:T(4,128)} %get-tuple-element.45), channel_id=1, source_target_pairs={{4,0},{8,4},{12,8},{16,12},{20,16},{24,20},{28,24},{32,28},{36,32}... | collective-permute-start | bytes 147464 | tf_op jit(solution)/shard_map/ppermute | solution.py:32
  18.5 0.7 copy-start.9
  30.1 8.6 %copy-start = (f32[62,32,256]{2,1,0:T(8,128)S(1)}, f32[62,32,256]{2,1,0:T(8,128)}, u32[]{:S(2)}) copy-start(f32[62,32,256]{2,1,0:T(8,128)} %param.19) | copy-start | bytes 6094852
  30.1 37.1 %all-to-all-start = ((bf16[128,32,144]{2,1,0:T(8,128)(2,1)}), bf16[128,32,144]{2,1,0:T(8,128)(2,1)}, u32[]{:S(2)}, u32[]{:S(2)}) async-start(bf16[128,32,144]{2,1,0:T(8,128)(2,1)} %bitcast.146), calls=%async_computation | async-start | bytes 4194304 | tf_op jit(solution)/shard_map/all_to_all | solution.py:285
  42.4 51.9 %collective-permute-start.6 = (f32[62,32]{0,1:T(8,128)}, f32[62,32]{0,1:T(8,128)}, u32[]{:S(2)}, u32[]{:S(2)}) collective-permute-start(f32[62,32]{0,1:T(8,128)} %bitcast.163), channel_id=1, source_target_pairs={{1,0},{2,1},{3,2},{5,4},{6,5},{7,6},{9,8},{10,9},{11,10},{13,12},{... | collective-permute-start | bytes 23816 | tf_op jit(solution)/shard_map/ppermute | solution.py:47
  46.2 42.8 %collective-permute-start.7 = (f32[62,32]{0,1:T(8,128)}, f32[62,32]{0,1:T(8,128)S(1)}, u32[]{:S(2)}, u32[]{:S(2)}) collective-permute-start(f32[62,32]{0,1:T(8,128)} %bitcast.165), channel_id=1, source_target_pairs={{0,1},{1,2},{2,3},{4,5},{5,6},{6,7},{8,9},{9,10},{10,11},{12,13},{... | collective-permute-start | bytes 23816 | tf_op jit(solution)/shard_map/ppermute | solution.py:46
  73.3 38.4 %all-to-all-start.1 = ((bf16[128,32,148]{2,1,0:T(8,128)(2,1)}), bf16[128,32,148]{2,1,0:T(8,128)(2,1)}, u32[]{:S(2)}, u32[]{:S(2)}) async-start(bf16[128,32,148]{2,1,0:T(8,128)(2,1)} %bitcast.145), calls=%async_computation.1 | async-start | bytes 4194304 | tf_op jit(solution)/shard_map/all_to_all | solution.py:286
  82.4 26.0 %collective-permute-start.2 = (f32[12,40,4]{2,1,0:T(8,128)}, f32[12,40,4]{2,1,0:T(8,128)}, u32[]{:S(2)}, u32[]{:S(2)}) collective-permute-start(f32[12,40,4]{2,1,0:T(8,128)} %get-tuple-element.42), channel_id=1, source_target_pairs={{0,1},{1,2},{2,3},{4,5},{5,6},{6,7},{8,9},{9,10},{10,11},{12,13},{... | collective-permute-start | bytes 23048 | tf_op jit(solution)/shard_map/ppermute | solution.py:34
  85.8 23.6 %collective-permute-start.3 = (f32[12,40,4]{2,1,0:T(8,128)}, f32[12,40,4]{2,1,0:T(8,128)}, u32[]{:S(2)}, u32[]{:S(2)}) collective-permute-start(f32[12,40,4]{2,1,0:T(8,128)} %get-tuple-element.43), channel_id=1, source_target_pairs={{1,0},{2,1},{3,2},{5,4},{6,5},{7,6},{9,8},{10,9},{11,10},{13,12},{... | collective-permute-start | bytes 23048 | tf_op jit(solution)/shard_map/ppermute | solution.py:35
  89.0 3.7 %copy-start.17 = (f32[62,32]{0,1:T(8,128)}, f32[62,32]{0,1:T(8,128)S(1)}, u32[]{:S(2)}) copy-start(f32[62,32]{0,1:T(8,128)S(1)} %collective-permute-done.7) | copy-start | bytes 23812
  89.0 57.4 %collective-permute-start.4 = (f32[62,1,256]{2,1,0:T(1,128)}, f32[62,1,256]{2,1,0:T(1,128)}, u32[]{:S(2)}, u32[]{:S(2)}) collective-permute-start(f32[62,1,256]{2,1,0:T(1,128)} %get-tuple-element.37), channel_id=1, source_target_pairs={{4,0},{8,4},{12,8},{16,12},{20,16},{24,20},{28,24},{32,28},{36,32}... | collective-permute-start | bytes 190472 | tf_op jit(solution)/shard_map/ppermute | solution.py:45
  121.1 18.8 %copy-start.14 = (pred[134,264]{1,0:T(8,128)(4,1)S(1)}, pred[134,264]{1,0:T(8,128)(4,1)}, u32[]{:S(2)}) copy-start(pred[134,264]{1,0:T(8,128)(4,1)} %iota_compare_fusion.9) | copy-start | bytes 106132
  121.1 18.8 %copy-start.15 = (pred[134,264]{1,0:T(8,128)(4,1)S(1)}, pred[134,264]{1,0:T(8,128)(4,1)}, u32[]{:S(2)}) copy-start(pred[134,264]{1,0:T(8,128)(4,1)} %iota_compare_fusion.11) | copy-start | bytes 106132
  121.1 18.8 %copy-start.16 = (pred[134,264]{1,0:T(8,128)(4,1)S(1)}, pred[134,264]{1,0:T(8,128)(4,1)}, u32[]{:S(2)}) copy-start(pred[134,264]{1,0:T(8,128)(4,1)} %iota_compare_fusion.10) | copy-start | bytes 106132
  121.8 9.1 %collective-permute-start.8 = (bf16[4,3,128]{2,1,0:T(4,128)(2,1)S(1)}, bf16[4,3,128]{2,1,0:T(4,128)(2,1)S(1)}, u32[]{:S(2)}, u32[]{:S(2)}) collective-permute-start(bf16[4,3,128]{2,1,0:T(4,128)(2,1)S(1)} %get-tuple-element.71), channel_id=1, source_target_pairs={{0,4},{4,8},{8,12},{12,16},{16,20},{20,24},{24,28},{28,32},{32,36}... | collective-permute-start | bytes 9224 | tf_op jit(solution)/shard_map/ppermute | solution.py:31
  123.8 7.2 %collective-permute-start.9 = (bf16[4,3,128]{2,1,0:T(4,128)(2,1)S(1)}, bf16[4,3,128]{2,1,0:T(4,128)(2,1)S(1)}, u32[]{:S(2)}, u32[]{:S(2)}) collective-permute-start(bf16[4,3,128]{2,1,0:T(4,128)(2,1)S(1)} %get-tuple-element.72), channel_id=1, source_target_pairs={{4,0},{8,4},{12,8},{16,12},{20,16},{24,20},{28,24},{32,28},{36,32}... | collective-permute-start | bytes 9224 | tf_op jit(solution)/shard_map/ppermute | solution.py:32
  131.0 6.8 %collective-permute-start.10 = (bf16[4,22,3]{2,1,0:T(8,128)(2,1)S(1)}, bf16[4,22,3]{2,1,0:T(8,128)(2,1)S(1)}, u32[]{:S(2)}, u32[]{:S(2)}) collective-permute-start(bf16[4,22,3]{2,1,0:T(8,128)(2,1)S(1)} %get-tuple-element.69), channel_id=1, source_target_pairs={{0,1},{1,2},{2,3},{4,5},{5,6},{6,7},{8,9},{9,10},{10,11},{12,13},{... | collective-permute-start | bytes 1592 | tf_op jit(solution)/shard_map/ppermute | solution.py:34
  134.1 5.7 %collective-permute-start.11 = (bf16[4,22,3]{2,1,0:T(8,128)(2,1)S(1)}, bf16[4,22,3]{2,1,0:T(8,128)(2,1)S(1)}, u32[]{:S(2)}, u32[]{:S(2)}) collective-permute-start(bf16[4,22,3]{2,1,0:T(8,128)(2,1)S(1)} %get-tuple-element.70), channel_id=1, source_target_pairs={{1,0},{2,1},{3,2},{5,4},{6,5},{7,6},{9,8},{10,9},{11,10},{13,12},{... | collective-permute-start | bytes 1592 | tf_op jit(solution)/shard_map/ppermute | solution.py:35
  141.1 5.3 %copy-start.5 = (f32[62,32,1]{2,1,0:T(8,128)S(1)}, f32[62,32,1]{2,1,0:T(8,128)}, u32[]{:S(2)}) copy-start(f32[62,32,1]{2,1,0:T(8,128)} %copy.24) | copy-start | bytes 23812
  141.6 4.8 %copy-start.4 = (f32[62,31,256]{2,1,0:T(8,128)S(1)}, f32[62,31,256]{2,1,0:T(8,128)}, u32[]{:S(2)}) copy-start(f32[62,31,256]{2,1,0:T(8,128)} %get-tuple-element.39) | copy-start | bytes 5904388
  143.0 3.4 %copy-start.3 = (f32[62,31,256]{2,1,0:T(8,128)S(1)}, f32[62,31,256]{2,1,0:T(8,128)}, u32[]{:S(2)}) copy-start(f32[62,31,256]{2,1,0:T(8,128)} %get-tuple-element.38) | copy-start | bytes 5904388
  144.2 1.4 copy-start.8
  144.2 1.4 copy-start.10
  144.3 1.4 copy-start.11
  144.3 1.4 copy-start.12
  144.3 1.4 copy-start.13
  144.3 2.1 %copy-start.1 = (f32[62,32,255]{2,1,0:T(8,128)S(1)}, f32[62,32,255]{2,1,0:T(8,128)}, u32[]{:S(2)}) copy-start(f32[62,32,255]{2,1,0:T(8,128)} %get-tuple-element.34) | copy-start | bytes 6071044
  144.4 2.3 %copy-start.2 = (f32[62,32,255]{2,1,0:T(8,128)S(1)}, f32[62,32,255]{2,1,0:T(8,128)}, u32[]{:S(2)}) copy-start(f32[62,32,255]{2,1,0:T(8,128)} %get-tuple-element.35) | copy-start | bytes 6071044
  149.4 1.3 copy-start.6

commit v9 on v8

--- a/solution.py
+++ b/solution.py
@@ -54,23 +54,39 @@
     return jnp.sum(before * onehot, axis=1)
 
 
-def block_width():
-    return 512
+def place_kernel(slots_ref, atm_ref, out_ref):
+    tile = out_ref.shape[0]
+    columns = slots_ref.shape[1]
+    first = pl.program_id(0) * tile
+    picked = (
+        first + lax.broadcasted_iota(jnp.int32, (tile, columns), 0) == slots_ref[...]
+    ).astype(jnp.bfloat16)
+    out_ref[...] = lax.dot_general(
+        picked,
+        atm_ref[...].astype(jnp.bfloat16),
+        (((1,), (1,)), ((), ())),
+        preferred_element_type=jnp.float32,
+    ).astype(out_ref.dtype)
 
 
 def place_columns(source, slots, total):
-    width = block_width()
-    pieces = []
-    for start in range(0, total, width):
-        selector = ((start + jnp.arange(width, dtype=jnp.int32))[:, None] == slots[None, :]).astype(
-            jnp.bfloat16
-        )
-        pieces.append(
-            lax.dot_general(
-                selector, source, (((1,), (1,)), ((), ())), preferred_element_type=jnp.float32
-            ).astype(jnp.bfloat16)
-        )
-    return jnp.concatenate(pieces, axis=0)
+    features, columns = source.shape
+    tile = min(total, 1024)
+    return pl.pallas_call(
+        place_kernel,
+        out_shape=jax.ShapeDtypeStruct((total, features), jnp.bfloat16),
+        grid=(total // tile,),
+        in_specs=[
+            pl.BlockSpec((1, columns), lambda i: (0, 0)),
+            pl.BlockSpec((features, columns), lambda i: (0, 0)),
+        ],
+        out_specs=pl.BlockSpec((tile, features), lambda i: (i, 0)),
+        cost_estimate=pl.CostEstimate(
+            flops=2 * total * columns * features,
+            transcendentals=0,
+            bytes_accessed=4 * features * columns + 2 * total * features,
+        ),
+    )(slots.reshape(1, columns), source)
 
 
 def physics_kernel(x_ref, op_ref, fm_ref, out_ref):
@@ -129,7 +145,7 @@
 def fetch(back, slots, atm_state):
     count, width = back.shape
     features, columns = atm_state.shape
-    tile = min(columns, 256)
+    tile = min(columns, 1024)
     return pl.pallas_call(
         fetch_kernel,
         out_shape=(
@@ -280,8 +296,7 @@
 
     owners = group_owner[:, 0]
     slots = owners * capacity + column_ranks(owners, peers)
-    initial = atm_state.astype(jnp.bfloat16)
-    outgoing = place_columns(initial, slots, total_slots)
+    outgoing = place_columns(atm_state, slots, total_slots)
     arrived = lax.all_to_all(outgoing, ("wide", "narrow"), split_axis=0, concat_axis=0, tiled=True)
     back = lax.all_to_all(
         physics(regime_ops[0], arrived, flux_map),

time: 153 us -> 155 us (1.013)
  waiting for transfers between devices: 22 us -> 33.8 us
  matrix products: 9.05 us -> 1.22 us
  local copies, waits for them, and re-layouts: 30 us -> 24.2 us
  Pallas kernels: 15.4 us -> 19.1 us
    all_to_all x1, waiting for transfers between devices: 7.45 us -> 22.3 us  [per_device(): lax.all_to_all(outgoing, ('wide', 'narrow'), split_axis=0, concat_axis=0,...]
    dot_general x8 -> x0, matrix products: 7.83 us -> none  [place_columns(): lax.dot_general(selector, source, (((1,), (1,)), ((), ())), preferred_ele...]
    pallas_call x0 -> x1, Pallas kernels: none -> 7.14 us  [place_columns(): pl.pallas_call(place_kernel, out_shape=jax.ShapeDtypeStruct((total, featu...]
    pallas_call x1, Pallas kernels: 9.34 us -> 5.94 us  [fetch(): pl.pallas_call(fetch_kernel, out_shape=(jax.ShapeDtypeStruct((features, c...]
    unnamed x42 -> x50, local copies, waits for them, and re-layouts: 9.25 us -> 6.01 us
    ppermute x2, waiting for transfers between devices: 11.6 us -> 8.53 us  [with_halo(): lax.ppermute(cells[..., cols - width:], 'narrow', shift_pairs(narrow_coun...]
    concatenate x1 -> x0, local copies, waits for them, and re-layouts: 2.43 us -> none  [place_columns(): return jnp.concatenate(pieces, axis=0)]
  transfers between devices with their start and end apart: 14 -> 14, of which waited for: 4 -> 4; matrix products, arithmetic and copies ran while one was open for 34% -> 24% of each run, Pallas kernels for 10% -> 12%
where the time goes in v9:
time: 155 us; the launch traced here: 153 us
  starting transfers between devices  55.2 us (36%)
  waiting for transfers between devices  33.8 us (22%)
  local copies, waits for them, and re-layouts  24.2 us (16%)
  Pallas kernels  19.1 us (12%)
  other arithmetic  18.4 us (12%)
    all_to_all x1, waiting for transfers between devices, per_device(): lax.all_to_all(outgoing, ('wide', 'narrow'), split_axis=0, concat_axis=0,...  22.3 us
    ppermute x2, starting transfers between devices, with_halo(): lax.ppermute(cells[..., :width, :], 'wide', shift_pairs(wide_count, -1))  9.84 us
    all_to_all x1, starting transfers between devices, per_device(): lax.all_to_all(outgoing, ('wide', 'narrow'), split_axis=0, concat_axis=0,...  9.13 us
    ppermute x2, waiting for transfers between devices, with_halo(): lax.ppermute(cells[..., cols - width:], 'narrow', shift_pairs(narrow_coun...  8.53 us
    pallas_call x1, Pallas kernels, place_columns(): pl.pallas_call(place_kernel, out_shape=jax.ShapeDtypeStruct((total, featu...  7.14 us
    all_to_all x1, starting transfers between devices, per_device(): lax.all_to_all(physics(regime_ops[0], arrived, flux_map), ('wide', 'narro...  6.85 us
    ppermute x2, starting transfers between devices, with_halo(): lax.ppermute(cells[..., cols - width:], 'narrow', shift_pairs(narrow_coun...  6.46 us
    pallas_call x1, Pallas kernels, physics(): pl.pallas_call(physics_kernel, out_shape=jax.ShapeDtypeStruct((slots, fea...  6.06 us
  transfers between devices with their start and end apart: 14, of which 4 were waited for; matrix products, arithmetic and copies ran while one was open for 24% of the time, Pallas kernels for 12%

profile of v9, /device:TPU:34, one launch (start us, length us, event | category | flops | bytes accessed | tf_op | source)
XLA Modules:
  0.0 153.2 jit_solution(1917760888930682831)
XLA Ops:
  0.6 1.9 %fusion.65 = (f32[62,1,256]{2,1,0:T(1,128)}, f32[62,1,256]{2,1,0:T(1,128)}) fusion(f32[62,32,256]{2,1,0:T(8,128)} %param.19), kind=kLoop, calls=%fused_computation.166 | loop fusion | bytes 253952 | tf_op jit(solution)/shard_map/slice | solution.py:44
  2.6 1.9 %collective-permute-start.5 = (f32[62,1,256]{2,1,0:T(1,128)}, f32[62,1,256]{2,1,0:T(1,128)}, u32[]{:S(2)}, u32[]{:S(2)}) collective-permute-start(f32[62,1,256]{2,1,0:T(1,128)} %get-tuple-element.36), channel_id=1, source_target_pairs={{0,4},{4,8},{8,12},{12,16},{16,20},{20,24},{24,28},{28,32},{32,36}... | collective-permute-start | bytes 190472 | tf_op jit(solution)/shard_map/ppermute | solution.py:44
  9.4 3.6 %collective-permute-start = (f32[12,4,256]{2,1,0:T(4,128)}, f32[12,4,256]{2,1,0:T(4,128)S(1)}, u32[]{:S(2)}, u32[]{:S(2)}) collective-permute-start(f32[12,4,256]{2,1,0:T(4,128)} %get-tuple-element.44), channel_id=1, source_target_pairs={{0,4},{4,8},{8,12},{12,16},{16,20},{20,24},{24,28},{28,32},{32,36}... | collective-permute-start | bytes 147464 | tf_op jit(solution)/shard_map/ppermute | solution.py:31
  12.9 4.1 %collective-permute-start.1 = (f32[12,4,256]{2,1,0:T(4,128)}, f32[12,4,256]{2,1,0:T(4,128)S(1)}, u32[]{:S(2)}, u32[]{:S(2)}) collective-permute-start(f32[12,4,256]{2,1,0:T(4,128)} %get-tuple-element.45), channel_id=1, source_target_pairs={{4,0},{8,4},{12,8},{16,12},{20,16},{24,20},{28,24},{32,28},{36,32}... | collective-permute-start | bytes 147464 | tf_op jit(solution)/shard_map/ppermute | solution.py:32
  17.0 1.9 %fusion.63 = (f32[62,32,1]{2,1,0:T(8,128)S(1)}, f32[62,32,1]{2,1,0:T(8,128)S(1)}) fusion(f32[62,32,256]{2,1,0:T(8,128)} %param.19), kind=kLoop, calls=%fused_computation.164 | loop fusion | bytes 31744 | tf_op jit(solution)/shard_map/slice | solution.py:46
  19.6 2.4 %collective-permute-start.6 = (f32[62,32]{0,1:T(8,128)S(1)}, f32[62,32]{0,1:T(8,128)}, u32[]{:S(2)}, u32[]{:S(2)}) collective-permute-start(f32[62,32]{0,1:T(8,128)S(1)} %bitcast.154), channel_id=1, source_target_pairs={{1,0},{2,1},{3,2},{5,4},{6,5},{7,6},{9,8},{10,9},{11,10},{13,12},{... | collective-permute-start | bytes 23816 | tf_op jit(solution)/shard_map/ppermute | solution.py:47
  22.7 3.4 %collective-permute-start.7 = (f32[62,32]{0,1:T(8,128)S(1)}, f32[62,32]{0,1:T(8,128)S(1)}, u32[]{:S(2)}, u32[]{:S(2)}) collective-permute-start(f32[62,32]{0,1:T(8,128)S(1)} %bitcast.156), channel_id=1, source_target_pairs={{0,1},{1,2},{2,3},{4,5},{5,6},{6,7},{8,9},{9,10},{10,11},{12,13},{... | collective-permute-start | bytes 23816 | tf_op jit(solution)/shard_map/ppermute | solution.py:46
  28.3 7.1 %shard_map.129 = bf16[4096,144]{1,0:T(8,128)(2,1)} custom-call(s32[1,2048]{1,0:T(1,128)} %bitcast_add_fusion.slots_ref, f32[144,2048]{1,0:T(8,128)} %atm_ref.3), custom_call_target="tpu_custom_call" | custom-call | flops 2415919104 | bytes 2359296 | tf_op jit(solution)/shard_map/pallas_call | solution.py:75
  35.5 9.1 %all-to-all-start = ((bf16[128,32,144]{2,1,0:T(8,128)(2,1)}), bf16[128,32,144]{2,1,0:T(8,128)(2,1)}, u32[]{:S(2)}, u32[]{:S(2)}) async-start(bf16[128,32,144]{2,1,0:T(8,128)(2,1)} %bitcast.138), calls=%async_computation | async-start | bytes 4194304 | tf_op jit(solution)/shard_map/all_to_all | solution.py:300
  48.0 2.8 %fusion.64 = (f32[62,32,255]{2,1,0:T(8,128)}, f32[62,32,255]{2,1,0:T(8,128)}) fusion(f32[62,32,256]{2,1,0:T(8,128)S(1)} %copy-done), kind=kLoop, calls=%fused_computation.165 | loop fusion | bytes 8094720 | tf_op jit(solution)/shard_map/slice | solution.py:219
  50.8 22.3 %all-to-all-done = bf16[128,32,144]{2,1,0:T(8,128)(2,1)} async-done(((bf16[128,32,144]{2,1,0:T(8,128)(2,1)}), bf16[128,32,144]{2,1,0:T(8,128)(2,1)}, u32[]{:S(2)}, u32[]{:S(2)}) %all-to-all-start) | async-done | bytes 1179680 | tf_op jit(solution)/shard_map/all_to_all | solution.py:300
  73.1 6.1 %shard_map.130 = bf16[4096,148]{1,0:T(8,128)(2,1)} custom-call(bf16[4096,144]{1,0:T(8,128)(2,1)} %bitcast.8.x_ref, bf16[4,144,144]{2,1,0:T(8,128)(2,1)} %bitcast.147, bf16[144,4]{1,0:T(8,128)(2,1)} %copy.20.fm_ref), custom_call_target="tpu_custom_call" | custom-call | flops 684195840 | bytes 2557952 | tf_op jit(solution)/shard_map/pallas_call | solution.py:113
  79.2 6.8 %all-to-all-start.1 = ((bf16[128,32,148]{2,1,0:T(8,128)(2,1)}), bf16[128,32,148]{2,1,0:T(8,128)(2,1)}, u32[]{:S(2)}, u32[]{:S(2)}) async-start(bf16[128,32,148]{2,1,0:T(8,128)(2,1)} %bitcast.137), calls=%async_computation.1 | async-start | bytes 4194304 | tf_op jit(solution)/shard_map/all_to_all | solution.py:301
  86.7 2.5 %fusion.66 = (f32[62,31,256]{2,1,0:T(8,128)}, f32[62,31,256]{2,1,0:T(8,128)}) fusion(f32[62,32,256]{2,1,0:T(8,128)S(1)} %copy-done), kind=kLoop, calls=%fused_computation.167 | loop fusion | bytes 7872512 | tf_op jit(solution)/shard_map/slice | solution.py:217
  90.6 3.4 %collective-permute-start.2 = (f32[12,40,4]{2,1,0:T(8,128)}, f32[12,40,4]{2,1,0:T(8,128)}, u32[]{:S(2)}, u32[]{:S(2)}) collective-permute-start(f32[12,40,4]{2,1,0:T(8,128)} %get-tuple-element.42), channel_id=1, source_target_pairs={{0,1},{1,2},{2,3},{4,5},{5,6},{6,7},{8,9},{9,10},{10,11},{12,13},{... | collective-permute-start | bytes 23048 | tf_op jit(solution)/shard_map/ppermute | solution.py:34
  94.0 3.1 %collective-permute-start.3 = (f32[12,40,4]{2,1,0:T(8,128)}, f32[12,40,4]{2,1,0:T(8,128)}, u32[]{:S(2)}, u32[]{:S(2)}) collective-permute-start(f32[12,40,4]{2,1,0:T(8,128)} %get-tuple-element.43), channel_id=1, source_target_pairs={{1,0},{2,1},{3,2},{5,4},{6,5},{7,6},{9,8},{10,9},{11,10},{13,12},{... | collective-permute-start | bytes 23048 | tf_op jit(solution)/shard_map/ppermute | solution.py:35
  97.7 3.9 %collective-permute-start.4 = (f32[62,1,256]{2,1,0:T(1,128)}, f32[62,1,256]{2,1,0:T(1,128)}, u32[]{:S(2)}, u32[]{:S(2)}) collective-permute-start(f32[62,1,256]{2,1,0:T(1,128)} %get-tuple-element.37), channel_id=1, source_target_pairs={{4,0},{8,4},{12,8},{16,12},{20,16},{24,20},{28,24},{32,28},{36,32}... | collective-permute-start | bytes 190472 | tf_op jit(solution)/shard_map/ppermute | solution.py:45
  101.5 1.7 %copy.24 = f32[62,32,1]{2,1,0:T(8,128)S(1)} copy(f32[62,32,1]{0,1,2:T(8,128)} %bitcast.155) | data formatting | bytes 15872 | tf_op jit(solution)/shard_map/broadcast_in_dim | solution.py:48
  103.2 2.5 %copy.22 = f32[62,32,1]{2,1,0:T(8,128)} copy(f32[62,32,1]{0,1,2:T(8,128)} %bitcast.19) | data formatting | bytes 15872 | tf_op jit(solution)/shard_map/broadcast_in_dim | solution.py:48
  105.8 8.5 %collective-permute-done.2 = f32[12,40,4]{2,1,0:T(8,128)} collective-permute-done((f32[12,40,4]{2,1,0:T(8,128)}, f32[12,40,4]{2,1,0:T(8,128)}, u32[]{:S(2)}, u32[]{:S(2)}) %collective-permute-start.2) | collective-permute-done | bytes 7712 | tf_op jit(solution)/shard_map/ppermute | solution.py:34
  115.2 2.3 %pad_maximum_fusion = f32[12,40,264]{2,1,0:T(8,128)} fusion(f32[12,40,4]{2,1,0:T(8,128)} %collective-permute-done.3, f32[12,4,256]{2,1,0:T(4,128)S(1)} %collective-permute-done.1, f32[12,32,256]{2,1,0:T(8,128)S(1)} %constant_dynamic-update-slice_fusion, f32[12,4,256]{2,1,0:T(4,128)S(1)} %collective-permute-done, f32[12,40,4]{2,1,0:T(8,128)} %collective-permute-done.2), kind=kLoop, calls=%fused_computation.24 | loop fusion | flops 506880 | bytes 1013760 | tf_op jit(solution)/shard_map/concatenate | solution.py:36
  117.6 5.9 %shard_map.131 = (f32[144,2048]{1,0:T(8,128)}, bf16[4,2048]{1,0:T(4,128)(2,1)}) custom-call(s32[1,2048]{1,0:T(1,128)} %bitcast_add_fusion.slots_ref, bf16[4096,148]{1,0:T(8,128)(2,1)} %bitcast.11.back_ref, f32[144,2048]{1,0:T(8,128)} %atm_ref.3), custom_call_target="tpu_custom_call" | custom-call | flops 2483027968 | bytes 4177920 | tf_op jit(solution)/shard_map/pallas_call | solution.py:149
  124.3 1.9 %collective-permute-start.8 = (bf16[4,3,128]{2,1,0:T(4,128)(2,1)S(1)}, bf16[4,3,128]{2,1,0:T(4,128)(2,1)S(1)}, u32[]{:S(2)}, u32[]{:S(2)}) collective-permute-start(bf16[4,3,128]{2,1,0:T(4,128)(2,1)S(1)} %get-tuple-element.71), channel_id=1, source_target_pairs={{0,4},{4,8},{8,12},{12,16},{16,20},{20,24},{24,28},{28,32},{32,36}... | collective-permute-start | bytes 9224 | tf_op jit(solution)/shard_map/ppermute | solution.py:31
  126.3 5.8 %collective-permute-start.9 = (bf16[4,3,128]{2,1,0:T(4,128)(2,1)S(1)}, bf16[4,3,128]{2,1,0:T(4,128)(2,1)S(1)}, u32[]{:S(2)}, u32[]{:S(2)}) collective-permute-start(bf16[4,3,128]{2,1,0:T(4,128)(2,1)S(1)} %get-tuple-element.72), channel_id=1, source_target_pairs={{4,0},{8,4},{12,8},{16,12},{20,16},{24,20},{28,24},{32,28},{36,32}... | collective-permute-start | bytes 9224 | tf_op jit(solution)/shard_map/ppermute | solution.py:32
  132.0 1.4 select_reduce_fusion.8
  133.5 3.1 %collective-permute-start.10 = (bf16[4,22,3]{2,1,0:T(8,128)(2,1)S(1)}, bf16[4,22,3]{2,1,0:T(8,128)(2,1)S(1)}, u32[]{:S(2)}, u32[]{:S(2)}) collective-permute-start(bf16[4,22,3]{2,1,0:T(8,128)(2,1)S(1)} %get-tuple-element.69), channel_id=1, source_target_pairs={{0,1},{1,2},{2,3},{4,5},{5,6},{6,7},{8,9},{9,10},{10,11},{12,13},{... | collective-permute-start | bytes 1592 | tf_op jit(solution)/shard_map/ppermute | solution.py:34
  136.6 2.7 %collective-permute-start.11 = (bf16[4,22,3]{2,1,0:T(8,128)(2,1)S(1)}, bf16[4,22,3]{2,1,0:T(8,128)(2,1)S(1)}, u32[]{:S(2)}, u32[]{:S(2)}) collective-permute-start(bf16[4,22,3]{2,1,0:T(8,128)(2,1)S(1)} %get-tuple-element.70), channel_id=1, source_target_pairs={{1,0},{2,1},{3,2},{5,4},{6,5},{7,6},{9,8},{10,9},{11,10},{13,12},{... | collective-permute-start | bytes 1592 | tf_op jit(solution)/shard_map/ppermute | solution.py:35
  140.3 2.0 %collective-permute-done.11 = bf16[4,22,3]{2,1,0:T(8,128)(2,1)S(1)} collective-permute-done((bf16[4,22,3]{2,1,0:T(8,128)(2,1)S(1)}, bf16[4,22,3]{2,1,0:T(8,128)(2,1)S(1)}, u32[]{:S(2)}, u32[]{:S(2)}) %collective-permute-start.11) | collective-permute-done | bytes 560 | tf_op jit(solution)/shard_map/ppermute | solution.py:35
  144.1 1.1 fusion.30
  145.6 1.0 fusion.34
  149.2 2.7 %fusion.5 = f32[62,32,256]{2,1,0:T(8,128)S(1)} fusion(f32[62,32,256]{2,1,0:T(8,128)S(1)} %copy-done, f32[62,1,256]{2,1,0:T(1,128)} %collective-permute-done.4, f32[62,31,256]{2,1,0:T(8,128)S(1)} %copy-done.4, f32[62,31,256]{2,1,0:T(8,128)S(1)} %copy-done.3, f32[62,1,256]{2,1,0:T(1,128)} %collective-permute-done.5, f32[62,32,1]{2,1,0:T(8,128)S(1)} %copy-done.5, ...), kind=kLoop, calls=%fused_computation.6 | loop fusion | flops 8634368 | bytes 12320768 | tf_op jit(solution)/shard_map/add | solution.py:227
  151.9 1.3 copy-done.6
  (115 shorter events, 21.6 us)
Async XLA Ops:
  2.6 146.4 %collective-permute-start.5 = (f32[62,1,256]{2,1,0:T(1,128)}, f32[62,1,256]{2,1,0:T(1,128)}, u32[]{:S(2)}, u32[]{:S(2)}) collective-permute-start(f32[62,1,256]{2,1,0:T(1,128)} %get-tuple-element.36), channel_id=1, source_target_pairs={{0,4},{4,8},{8,12},{12,16},{16,20},{20,24},{24,28},{28,32},{32,36}... | collective-permute-start | bytes 190472 | tf_op jit(solution)/shard_map/ppermute | solution.py:44
  9.4 80.4 %collective-permute-start = (f32[12,4,256]{2,1,0:T(4,128)}, f32[12,4,256]{2,1,0:T(4,128)S(1)}, u32[]{:S(2)}, u32[]{:S(2)}) collective-permute-start(f32[12,4,256]{2,1,0:T(4,128)} %get-tuple-element.44), channel_id=1, source_target_pairs={{0,4},{4,8},{8,12},{12,16},{16,20},{20,24},{24,28},{28,32},{32,36}... | collective-permute-start | bytes 147464 | tf_op jit(solution)/shard_map/ppermute | solution.py:31
  12.9 76.8 %collective-permute-start.1 = (f32[12,4,256]{2,1,0:T(4,128)}, f32[12,4,256]{2,1,0:T(4,128)S(1)}, u32[]{:S(2)}, u32[]{:S(2)}) collective-permute-start(f32[12,4,256]{2,1,0:T(4,128)} %get-tuple-element.45), channel_id=1, source_target_pairs={{4,0},{8,4},{12,8},{16,12},{20,16},{24,20},{28,24},{32,28},{36,32}... | collective-permute-start | bytes 147464 | tf_op jit(solution)/shard_map/ppermute | solution.py:32
  18.9 7.2 %copy-start.13 = (s32[2048,1]{0,1:T(1,128)S(1)}, s32[2048,1]{0,1:T(1,128)}, u32[]{:S(2)}) copy-start(s32[2048,1]{0,1:T(1,128)} %param.13) | copy-start | bytes 24580
  19.6 83.6 %collective-permute-start.6 = (f32[62,32]{0,1:T(8,128)S(1)}, f32[62,32]{0,1:T(8,128)}, u32[]{:S(2)}, u32[]{:S(2)}) collective-permute-start(f32[62,32]{0,1:T(8,128)S(1)} %bitcast.154), channel_id=1, source_target_pairs={{1,0},{2,1},{3,2},{5,4},{6,5},{7,6},{9,8},{10,9},{11,10},{13,12},{... | collective-permute-start | bytes 23816 | tf_op jit(solution)/shard_map/ppermute | solution.py:47
  22.7 74.9 %collective-permute-start.7 = (f32[62,32]{0,1:T(8,128)S(1)}, f32[62,32]{0,1:T(8,128)S(1)}, u32[]{:S(2)}, u32[]{:S(2)}) collective-permute-start(f32[62,32]{0,1:T(8,128)S(1)} %bitcast.156), channel_id=1, source_target_pairs={{0,1},{1,2},{2,3},{4,5},{5,6},{6,7},{8,9},{9,10},{10,11},{12,13},{... | collective-permute-start | bytes 23816 | tf_op jit(solution)/shard_map/ppermute | solution.py:46
  35.5 9.2 %copy-start.20 = (bf16[144,4]{0,1:T(4,128)(2,1)S(1)}, bf16[144,4]{0,1:T(4,128)(2,1)}, u32[]{:S(2)}) copy-start(bf16[144,4]{0,1:T(4,128)(2,1)} %param.15) | copy-start | bytes 3460
  35.5 11.2 %copy-start.7 = (s32[32,256]{1,0:T(8,128)S(1)}, s32[32,256]{1,0:T(8,128)}, u32[]{:S(2)}) copy-start(s32[32,256]{1,0:T(8,128)} %param.18) | copy-start | bytes 98308
  35.5 12.6 %copy-start = (f32[62,32,256]{2,1,0:T(8,128)S(1)}, f32[62,32,256]{2,1,0:T(8,128)}, u32[]{:S(2)}) copy-start(f32[62,32,256]{2,1,0:T(8,128)} %param.19) | copy-start | bytes 6094852
  35.5 37.7 %all-to-all-start = ((bf16[128,32,144]{2,1,0:T(8,128)(2,1)}), bf16[128,32,144]{2,1,0:T(8,128)(2,1)}, u32[]{:S(2)}, u32[]{:S(2)}) async-start(bf16[128,32,144]{2,1,0:T(8,128)(2,1)} %bitcast.138), calls=%async_computation | async-start | bytes 4194304 | tf_op jit(solution)/shard_map/all_to_all | solution.py:300
  79.2 38.4 %all-to-all-start.1 = ((bf16[128,32,148]{2,1,0:T(8,128)(2,1)}), bf16[128,32,148]{2,1,0:T(8,128)(2,1)}, u32[]{:S(2)}, u32[]{:S(2)}) async-start(bf16[128,32,148]{2,1,0:T(8,128)(2,1)} %bitcast.137), calls=%async_computation.1 | async-start | bytes 4194304 | tf_op jit(solution)/shard_map/all_to_all | solution.py:301
  90.6 23.7 %collective-permute-start.2 = (f32[12,40,4]{2,1,0:T(8,128)}, f32[12,40,4]{2,1,0:T(8,128)}, u32[]{:S(2)}, u32[]{:S(2)}) collective-permute-start(f32[12,40,4]{2,1,0:T(8,128)} %get-tuple-element.42), channel_id=1, source_target_pairs={{0,1},{1,2},{2,3},{4,5},{5,6},{6,7},{8,9},{9,10},{10,11},{12,13},{... | collective-permute-start | bytes 23048 | tf_op jit(solution)/shard_map/ppermute | solution.py:34
  94.0 21.2 %collective-permute-start.3 = (f32[12,40,4]{2,1,0:T(8,128)}, f32[12,40,4]{2,1,0:T(8,128)}, u32[]{:S(2)}, u32[]{:S(2)}) collective-permute-start(f32[12,40,4]{2,1,0:T(8,128)} %get-tuple-element.43), channel_id=1, source_target_pairs={{1,0},{2,1},{3,2},{5,4},{6,5},{7,6},{9,8},{10,9},{11,10},{13,12},{... | collective-permute-start | bytes 23048 | tf_op jit(solution)/shard_map/ppermute | solution.py:35
  97.7 3.9 %copy-start.17 = (f32[62,32]{0,1:T(8,128)}, f32[62,32]{0,1:T(8,128)S(1)}, u32[]{:S(2)}) copy-start(f32[62,32]{0,1:T(8,128)S(1)} %collective-permute-done.7) | copy-start | bytes 23812
  97.7 51.3 %collective-permute-start.4 = (f32[62,1,256]{2,1,0:T(1,128)}, f32[62,1,256]{2,1,0:T(1,128)}, u32[]{:S(2)}, u32[]{:S(2)}) collective-permute-start(f32[62,1,256]{2,1,0:T(1,128)} %get-tuple-element.37), channel_id=1, source_target_pairs={{4,0},{8,4},{12,8},{16,12},{20,16},{24,20},{28,24},{32,28},{36,32}... | collective-permute-start | bytes 190472 | tf_op jit(solution)/shard_map/ppermute | solution.py:45
  123.5 18.8 %copy-start.14 = (pred[134,264]{1,0:T(8,128)(4,1)S(1)}, pred[134,264]{1,0:T(8,128)(4,1)}, u32[]{:S(2)}) copy-start(pred[134,264]{1,0:T(8,128)(4,1)} %iota_compare_fusion.3) | copy-start | bytes 106132
  123.5 18.8 %copy-start.15 = (pred[134,264]{1,0:T(8,128)(4,1)S(1)}, pred[134,264]{1,0:T(8,128)(4,1)}, u32[]{:S(2)}) copy-start(pred[134,264]{1,0:T(8,128)(4,1)} %iota_compare_fusion.5) | copy-start | bytes 106132
  123.5 18.8 %copy-start.16 = (pred[134,264]{1,0:T(8,128)(4,1)S(1)}, pred[134,264]{1,0:T(8,128)(4,1)}, u32[]{:S(2)}) copy-start(pred[134,264]{1,0:T(8,128)(4,1)} %iota_compare_fusion.4) | copy-start | bytes 106132
  123.5 19.2 %copy-start.19 = (s32[40]{0:T(128)S(1)}, s32[40]{0:T(128)}, u32[]{:S(2)}) copy-start(s32[40]{0:T(128)} %get-tuple-element.75) | copy-start | bytes 484
  123.5 19.5 %copy-start.18 = (s32[40]{0:T(128)S(1)}, s32[40]{0:T(128)}, u32[]{:S(2)}) copy-start(s32[40]{0:T(128)} %get-tuple-element.76) | copy-start | bytes 484
  124.3 9.1 %collective-permute-start.8 = (bf16[4,3,128]{2,1,0:T(4,128)(2,1)S(1)}, bf16[4,3,128]{2,1,0:T(4,128)(2,1)S(1)}, u32[]{:S(2)}, u32[]{:S(2)}) collective-permute-start(bf16[4,3,128]{2,1,0:T(4,128)(2,1)S(1)} %get-tuple-element.71), channel_id=1, source_target_pairs={{0,4},{4,8},{8,12},{12,16},{16,20},{20,24},{24,28},{28,32},{32,36}... | collective-permute-start | bytes 9224 | tf_op jit(solution)/shard_map/ppermute | solution.py:31
  126.3 7.2 %collective-permute-start.9 = (bf16[4,3,128]{2,1,0:T(4,128)(2,1)S(1)}, bf16[4,3,128]{2,1,0:T(4,128)(2,1)S(1)}, u32[]{:S(2)}, u32[]{:S(2)}) collective-permute-start(bf16[4,3,128]{2,1,0:T(4,128)(2,1)S(1)} %get-tuple-element.72), channel_id=1, source_target_pairs={{4,0},{8,4},{12,8},{16,12},{20,16},{24,20},{28,24},{32,28},{36,32}... | collective-permute-start | bytes 9224 | tf_op jit(solution)/shard_map/ppermute | solution.py:32
  133.4 9.9 %copy-start.21 = (s32[40]{0:T(128)S(1)}, s32[40]{0:T(128)}, u32[]{:S(2)}) copy-start(s32[40]{0:T(128)} %clamp_subtract_fusion.5) | copy-start | bytes 484
  133.5 6.8 %collective-permute-start.10 = (bf16[4,22,3]{2,1,0:T(8,128)(2,1)S(1)}, bf16[4,22,3]{2,1,0:T(8,128)(2,1)S(1)}, u32[]{:S(2)}, u32[]{:S(2)}) collective-permute-start(bf16[4,22,3]{2,1,0:T(8,128)(2,1)S(1)} %get-tuple-element.69), channel_id=1, source_target_pairs={{0,1},{1,2},{2,3},{4,5},{5,6},{6,7},{8,9},{9,10},{10,11},{12,13},{... | collective-permute-start | bytes 1592 | tf_op jit(solution)/shard_map/ppermute | solution.py:34
  136.6 5.7 %collective-permute-start.11 = (bf16[4,22,3]{2,1,0:T(8,128)(2,1)S(1)}, bf16[4,22,3]{2,1,0:T(8,128)(2,1)S(1)}, u32[]{:S(2)}, u32[]{:S(2)}) collective-permute-start(bf16[4,22,3]{2,1,0:T(8,128)(2,1)S(1)} %get-tuple-element.70), channel_id=1, source_target_pairs={{1,0},{2,1},{3,2},{5,4},{6,5},{7,6},{9,8},{10,9},{11,10},{13,12},{... | collective-permute-start | bytes 1592 | tf_op jit(solution)/shard_map/ppermute | solution.py:35
  143.6 5.3 %copy-start.5 = (f32[62,32,1]{2,1,0:T(8,128)S(1)}, f32[62,32,1]{2,1,0:T(8,128)}, u32[]{:S(2)}) copy-start(f32[62,32,1]{2,1,0:T(8,128)} %copy.22) | copy-start | bytes 23812
  144.1 4.8 %copy-start.4 = (f32[62,31,256]{2,1,0:T(8,128)S(1)}, f32[62,31,256]{2,1,0:T(8,128)}, u32[]{:S(2)}) copy-start(f32[62,31,256]{2,1,0:T(8,128)} %get-tuple-element.39) | copy-start | bytes 5904388
  145.6 3.4 %copy-start.3 = (f32[62,31,256]{2,1,0:T(8,128)S(1)}, f32[62,31,256]{2,1,0:T(8,128)}, u32[]{:S(2)}) copy-start(f32[62,31,256]{2,1,0:T(8,128)} %get-tuple-element.38) | copy-start | bytes 5904388
  146.8 1.4 copy-start.8
  146.8 1.4 copy-start.9
  146.9 2.1 %copy-start.1 = (f32[62,32,255]{2,1,0:T(8,128)S(1)}, f32[62,32,255]{2,1,0:T(8,128)}, u32[]{:S(2)}) copy-start(f32[62,32,255]{2,1,0:T(8,128)} %get-tuple-element.34) | copy-start | bytes 6071044
  146.9 2.3 %copy-start.2 = (f32[62,32,255]{2,1,0:T(8,128)S(1)}, f32[62,32,255]{2,1,0:T(8,128)}, u32[]{:S(2)}) copy-start(f32[62,32,255]{2,1,0:T(8,128)} %get-tuple-element.35) | copy-start | bytes 6071044
  (4 other events, 5.5 us)
